TPU v7x, 512 devices: a whole 4x8x8 slice. The times are simulated.
512 devices in a mesh: ulysses: 8 (over z_hi, x), context: 64 (over y, z_lo, core).
Axes of the slice: x: 4, y: 8, z: 8 (z_hi: 2, z_lo: 4; z = z_hi * 4 + z_lo), core: 2. Of those that a mesh axis runs over, the one named last changes fastest.
Arguments:
- queries: bfloat16 [49152, 5120], P(('context', 'ulysses')), may hold values from -7 to 7
- key_vectors: bfloat16 [49152, 5120], P(('context', 'ulysses')), may hold values from -7 to 7
- value_vectors: bfloat16 [49152, 5120], P(('context', 'ulysses')), may hold values from -6 to 6
- labels: int32 [40], replicated, may hold values from 0 to 1, as said below
- block_lists: int32 [40, 768, 5], replicated, may hold values from 0 to 767, as said below
- counts: int32 [40, 768], replicated, may hold values from 1 to 5, as said below
- query_scale: float32 [40], replicated, may hold values from 1.5 to 3
- key_scale: float32 [40], replicated, may hold values from 1.5 to 3
- value_scale: float32 [40], replicated, may hold values from 0.5 to 2
Outputs:
- attended: bfloat16 [49152, 5120], P(('context', 'ulysses'))
Inputs may be any that keep to these rules, and one draw needn't show every extreme that they name: `labels`: exactly 16 entries are 1, the others 0; every aligned run of 5 heads holds at least one 0. Every entry of block_lists[h, b] lies within 2 blocks of b; the first entry is b itself and the first counts[h, b] entries are distinct. counts[h, b] is at least one less than and at most the number of blocks of the clip within 2 blocks of b; every head has a query block that uses all 5 entries.
All inputs are finite; a program needn't handle non-finite values.
Results may differ from a plain program's by a relative error of at most 0.0024.
Values may be sent and summed in bfloat16 or wider, within the bound.
No kernel may reach another device: no remote copies, remote signals or barrier semaphores. Data moves between devices by JAX's collectives and lax.ppermute only.
A program may use at most 128 MiB of HBM per device.

v0:
```python
import math

import jax
import jax.numpy as jnp
from jax import lax
from jax.sharding import PartitionSpec as P

FRAMES = 16
MARGIN = 2
BLOCK = 64


def padded(cells, sides, width, closed):
    for axis, dim in sides:
        count = lax.axis_size(axis)
        ends = count if closed else count - 1
        head = lax.slice_in_dim(cells, 0, width, axis=dim)
        tail = lax.slice_in_dim(cells, cells.shape[dim] - width, cells.shape[dim], axis=dim)
        cells = jnp.concatenate(
            [
                lax.ppermute(tail, axis, [(i, (i + 1) % count) for i in range(ends)]),
                cells,
                lax.ppermute(head, axis, [((i + 1) % count, i) for i in range(ends)]),
            ],
            axis=dim,
        )
    return cells


def attend_heads(
    query_rows,
    extended,
    head_ids,
    block_ids,
    anchors,
    block_lists,
    counts,
    query_scale,
    key_scale,
    value_scale,
):
    rows, heads_here, head_width = query_rows.shape
    blocks = rows // BLOCK
    list_length = block_lists.shape[2]
    logit_scale = (
        jnp.take(query_scale, head_ids) * jnp.take(key_scale, head_ids) / math.sqrt(head_width)
    )
    value_factor = jnp.take(value_scale, head_ids)

    def one_head(head_index):
        head = lax.dynamic_index_in_dim(head_ids, head_index, 0, keepdims=False)
        query_tiles = lax.dynamic_index_in_dim(query_rows, head_index, 1, keepdims=False).reshape(
            blocks, BLOCK, head_width
        )
        key_column = lax.dynamic_index_in_dim(extended, head_index, 1, keepdims=False).reshape(
            -1, BLOCK, head_width
        )
        value_column = lax.dynamic_index_in_dim(
            extended, head_index + heads_here, 1, keepdims=False
        ).reshape(-1, BLOCK, head_width)
        global_ids = lax.dynamic_index_in_dim(block_ids, head_index, 0, keepdims=False)
        anchor = lax.dynamic_index_in_dim(anchors, head_index, 0, keepdims=False)
        head_lists = jnp.take(
            lax.dynamic_index_in_dim(block_lists, head, 0, keepdims=False), global_ids, axis=0
        )
        allowed = jnp.take(
            lax.dynamic_index_in_dim(counts, head, 0, keepdims=False), global_ids, axis=0
        )
        chosen = anchor[:, None] + head_lists - global_ids[:, None]
        collected_keys = key_column[chosen].reshape(blocks, list_length * BLOCK, head_width)
        collected_values = value_column[chosen].reshape(blocks, list_length * BLOCK, head_width)
        attention_logits = (
            jnp.einsum(
                "fac,foc->fao", query_tiles, collected_keys, preferred_element_type=jnp.float32
            )
            * logit_scale[head_index]
        )
        valid = jnp.repeat(jnp.arange(list_length)[None, :] < allowed[:, None], BLOCK, axis=1)
        attention_logits = jnp.where(valid[:, None, :], attention_logits, -jnp.inf)
        peak = jnp.max(attention_logits, axis=-1, keepdims=True)
        weight = jnp.exp(attention_logits - peak)
        total = jnp.sum(weight, axis=-1, keepdims=True)
        blended_output = jnp.einsum(
            "oem,omg->oeg",
            weight.astype(jnp.bfloat16),
            collected_values,
            preferred_element_type=jnp.float32,
        )
        output = (blended_output * (value_factor[head_index] / total)).astype(jnp.bfloat16)
        return output.reshape(rows, head_width)

    result = lax.map(one_head, jnp.arange(heads_here, dtype=jnp.int32))
    return jnp.transpose(result, (1, 0, 2))


def block_maps(context_index, context, spans, run_blocks):
    local = jnp.arange(spans * run_blocks, dtype=jnp.int32)
    run = local // run_blocks
    inner = local % run_blocks
    line_ids = (run * context + context_index) * run_blocks + inner
    line_anchor = run * (run_blocks + 2 * MARGIN) + inner + MARGIN
    frame_ids = context_index * (spans * run_blocks) + local
    frame_anchor = local + MARGIN
    return (line_ids, line_anchor, frame_ids, frame_anchor)


def into_pieces(rows_array, context):
    rows, heads_here, head_width = rows_array.shape
    return rows_array.reshape(context, rows // context, heads_here, head_width)


def into_lines(moved, spans):
    context, piece, heads_here, head_width = moved.shape
    frames = context // spans
    lines = moved.reshape(frames, spans, piece, heads_here, head_width).transpose(1, 2, 0, 3, 4)
    return lines.reshape(spans, piece * frames, heads_here, head_width)


def out_of_lines(line_rows, context, spans):
    rows, heads_here, head_width = line_rows.shape
    piece = rows // context
    frames = context // spans
    pieces = line_rows.reshape(spans, piece, frames, heads_here, head_width).transpose(
        2, 0, 1, 3, 4
    )
    return pieces.reshape(context, piece, heads_here, head_width)


def line_rims(line_joined):
    width = MARGIN * BLOCK
    extended = padded(line_joined, (("context", 1),), MARGIN * BLOCK, True)
    context_index = lax.axis_index("context")
    last_index = lax.axis_size("context") - 1
    lower = extended[:, :width]
    middle = extended[:, width:-width]
    upper = extended[:, -width:]
    lower_moved = jnp.concatenate([jnp.zeros_like(lower[:1]), lower[:-1]], axis=0)
    upper_moved = jnp.concatenate([upper[1:], jnp.zeros_like(upper[:1])], axis=0)
    lower = jnp.where(context_index == 0, lower_moved, lower)
    upper = jnp.where(context_index == last_index, upper_moved, upper)
    joined = jnp.concatenate([lower, middle, upper], axis=1)
    return joined.reshape(-1, joined.shape[2], joined.shape[3])


def frame_rims(frame_joined):
    return padded(frame_joined, (("context", 0),), MARGIN * BLOCK, False)


def shards(
    queries,
    key_vectors,
    value_vectors,
    labels,
    block_lists,
    counts,
    query_scale,
    key_scale,
    value_scale,
):
    groups = lax.axis_size("ulysses")
    context = lax.axis_size("context")
    tokens_here = queries.shape[0]
    head_count = labels.shape[0]
    head_width = queries.shape[1] // head_count
    per_group = head_count // groups
    shard_rows = tokens_here * groups
    spans = context // FRAMES
    piece = shard_rows // context
    run_blocks = piece * FRAMES // BLOCK
    group_index = lax.axis_index("ulysses")
    context_index = lax.axis_index("context")
    line_ids, line_anchor, frame_ids, frame_anchor = block_maps(
        context_index, context, spans, run_blocks
    )
    split_queries = queries.reshape(tokens_here, head_count, head_width)
    split_keys = key_vectors.reshape(tokens_here, head_count, head_width)
    split_values = value_vectors.reshape(tokens_here, head_count, head_width)
    grouped_queries = split_queries.reshape(tokens_here, groups, per_group, head_width)
    grouped_keys = split_keys.reshape(tokens_here, groups, per_group, head_width)
    grouped_values = split_values.reshape(tokens_here, groups, per_group, head_width)
    frame_queries, frame_keys, frame_values = (
        lax.all_to_all(grouped_queries, "ulysses", split_axis=1, concat_axis=0, tiled=True),
        lax.all_to_all(grouped_keys, "ulysses", split_axis=1, concat_axis=0, tiled=True),
        lax.all_to_all(grouped_values, "ulysses", split_axis=1, concat_axis=0, tiled=True),
    )
    frame_queries = frame_queries.reshape(shard_rows, per_group, head_width)
    frame_keys = frame_keys.reshape(shard_rows, per_group, head_width)
    frame_values = frame_values.reshape(shard_rows, per_group, head_width)
    moved_queries, moved_keys, moved_values = (
        lax.all_to_all(
            into_pieces(frame_queries, context), "context", split_axis=0, concat_axis=0, tiled=True
        ),
        lax.all_to_all(
            into_pieces(frame_keys, context), "context", split_axis=0, concat_axis=0, tiled=True
        ),
        lax.all_to_all(
            into_pieces(frame_values, context), "context", split_axis=0, concat_axis=0, tiled=True
        ),
    )
    head_ids = group_index * per_group + jnp.arange(per_group, dtype=jnp.int32)
    temporal = jnp.take(labels, head_ids) == 1
    line_query = into_lines(moved_queries, spans).reshape(shard_rows, per_group, head_width)
    line_ext = line_rims(
        jnp.concatenate([into_lines(moved_keys, spans), into_lines(moved_values, spans)], axis=2)
    )
    frame_ext = frame_rims(jnp.concatenate([frame_keys, frame_values], axis=1))
    extra = line_ext.shape[0] - frame_ext.shape[0]
    frame_ext = jnp.pad(frame_ext, ((0, extra), (0, 0), (0, 0)))
    doubled = jnp.concatenate([temporal, temporal])
    query_rows = jnp.where(temporal[None, :, None], line_query, frame_queries)
    extended = jnp.where(doubled[None, :, None], line_ext, frame_ext)
    block_ids = jnp.where(temporal[:, None], line_ids[None, :], frame_ids[None, :])
    anchors = jnp.where(temporal[:, None], line_anchor[None, :], frame_anchor[None, :])
    outputs = attend_heads(
        query_rows,
        extended,
        head_ids,
        block_ids,
        anchors,
        block_lists,
        counts,
        query_scale,
        key_scale,
        value_scale,
    )
    returned = lax.all_to_all(
        out_of_lines(outputs, context, spans), "context", split_axis=0, concat_axis=0, tiled=True
    )
    returned = returned.reshape(shard_rows, per_group, head_width)
    frame_outputs = jnp.where(temporal[None, :, None], returned, outputs)
    merged = lax.all_to_all(
        frame_outputs.reshape(shard_rows, 1, per_group, head_width),
        "ulysses",
        split_axis=0,
        concat_axis=1,
        tiled=True,
    )
    return merged.reshape(tokens_here, head_count * head_width)


def solution(mesh):
    placed = (
        P(("context", "ulysses"), None),
        P(("context", "ulysses"), None),
        P(("context", "ulysses"), None),
        P(),
        P(),
        P(),
        P(),
        P(),
        P(),
    )
    return jax.shard_map(
        shards,
        mesh=mesh,
        in_specs=placed,
        out_specs=P(("context", "ulysses"), None),
        check_vma=False,
    )
```

profile of v0, /device:TPU:72, one launch (start us, length us, event | category | flops | bytes accessed | tf_op | source)
XLA Modules:
  0.0 460.1 jit_solution(15324251279415302545)
XLA Ops:
  0.0 1.7 copy.101
  1.7 1.4 copy.102
  3.1 12.0 %all-to-all-start.2 = ((bf16[96,8,5,128]{3,0,2,1:T(8,128)(2,1)}), bf16[96,8,5,128]{3,0,2,1:T(8,128)(2,1)S(1)}, u32[]{:S(2)}, u32[]{:S(2)}) async-start(bf16[96,8,5,128]{3,0,2,1:T(8,128)(2,1)} %copy.102), calls=%async_computation.2 | async-start | bytes 1966080 | tf_op jit(solution)/shard_map/all_to_all | solution.py:183
  15.9 1.4 copy.108
  17.2 26.0 %all-to-all-done.2 = bf16[96,8,5,128]{3,0,2,1:T(8,128)(2,1)S(1)} async-done(((bf16[96,8,5,128]{3,0,2,1:T(8,128)(2,1)}), bf16[96,8,5,128]{3,0,2,1:T(8,128)(2,1)S(1)}, u32[]{:S(2)}, u32[]{:S(2)}) %all-to-all-start.2) | async-done | bytes 983072 | tf_op jit(solution)/shard_map/all_to_all | solution.py:183
  44.2 3.6 all-to-all-start.4
  48.5 1.4 copy.96
  49.9 22.0 %all-to-all-done.4 = bf16[96,8,5,128]{3,0,2,1:T(8,128)(2,1)S(1)} async-done(((bf16[96,8,5,128]{3,0,2,1:T(8,128)(2,1)}), bf16[96,8,5,128]{3,0,2,1:T(8,128)(2,1)S(1)}, u32[]{:S(2)}, u32[]{:S(2)}) %all-to-all-start.4) | async-done | bytes 983072 | tf_op jit(solution)/shard_map/all_to_all | solution.py:184
  71.9 4.7 %all-to-all-start = ((bf16[96,8,5,128]{3,0,2,1:T(8,128)(2,1)}), bf16[96,8,5,128]{3,0,2,1:T(8,128)(2,1)S(1)}, u32[]{:S(2)}, u32[]{:S(2)}) async-start(bf16[96,8,5,128]{3,0,2,1:T(8,128)(2,1)} %copy.96), calls=%async_computation | async-start | bytes 1966080 | tf_op jit(solution)/shard_map/all_to_all | solution.py:182
  76.6 1.3 copy.128
  78.2 1.3 copy.104
  79.5 19.5 %all-to-all-done = bf16[96,8,5,128]{3,0,2,1:T(8,128)(2,1)S(1)} async-done(((bf16[96,8,5,128]{3,0,2,1:T(8,128)(2,1)}), bf16[96,8,5,128]{3,0,2,1:T(8,128)(2,1)S(1)}, u32[]{:S(2)}, u32[]{:S(2)}) %all-to-all-start) | async-done | bytes 983072 | tf_op jit(solution)/shard_map/all_to_all | solution.py:182
  99.9 9.4 %all-to-all-start.3 = ((bf16[64,12,5,128]{3,1,2,0:T(8,128)(2,1)}), bf16[64,12,5,128]{3,1,2,0:T(8,128)(2,1)S(1)}, u32[]{:S(2)}, u32[]{:S(2)}) async-start(bf16[64,12,5,128]{3,1,2,0:T(8,128)(2,1)} %copy.104), calls=%async_computation.3 | async-start | bytes 2621440 | tf_op jit(solution)/shard_map/all_to_all | solution.py:193
  109.3 1.3 copy.127
  110.6 1.2 reshape_reshape.27
  111.9 2.6 copy.110
  114.5 28.4 %all-to-all-done.3 = bf16[64,12,5,128]{3,1,2,0:T(8,128)(2,1)S(1)} async-done(((bf16[64,12,5,128]{3,1,2,0:T(8,128)(2,1)}), bf16[64,12,5,128]{3,1,2,0:T(8,128)(2,1)S(1)}, u32[]{:S(2)}, u32[]{:S(2)}) %all-to-all-start.3) | async-done | bytes 983072 | tf_op jit(solution)/shard_map/all_to_all | solution.py:193
  144.0 6.8 %all-to-all-start.5 = ((bf16[64,12,5,128]{3,1,2,0:T(8,128)(2,1)}), bf16[64,12,5,128]{3,1,2,0:T(8,128)(2,1)}, u32[]{:S(2)}, u32[]{:S(2)}) async-start(bf16[64,12,5,128]{3,1,2,0:T(8,128)(2,1)} %copy.110), calls=%async_computation.5 | async-start | bytes 2621440 | tf_op jit(solution)/shard_map/all_to_all | solution.py:196
  150.8 1.3 copy.129
  153.2 2.6 copy.98
  155.9 28.4 %all-to-all-done.5 = bf16[64,12,5,128]{3,1,2,0:T(8,128)(2,1)} async-done(((bf16[64,12,5,128]{3,1,2,0:T(8,128)(2,1)}), bf16[64,12,5,128]{3,1,2,0:T(8,128)(2,1)}, u32[]{:S(2)}, u32[]{:S(2)}) %all-to-all-start.5) | async-done | bytes 983072 | tf_op jit(solution)/shard_map/all_to_all | solution.py:196
  184.3 6.8 %all-to-all-start.1 = ((bf16[64,12,5,128]{3,1,2,0:T(8,128)(2,1)}), bf16[64,12,5,128]{3,1,2,0:T(8,128)(2,1)}, u32[]{:S(2)}, u32[]{:S(2)}) async-start(bf16[64,12,5,128]{3,1,2,0:T(8,128)(2,1)} %copy.98), calls=%async_computation.1 | async-start | bytes 2621440 | tf_op jit(solution)/shard_map/all_to_all | solution.py:190
  193.7 1.6 copy.105
  195.5 1.9 copy.111
  197.7 1.9 fusion.19
  199.5 2.0 collective-permute-start
  201.6 3.5 collective-permute-start.1
  206.2 1.9 collective-permute-start.2
  208.1 3.8 collective-permute-start.3
  212.0 12.6 %all-to-all-done.1 = bf16[64,12,5,128]{3,1,2,0:T(8,128)(2,1)} async-done(((bf16[64,12,5,128]{3,1,2,0:T(8,128)(2,1)}), bf16[64,12,5,128]{3,1,2,0:T(8,128)(2,1)}, u32[]{:S(2)}, u32[]{:S(2)}) %all-to-all-start.1) | async-done | bytes 983072 | tf_op jit(solution)/shard_map/all_to_all | solution.py:190
  224.5 1.6 copy.99
  226.3 1.3 bitcast_select_fusion.1
  227.6 21.9 %collective-permute-done = bf16[4,128,10,128]{3,1,2,0:T(8,128)(2,1)} collective-permute-done((bf16[4,128,10,128]{3,1,2,0:T(8,128)(2,1)}, bf16[4,128,10,128]{3,1,2,0:T(8,128)(2,1)}, u32[]{:S(2)}, u32[]{:S(2)}) %collective-permute-start) | collective-permute-done | bytes 1310752 | tf_op jit(solution)/shard_map/ppermute | solution.py:21
  249.4 1.3 slice.42
  250.7 1.3 slice.43
  252.0 1.4 pad_select_fusion.1
  253.5 1.6 pad_select_fusion
  256.1 9.3 %fusion.17 = bf16[1792,10,128]{2,0,1:T(8,128)(2,1)} fusion(bf16[128,10,128]{2,0,1:T(8,128)(2,1)} %collective-permute-done.3, bf16[128,10,128]{2,0,1:T(8,128)(2,1)S(1)} %collective-permute-done.2, bf16[768,5,128]{2,0,1:T(8,128)(2,1)S(1)} %bitcast.153, bf16[768,5,128]{2,0,1:T(8,128)(2,1)S(1)} %bitcast.150, bf16[4,448,10,128]{3,1,0,2:T(8,128)(2,1)S(1)} %copy.113, ...), kind=kLoop, calls=%fused_computation.46 | loop fusion | flops 32112640 | bytes 11796490 | tf_op jit(solution)/shard_map/jit(_where)/select_n | solution.py:211
  265.4 97.5 %while.12 = (s32[]{:T(128)}, bf16[5,768,128]{2,1,0:T(8,128)(2,1)}, s32[5]{0:T(128)S(1)}, s32[5,12]{1,0:T(8,128)S(1)}, s32[5]{0:T(128)S(1)}, /*index=5*/s32[40,76...) while((s32[]{:T(128)}, bf16[5,768,128]{2,1,0:T(8,128)(2,1)}, ...), condition=%wide.region_3.5_spmd, body=%wide.region_0.4_spmd.sunk | while | flops 127747880 | bytes 11979580 | solution.py:92
  276.2 1.2 constant_dynamic-slice_fusion.9
  295.7 1.2 constant_dynamic-slice_fusion.9
  315.2 1.2 constant_dynamic-slice_fusion.9
  334.7 1.2 constant_dynamic-slice_fusion.9
  362.9 1.5 copy.115
  364.4 45.8 %all_to_all.80 = bf16[64,12,5,128]{3,1,2,0:T(8,128)(2,1)S(1)} all-to-all(bf16[64,12,5,128]{3,1,2,0:T(8,128)(2,1)S(1)} %bitcast.165), channel_id=1, replica_groups=mesh['ulysses'=8,'context'=64] {'context'}, dimensions={0} | all-to-all | bytes 1966080 | tf_op jit(solution)/shard_map/all_to_all | solution.py:226
  410.7 1.4 fusion.20
  412.9 44.9 %all_to_all.81 = bf16[768,1,5,128]{3,2,1,0:T(8,128)(2,1)S(1)} all-to-all(bf16[768,1,5,128]{3,2,1,0:T(8,128)(2,1)S(1)} %copy.117), channel_id=1, replica_groups=mesh['ulysses'=8,'context'=64] {'ulysses'}, dimensions={0} | all-to-all | bytes 1966080 | tf_op jit(solution)/shard_map/all_to_all | solution.py:231
  458.7 1.4 copy.119
  (210 shorter events, 75.1 us)
Async XLA Ops:
  0.0 191.1 %copy-start = (f32[40]{0:T(128)S(1)}, f32[40]{0:T(128)}, u32[]{:S(2)}) copy-start(f32[40]{0:T(128)} %param.21) | copy-start | bytes 484
  3.1 12.0 %copy-start.13 = (bf16[96,5120]{1,0:T(8,128)(2,1)S(1)}, bf16[96,5120]{1,0:T(8,128)(2,1)}, u32[]{:S(2)}) copy-start(bf16[96,5120]{1,0:T(8,128)(2,1)} %param.15) | copy-start | bytes 2949124
  3.1 40.1 %all-to-all-start.2 = ((bf16[96,8,5,128]{3,0,2,1:T(8,128)(2,1)}), bf16[96,8,5,128]{3,0,2,1:T(8,128)(2,1)S(1)}, u32[]{:S(2)}, u32[]{:S(2)}) async-start(bf16[96,8,5,128]{3,0,2,1:T(8,128)(2,1)} %copy.102), calls=%async_computation.2 | async-start | bytes 1966080 | tf_op jit(solution)/shard_map/all_to_all | solution.py:183
  17.2 30.5 %copy-start.14 = (bf16[96,5120]{1,0:T(8,128)(2,1)S(1)}, bf16[96,5120]{1,0:T(8,128)(2,1)}, u32[]{:S(2)}) copy-start(bf16[96,5120]{1,0:T(8,128)(2,1)} %param.13) | copy-start | bytes 2949124
  43.2 1.0 copy-start.12
  44.2 27.8 %all-to-all-start.4 = ((bf16[96,8,5,128]{3,0,2,1:T(8,128)(2,1)}), bf16[96,8,5,128]{3,0,2,1:T(8,128)(2,1)S(1)}, u32[]{:S(2)}, u32[]{:S(2)}) async-start(bf16[96,8,5,128]{3,0,2,1:T(8,128)(2,1)} %copy.108), calls=%async_computation.4 | async-start | bytes 1966080 | tf_op jit(solution)/shard_map/all_to_all | solution.py:184
  71.9 6.0 %copy-start.11 = (bf16[96,8,5,128]{3,0,2,1:T(8,128)(2,1)}, bf16[96,8,5,128]{3,0,2,1:T(8,128)(2,1)S(1)}, u32[]{:S(2)}) copy-start(bf16[96,8,5,128]{3,0,2,1:T(8,128)(2,1)S(1)} %all-to-all-done.4) | copy-start | bytes 2949124
  71.9 27.0 %all-to-all-start = ((bf16[96,8,5,128]{3,0,2,1:T(8,128)(2,1)}), bf16[96,8,5,128]{3,0,2,1:T(8,128)(2,1)S(1)}, u32[]{:S(2)}, u32[]{:S(2)}) async-start(bf16[96,8,5,128]{3,0,2,1:T(8,128)(2,1)} %copy.96), calls=%async_computation | async-start | bytes 1966080 | tf_op jit(solution)/shard_map/all_to_all | solution.py:182
  99.0 0.9 copy-start.10
  99.9 43.0 %all-to-all-start.3 = ((bf16[64,12,5,128]{3,1,2,0:T(8,128)(2,1)}), bf16[64,12,5,128]{3,1,2,0:T(8,128)(2,1)S(1)}, u32[]{:S(2)}, u32[]{:S(2)}) async-start(bf16[64,12,5,128]{3,1,2,0:T(8,128)(2,1)} %copy.104), calls=%async_computation.3 | async-start | bytes 2621440 | tf_op jit(solution)/shard_map/all_to_all | solution.py:193
  142.9 1.1 copy-start.9
  144.0 40.3 %all-to-all-start.5 = ((bf16[64,12,5,128]{3,1,2,0:T(8,128)(2,1)}), bf16[64,12,5,128]{3,1,2,0:T(8,128)(2,1)}, u32[]{:S(2)}, u32[]{:S(2)}) async-start(bf16[64,12,5,128]{3,1,2,0:T(8,128)(2,1)} %copy.110), calls=%async_computation.5 | async-start | bytes 2621440 | tf_op jit(solution)/shard_map/all_to_all | solution.py:196
  155.9 35.9 %copy-start.2 = (f32[40]{0:T(128)S(1)}, f32[40]{0:T(128)}, u32[]{:S(2)}) copy-start(f32[40]{0:T(128)} %param.19) | copy-start | bytes 484
  155.9 36.5 %copy-start.3 = (f32[40]{0:T(128)S(1)}, f32[40]{0:T(128)}, u32[]{:S(2)}) copy-start(f32[40]{0:T(128)} %param.20) | copy-start | bytes 484
  184.3 40.3 %all-to-all-start.1 = ((bf16[64,12,5,128]{3,1,2,0:T(8,128)(2,1)}), bf16[64,12,5,128]{3,1,2,0:T(8,128)(2,1)}, u32[]{:S(2)}, u32[]{:S(2)}) async-start(bf16[64,12,5,128]{3,1,2,0:T(8,128)(2,1)} %copy.98), calls=%async_computation.1 | async-start | bytes 2621440 | tf_op jit(solution)/shard_map/all_to_all | solution.py:190
  191.0 2.0 copy-start.4
  195.5 2.2 copy-start.5
  197.7 1.9 copy-start.7
  199.5 49.9 %collective-permute-start = (bf16[4,128,10,128]{3,1,2,0:T(8,128)(2,1)}, bf16[4,128,10,128]{3,1,2,0:T(8,128)(2,1)}, u32[]{:S(2)}, u32[]{:S(2)}) collective-permute-start(bf16[4,128,10,128]{3,1,2,0:T(8,128)(2,1)} %get-tuple-element.259), channel_id=1, source_target_pairs={{0,1},{1,2},{2,3},{3,4},{4,5},{5,6},{6,7},{7,8},{8,9},{9,10},{10,1... | collective-permute-start | bytes 3932168 | tf_op jit(solution)/shard_map/ppermute | solution.py:21
  201.6 49.1 %collective-permute-start.1 = (bf16[4,128,10,128]{3,1,2,0:T(8,128)(2,1)}, bf16[4,128,10,128]{3,1,2,0:T(8,128)(2,1)}, u32[]{:S(2)}, u32[]{:S(2)}) collective-permute-start(bf16[4,128,10,128]{3,1,2,0:T(8,128)(2,1)} %get-tuple-element.260), channel_id=1, source_target_pairs={{1,0},{2,1},{3,2},{4,3},{5,4},{6,5},{7,6},{8,7},{9,8},{10,9},{11,1... | collective-permute-start | bytes 3932168 | tf_op jit(solution)/shard_map/ppermute | solution.py:23
  206.2 49.9 %collective-permute-start.2 = (bf16[128,10,128]{2,0,1:T(8,128)(2,1)}, bf16[128,10,128]{2,0,1:T(8,128)(2,1)S(1)}, u32[]{:S(2)}, u32[]{:S(2)}) collective-permute-start(bf16[128,10,128]{2,0,1:T(8,128)(2,1)} %get-tuple-element.261), channel_id=1, source_target_pairs={{0,1},{1,2},{2,3},{3,4},{4,5},{5,6},{6,7},{7,8},{8,9},{9,10},{10,1... | collective-permute-start | bytes 983048 | tf_op jit(solution)/shard_map/ppermute | solution.py:21
  208.1 48.0 %collective-permute-start.3 = (bf16[128,10,128]{2,0,1:T(8,128)(2,1)}, bf16[128,10,128]{2,0,1:T(8,128)(2,1)}, u32[]{:S(2)}, u32[]{:S(2)}) collective-permute-start(bf16[128,10,128]{2,0,1:T(8,128)(2,1)} %get-tuple-element.262), channel_id=1, source_target_pairs={{1,0},{2,1},{3,2},{4,3},{5,4},{6,5},{7,6},{8,7},{9,8},{10,9},{11,1... | collective-permute-start | bytes 983048 | tf_op jit(solution)/shard_map/ppermute | solution.py:23
  253.4 1.6 copy-start.6
  253.5 1.9 copy-start.8
  457.8 2.3 copy-start.1
where the time goes:
time: 463 us; the launch traced here: 460 us
  waiting for transfers between devices  159 us (34%)
  local copies, waits for them, and re-layouts  92.2 us (20%)
  blocking collectives  90.8 us (20%)
  starting transfers between devices  54.5 us (12%)
  loops' own time  30.9 us (7%)
  other arithmetic  24.5 us (5%)
  matrix products  8.12 us (2%)
    all_to_all x1, blocking collectives, shards(): lax.all_to_all(out_of_lines(outputs, context, spans), 'context', split_ax...  45.8 us
    all_to_all x1, blocking collectives, shards(): lax.all_to_all(frame_outputs.reshape(shard_rows, 1, per_group, head_width...  44.9 us
    another operation x1, loops' own time, attend_heads(): result = lax.map(one_head, jnp.arange(heads_here, dtype=jnp.int32))  30.9 us
    all_to_all x1, waiting for transfers between devices, shards(): lax.all_to_all(into_pieces(frame_keys, context), 'context', split_axis=0,...  28.4 us
    all_to_all x1, waiting for transfers between devices, shards(): lax.all_to_all(into_pieces(frame_values, context), 'context', split_axis=...  28.4 us
    all_to_all x1, waiting for transfers between devices, shards(): lax.all_to_all(grouped_keys, 'ulysses', split_axis=1, concat_axis=0, tile...  26 us
    all_to_all x1, waiting for transfers between devices, shards(): lax.all_to_all(grouped_values, 'ulysses', split_axis=1, concat_axis=0, ti...  22 us
    ppermute x2, waiting for transfers between devices, padded(): lax.ppermute(tail, axis, [(i, (i + 1) % count) for i in range(ends)])  21.9 us
  transfers between devices with their start and end apart: 10, of which 7 were waited for; matrix products, arithmetic and copies ran while one was open for 8% of the time, Pallas kernels for 0%

commit v1 on v0

v1 whole, which is shorter than its diff:
```python
import math

import jax
import jax.numpy as jnp
from jax import lax
from jax.sharding import Mesh, PartitionSpec as P

FRAMES = 16
MARGIN = 2
BLOCK = 64


def with_halo(cells, axes, order):
    width = MARGIN * BLOCK
    pairs = list(zip(order[:-1], order[1:]))
    lower = lax.ppermute(cells[-width:], axes, pairs)
    upper = lax.ppermute(cells[:width], axes, [(b, a) for a, b in pairs])
    return jnp.concatenate([lower, cells, upper], axis=0)


def window_mask(block_lists, counts, head_ids, base, blocks):
    span = 2 * MARGIN + 1
    list_length = block_lists.shape[2]
    head_lists = jnp.take(block_lists, head_ids, axis=0)
    head_counts = jnp.take(counts, head_ids, axis=0)
    global_ids = base[:, None] + jnp.arange(blocks, dtype=jnp.int32)[None, :]
    lists = jnp.take_along_axis(head_lists, global_ids[:, :, None], axis=1)
    used = jnp.take_along_axis(head_counts, global_ids, axis=1)
    wanted = global_ids[:, :, None] + jnp.arange(span, dtype=jnp.int32)[None, None, :] - MARGIN
    live = jnp.arange(list_length, dtype=jnp.int32)[None, None, :] < used[:, :, None]
    hit = (lists[:, :, None, :] == wanted[:, :, :, None]) & live[:, :, None, :]
    return jnp.any(hit, axis=-1)


def attend(query_rows, key_ext, value_ext, allowed, logit_scale, value_factor):
    rows, heads, width = query_rows.shape
    blocks = rows // BLOCK
    span = 2 * MARGIN + 1
    q = query_rows.reshape(blocks, BLOCK, heads, width)
    kb = key_ext.reshape(blocks + 2 * MARGIN, BLOCK, heads, width)
    vb = value_ext.reshape(blocks + 2 * MARGIN, BLOCK, heads, width)
    kw = jnp.stack([kb[o : o + blocks] for o in range(span)], axis=1)
    vw = jnp.stack([vb[o : o + blocks] for o in range(span)], axis=1)
    logits = jnp.einsum("bqhd,bokhd->hbqok", q, kw, preferred_element_type=jnp.float32)
    logits = logits * logit_scale[:, None, None, None, None]
    logits = jnp.where(allowed[:, :, None, :, None], logits, -jnp.inf)
    peak = jnp.max(logits, axis=(3, 4), keepdims=True)
    weight = jnp.exp(logits - peak)
    total = jnp.sum(weight, axis=(3, 4))
    mixed = jnp.einsum(
        "hbqok,bokhd->bqhd", weight.astype(jnp.bfloat16), vw, preferred_element_type=jnp.float32
    )
    factor = value_factor[:, None, None] / total
    out = mixed * jnp.transpose(factor, (1, 2, 0))[:, :, :, None]
    return out.astype(jnp.bfloat16).reshape(rows, heads, width)


def shards(
    queries,
    key_vectors,
    value_vectors,
    labels,
    block_lists,
    counts,
    query_scale,
    key_scale,
    value_scale,
):
    groups = lax.axis_size("ulysses")
    frames = lax.axis_size("frame")
    quarters = lax.axis_size("quarter")
    devices_along = frames * quarters
    tokens_here = queries.shape[0]
    head_count = labels.shape[0]
    width = queries.shape[1] // head_count
    per_group = head_count // groups
    rows = tokens_here * groups
    blocks = rows // BLOCK
    piece = rows // frames

    group_index = lax.axis_index("ulysses")
    frame_index = lax.axis_index("frame")
    quarter_index = lax.axis_index("quarter")
    spatial_slot = frame_index * quarters + quarter_index
    temporal_slot = quarter_index * frames + frame_index

    stacked = jnp.concatenate(
        [
            queries.reshape(tokens_here, groups, per_group, width),
            key_vectors.reshape(tokens_here, groups, per_group, width),
            value_vectors.reshape(tokens_here, groups, per_group, width),
        ],
        axis=2,
    )
    frame_rows = lax.all_to_all(stacked, "ulysses", split_axis=1, concat_axis=0, tiled=True)
    frame_rows = frame_rows.reshape(rows, 3 * per_group, width)
    moved = lax.all_to_all(
        frame_rows.reshape(frames, piece, 3 * per_group, width),
        "frame",
        split_axis=0,
        concat_axis=0,
        tiled=True,
    )
    line_rows = jnp.transpose(moved, (1, 0, 2, 3)).reshape(rows, 3 * per_group, width)

    spatial_order = list(range(devices_along))
    temporal_order = [(k % frames) * quarters + k // frames for k in range(devices_along)]
    frame_ext = with_halo(frame_rows[:, per_group:], ("frame", "quarter"), spatial_order)
    line_ext = with_halo(line_rows[:, per_group:], ("frame", "quarter"), temporal_order)

    head_ids = group_index * per_group + jnp.arange(per_group, dtype=jnp.int32)
    temporal = jnp.take(labels, head_ids) == 1
    doubled = jnp.concatenate([temporal, temporal])
    query_rows = jnp.where(temporal[None, :, None], line_rows[:, :per_group], frame_rows[:, :per_group])
    extended = jnp.where(doubled[None, :, None], line_ext, frame_ext)
    base = jnp.where(temporal, temporal_slot * blocks, spatial_slot * blocks).astype(jnp.int32)
    allowed = window_mask(block_lists, counts, head_ids, base, blocks)
    logit_scale = (
        jnp.take(query_scale, head_ids) * jnp.take(key_scale, head_ids) / math.sqrt(width)
    )
    value_factor = jnp.take(value_scale, head_ids)
    outputs = attend(
        query_rows,
        extended[:, :per_group],
        extended[:, per_group:],
        allowed,
        logit_scale,
        value_factor,
    )

    back = jnp.transpose(outputs.reshape(piece, frames, per_group, width), (1, 0, 2, 3))
    returned = lax.all_to_all(back, "frame", split_axis=0, concat_axis=0, tiled=True)
    returned = returned.reshape(rows, per_group, width)
    frame_outputs = jnp.where(temporal[None, :, None], returned, outputs)
    merged = lax.all_to_all(
        frame_outputs.reshape(rows, 1, per_group, width),
        "ulysses",
        split_axis=0,
        concat_axis=1,
        tiled=True,
    )
    return merged.reshape(tokens_here, head_count * width)


def solution(mesh):
    ulysses, context = mesh.devices.shape
    fine = Mesh(
        mesh.devices.reshape(ulysses, FRAMES, context // FRAMES), ("ulysses", "frame", "quarter")
    )
    rows = P(("frame", "quarter", "ulysses"), None)
    placed = (rows, rows, rows, P(), P(), P(), P(), P(), P())
    return jax.shard_map(
        shards,
        mesh=fine,
        in_specs=placed,
        out_specs=rows,
        check_vma=False,
    )
```

time: 463 us -> 333 us (0.72)
  the two profiles are of different devices: /device:TPU:72 before, /device:TPU:48 now
where the time goes in v1:
time: 333 us
  blocking collectives  155 us (47%)
  waiting for transfers between devices  101 us (30%)
  local copies, waits for them, and re-layouts  36 us (11%)
  starting transfers between devices  27.2 us (8%)
  other arithmetic  9.46 us (3%)
  matrix products  3.6 us (1%)
    all_to_all x1, waiting for transfers between devices, shards(): lax.all_to_all(frame_rows.reshape(frames, piece, 3 * per_group, width), '...  82.6 us
    all_to_all x1, blocking collectives, shards(): lax.all_to_all(stacked, 'ulysses', split_axis=1, concat_axis=0, tiled=True)  82.2 us
    all_to_all x1, blocking collectives, shards(): lax.all_to_all(frame_outputs.reshape(rows, 1, per_group, width), 'ulysses...  42 us
    all_to_all x1, blocking collectives, shards(): lax.all_to_all(back, 'frame', split_axis=0, concat_axis=0, tiled=True)  31.2 us
    ppermute x2, starting transfers between devices, with_halo(): upper = lax.ppermute(cells[:width], axes, [(b, a) for a, b in pairs])  12.2 us
    ppermute x2, waiting for transfers between devices, with_halo(): upper = lax.ppermute(cells[:width], axes, [(b, a) for a, b in pairs])  11.7 us
    all_to_all x1, starting transfers between devices, shards(): lax.all_to_all(frame_rows.reshape(frames, piece, 3 * per_group, width), '...  11.1 us
    unnamed x31, local copies, waits for them, and re-layouts  10.6 us
  transfers between devices with their start and end apart: 5, of which 3 were waited for; matrix products, arithmetic and copies ran while one was open for 4% of the time, Pallas kernels for 0%

profile of v1, /device:TPU:48, one launch (start us, length us, event | category | flops | bytes accessed | tf_op | source)
XLA Modules:
  0.0 332.7 jit_solution(10874801442408721896)
XLA Ops:
  0.0 1.8 copy.74
  1.8 1.7 copy.75
  3.5 2.4 copy.76
  5.9 3.4 %pad_maximum_fusion = bf16[96,8,15,128]{0,3,2,1:T(8,128)(2,1)} fusion(bf16[96,8,5,128]{0,3,2,1:T(8,128)(2,1)} %bitcast.67, bf16[96,8,5,128]{0,3,2,1:T(8,128)(2,1)S(1)} %bitcast.66, bf16[96,8,5,128]{0,3,2,1:T(8,128)(2,1)S(1)} %bitcast.65), kind=kLoop, calls=%fused_computation.16 | loop fusion | flops 2949120 | bytes 5898240 | tf_op jit(solution)/shard_map/concatenate | solution.py:87
  9.3 5.8 %copy.77 = bf16[96,8,15,128]{3,0,2,1:T(8,128)(2,1)} copy(bf16[96,8,15,128]{0,3,2,1:T(8,128)(2,1)} %pad_maximum_fusion) | data formatting | bytes 5898240 | tf_op jit(solution)/shard_map/concatenate | solution.py:87
  15.0 82.2 %all_to_all.40 = bf16[96,8,15,128]{3,0,2,1:T(8,128)(2,1)S(1)} all-to-all(bf16[96,8,15,128]{3,0,2,1:T(8,128)(2,1)} %copy.77), channel_id=1, replica_groups=mesh['ulysses'=8,'frame'=16,'quarter'=4] {'ulysses'}, dimensions={1} | all-to-all | bytes 5898240 | tf_op jit(solution)/shard_map/all_to_all | solution.py:95
  97.2 0.3 copy.78
  97.5 1.6 copy-done.6
  99.1 2.2 copy.79
  101.3 11.1 %all-to-all-start.1 = ((bf16[16,48,15,128]{3,1,2,0:T(8,128)(2,1)}), bf16[16,48,15,128]{3,1,2,0:T(8,128)(2,1)}, u32[]{:S(2)}, u32[]{:S(2)}) async-start(bf16[16,48,15,128]{3,1,2,0:T(8,128)(2,1)} %copy.79), calls=%async_computation.1 | async-start | bytes 5898240 | tf_op jit(solution)/shard_map/all_to_all | solution.py:97
  112.4 0.6 gather_fusion.7
  113.0 0.6 gather_fusion.6
  113.7 0.6 gather_fusion.5
  114.4 0.6 gather_fusion
  115.2 0.6 gather_fusion.2
  115.8 1.0 gather_fusion.4
  116.9 0.7 gather_fusion.1
  117.7 0.6 copy.86
  118.3 1.1 gather_fusion.3
  119.8 1.1 fusion.16
  121.0 1.9 collective-permute-start.2
  122.9 6.3 %collective-permute-start.3 = (bf16[128,10,128]{2,0,1:T(8,128)(2,1)S(1)}, bf16[128,10,128]{2,0,1:T(8,128)(2,1)S(1)}, u32[]{:S(2)}, u32[]{:S(2)}) collective-permute-start(bf16[128,10,128]{2,0,1:T(8,128)(2,1)S(1)} %get-tuple-element.11), channel_id=1, source_target_pairs={{1,0},{2,1},{3,2},{4,3},{5,4},{6,5},{7,6},{8,7},{9,8},{10,9},{11,1... | collective-permute-start | bytes 983048 | tf_op jit(solution)/shard_map/ppermute | solution.py:17
  129.2 82.6 %all-to-all-done.1 = bf16[16,48,15,128]{3,1,2,0:T(8,128)(2,1)} async-done(((bf16[16,48,15,128]{3,1,2,0:T(8,128)(2,1)}), bf16[16,48,15,128]{3,1,2,0:T(8,128)(2,1)}, u32[]{:S(2)}, u32[]{:S(2)}) %all-to-all-start.1) | async-done | bytes 2949152 | tf_op jit(solution)/shard_map/all_to_all | solution.py:97
  211.8 2.6 copy.80
  214.4 1.6 copy-done.7
  216.1 1.9 collective-permute-start
  218.0 5.9 %collective-permute-start.1 = (bf16[128,10,128]{2,0,1:T(8,128)(2,1)S(1)}, bf16[128,10,128]{2,0,1:T(8,128)(2,1)S(1)}, u32[]{:S(2)}, u32[]{:S(2)}) collective-permute-start(bf16[128,10,128]{2,0,1:T(8,128)(2,1)S(1)} %get-tuple-element.13), channel_id=1, source_target_pairs={{4,0},{8,4},{12,8},{16,12},{20,16},{24,20},{28,24},{32,28},{36,32}... | collective-permute-start | bytes 983048 | tf_op jit(solution)/shard_map/ppermute | solution.py:17
  224.0 0.1 copy.89
  224.1 1.9 slice.118
  226.0 0.6 copy-done.8
  226.6 0.1 slice.115
  226.7 1.4 slice_select_fusion
  228.1 6.4 %collective-permute-done = bf16[128,10,128]{2,0,1:T(8,128)(2,1)S(1)} collective-permute-done((bf16[128,10,128]{2,0,1:T(8,128)(2,1)S(1)}, bf16[128,10,128]{2,0,1:T(8,128)(2,1)S(1)}, u32[]{:S(2)}, u32[]{:S(2)}) %collective-permute-start) | collective-permute-done | bytes 327712 | tf_op jit(solution)/shard_map/ppermute | solution.py:16
  234.5 11.7 %collective-permute-done.1 = bf16[128,10,128]{2,0,1:T(8,128)(2,1)S(1)} collective-permute-done((bf16[128,10,128]{2,0,1:T(8,128)(2,1)S(1)}, bf16[128,10,128]{2,0,1:T(8,128)(2,1)S(1)}, u32[]{:S(2)}, u32[]{:S(2)}) %collective-permute-start.1) | collective-permute-done | bytes 327712 | tf_op jit(solution)/shard_map/ppermute | solution.py:17
  246.2 0.8 maximum_select_fusion
  247.1 0.8 fusion.18
  248.3 0.1 constant_dynamic-update-slice_fusion.6
  248.5 1.5 fusion
  250.1 3.0 fusion.1
  253.8 2.1 fusion.6
  255.9 0.3 copy.93
  256.2 31.2 %all_to_all.41 = bf16[16,48,5,128]{3,1,2,0:T(8,128)(2,1)S(1)} all-to-all(bf16[16,48,5,128]{3,1,2,0:T(8,128)(2,1)S(1)} %copy.93), channel_id=1, replica_groups=mesh['ulysses'=8,'frame'=16,'quarter'=4] {'frame'}, dimensions={0} | all-to-all | bytes 1966080 | tf_op jit(solution)/shard_map/all_to_all | solution.py:132
  287.5 0.2 bitcast_select_fusion
  287.7 0.7 copy.96
  288.5 42.0 %all_to_all.42 = bf16[768,1,5,128]{3,2,1,0:T(8,128)(2,1)S(1)} all-to-all(bf16[768,1,5,128]{3,2,1,0:T(8,128)(2,1)S(1)} %copy.96), channel_id=1, replica_groups=mesh['ulysses'=8,'frame'=16,'quarter'=4] {'ulysses'}, dimensions={0} | all-to-all | bytes 1966080 | tf_op jit(solution)/shard_map/all_to_all | solution.py:135
  330.5 0.1 copy.97
  330.6 0.8 copy.98
  331.4 1.4 copy.99
  (55 shorter events, 2.3 us)
Async XLA Ops:
  0.0 116.9 %copy-start = (s32[40,768,5]{1,0,2:T(8,128)S(1)}, s32[40,768,5]{1,0,2:T(8,128)}, u32[]{:S(2)}) copy-start(s32[40,768,5]{1,0,2:T(8,128)} %param.15) | copy-start | bytes 1843204
  97.5 1.6 copy-start.6
  99.1 13.3 %copy-start.2 = (f32[40]{0:T(128)S(1)}, f32[40]{0:T(128)}, u32[]{:S(2)}) copy-start(f32[40]{0:T(128)} %param.19) | copy-start | bytes 484
  99.1 13.9 %copy-start.3 = (f32[40]{0:T(128)S(1)}, f32[40]{0:T(128)}, u32[]{:S(2)}) copy-start(f32[40]{0:T(128)} %param.18) | copy-start | bytes 484
  101.3 12.4 %copy-start.4 = (f32[40]{0:T(128)S(1)}, f32[40]{0:T(128)}, u32[]{:S(2)}) copy-start(f32[40]{0:T(128)} %param.17) | copy-start | bytes 484
  101.3 13.1 %copy-start.5 = (s32[40]{0:T(128)S(1)}, s32[40]{0:T(128)}, u32[]{:S(2)}) copy-start(s32[40]{0:T(128)} %param.14) | copy-start | bytes 484
  101.3 13.9 %copy-start.9 = (s32[40,768]{1,0:T(8,128)S(1)}, s32[40,768]{1,0:T(8,128)}, u32[]{:S(2)}) copy-start(s32[40,768]{1,0:T(8,128)} %param.16) | copy-start | bytes 368644
  101.3 110.5 %all-to-all-start.1 = ((bf16[16,48,15,128]{3,1,2,0:T(8,128)(2,1)}), bf16[16,48,15,128]{3,1,2,0:T(8,128)(2,1)}, u32[]{:S(2)}, u32[]{:S(2)}) async-start(bf16[16,48,15,128]{3,1,2,0:T(8,128)(2,1)} %copy.79), calls=%async_computation.1 | async-start | bytes 5898240 | tf_op jit(solution)/shard_map/all_to_all | solution.py:97
  121.0 107.1 %collective-permute-start.2 = (bf16[128,10,128]{2,0,1:T(8,128)(2,1)S(1)}, bf16[128,10,128]{2,0,1:T(8,128)(2,1)S(1)}, u32[]{:S(2)}, u32[]{:S(2)}) collective-permute-start(bf16[128,10,128]{2,0,1:T(8,128)(2,1)S(1)} %get-tuple-element.10), channel_id=1, source_target_pairs={{0,1},{1,2},{2,3},{3,4},{4,5},{5,6},{6,7},{7,8},{8,9},{9,10},{10,1... | collective-permute-start | bytes 983048 | tf_op jit(solution)/shard_map/ppermute | solution.py:16
  122.9 105.2 %collective-permute-start.3 = (bf16[128,10,128]{2,0,1:T(8,128)(2,1)S(1)}, bf16[128,10,128]{2,0,1:T(8,128)(2,1)S(1)}, u32[]{:S(2)}, u32[]{:S(2)}) collective-permute-start(bf16[128,10,128]{2,0,1:T(8,128)(2,1)S(1)} %get-tuple-element.11), channel_id=1, source_target_pairs={{1,0},{2,1},{3,2},{4,3},{5,4},{6,5},{7,6},{8,7},{9,8},{10,9},{11,1... | collective-permute-start | bytes 983048 | tf_op jit(solution)/shard_map/ppermute | solution.py:17
  214.4 1.6 copy-start.7
  216.1 18.4 %collective-permute-start = (bf16[128,10,128]{2,0,1:T(8,128)(2,1)S(1)}, bf16[128,10,128]{2,0,1:T(8,128)(2,1)S(1)}, u32[]{:S(2)}, u32[]{:S(2)}) collective-permute-start(bf16[128,10,128]{2,0,1:T(8,128)(2,1)S(1)} %get-tuple-element.12), channel_id=1, source_target_pairs={{0,4},{4,8},{8,12},{12,16},{16,20},{20,24},{24,28},{28,32},{32,36}... | collective-permute-start | bytes 983048 | tf_op jit(solution)/shard_map/ppermute | solution.py:16
  218.0 28.2 %collective-permute-start.1 = (bf16[128,10,128]{2,0,1:T(8,128)(2,1)S(1)}, bf16[128,10,128]{2,0,1:T(8,128)(2,1)S(1)}, u32[]{:S(2)}, u32[]{:S(2)}) collective-permute-start(bf16[128,10,128]{2,0,1:T(8,128)(2,1)S(1)} %get-tuple-element.13), channel_id=1, source_target_pairs={{4,0},{8,4},{12,8},{16,12},{20,16},{24,20},{28,24},{32,28},{36,32}... | collective-permute-start | bytes 983048 | tf_op jit(solution)/shard_map/ppermute | solution.py:17
  224.1 2.4 copy-start.8
  287.7 45.0 %copy-start.1 = (s32[40,768,5]{1,0,2:T(8,128)S(1)}, s32[40,768,5]{1,0,2:T(8,128)}, u32[]{:S(2)}) copy-start(s32[40,768,5]{1,0,2:T(8,128)} %param.15) | copy-start | bytes 1843204

commit v2 on v1

--- a/solution.py
+++ b/solution.py
@@ -8,6 +8,7 @@
 FRAMES = 16
 MARGIN = 2
 BLOCK = 64
+TEMPORAL = 16
 
 
 def with_halo(cells, axes, order):
@@ -74,6 +75,8 @@
     head_count = labels.shape[0]
     width = queries.shape[1] // head_count
     per_group = head_count // groups
+    lines_per_group = TEMPORAL // groups
+    spaces_per_group = per_group - lines_per_group
     rows = tokens_here * groups
     blocks = rows // BLOCK
     piece = rows // frames
@@ -84,54 +87,66 @@
     spatial_slot = frame_index * quarters + quarter_index
     temporal_slot = quarter_index * frames + frame_index
 
+    ranked = jnp.argsort(1 - labels, stable=True).astype(jnp.int32)
+    slots = jnp.concatenate(
+        [
+            ranked[:TEMPORAL].reshape(groups, lines_per_group),
+            ranked[TEMPORAL:].reshape(groups, spaces_per_group),
+        ],
+        axis=1,
+    ).reshape(head_count)
+    unslots = jnp.argsort(slots).astype(jnp.int32)
+
+    def grouped(array):
+        picked = jnp.take(array.reshape(tokens_here, head_count, width), slots, axis=1)
+        return picked.reshape(tokens_here, groups, per_group, width)
+
+    gq, gk, gv = grouped(queries), grouped(key_vectors), grouped(value_vectors)
+    lo, hi = slice(0, lines_per_group), slice(lines_per_group, per_group)
     stacked = jnp.concatenate(
-        [
-            queries.reshape(tokens_here, groups, per_group, width),
-            key_vectors.reshape(tokens_here, groups, per_group, width),
-            value_vectors.reshape(tokens_here, groups, per_group, width),
-        ],
-        axis=2,
+        [gq[:, :, lo], gk[:, :, lo], gv[:, :, lo], gq[:, :, hi], gk[:, :, hi], gv[:, :, hi]], axis=2
     )
     frame_rows = lax.all_to_all(stacked, "ulysses", split_axis=1, concat_axis=0, tiled=True)
     frame_rows = frame_rows.reshape(rows, 3 * per_group, width)
+    line_part = frame_rows[:, : 3 * lines_per_group]
+    space_part = frame_rows[:, 3 * lines_per_group :]
     moved = lax.all_to_all(
-        frame_rows.reshape(frames, piece, 3 * per_group, width),
+        line_part.reshape(frames, piece, 3 * lines_per_group, width),
         "frame",
         split_axis=0,
         concat_axis=0,
         tiled=True,
     )
-    line_rows = jnp.transpose(moved, (1, 0, 2, 3)).reshape(rows, 3 * per_group, width)
+    line_rows = jnp.transpose(moved, (1, 0, 2, 3)).reshape(rows, 3 * lines_per_group, width)
 
     spatial_order = list(range(devices_along))
     temporal_order = [(k % frames) * quarters + k // frames for k in range(devices_along)]
-    frame_ext = with_halo(frame_rows[:, per_group:], ("frame", "quarter"), spatial_order)
-    line_ext = with_halo(line_rows[:, per_group:], ("frame", "quarter"), temporal_order)
+    space_ext = with_halo(space_part[:, spaces_per_group:], ("frame", "quarter"), spatial_order)
+    line_ext = with_halo(line_rows[:, lines_per_group:], ("frame", "quarter"), temporal_order)
 
-    head_ids = group_index * per_group + jnp.arange(per_group, dtype=jnp.int32)
-    temporal = jnp.take(labels, head_ids) == 1
-    doubled = jnp.concatenate([temporal, temporal])
-    query_rows = jnp.where(temporal[None, :, None], line_rows[:, :per_group], frame_rows[:, :per_group])
-    extended = jnp.where(doubled[None, :, None], line_ext, frame_ext)
-    base = jnp.where(temporal, temporal_slot * blocks, spatial_slot * blocks).astype(jnp.int32)
-    allowed = window_mask(block_lists, counts, head_ids, base, blocks)
+    group_heads = lax.dynamic_slice_in_dim(slots, group_index * per_group, per_group)
     logit_scale = (
-        jnp.take(query_scale, head_ids) * jnp.take(key_scale, head_ids) / math.sqrt(width)
+        jnp.take(query_scale, group_heads) * jnp.take(key_scale, group_heads) / math.sqrt(width)
     )
-    value_factor = jnp.take(value_scale, head_ids)
-    outputs = attend(
-        query_rows,
-        extended[:, :per_group],
-        extended[:, per_group:],
-        allowed,
-        logit_scale,
-        value_factor,
-    )
+    value_factor = jnp.take(value_scale, group_heads)
 
-    back = jnp.transpose(outputs.reshape(piece, frames, per_group, width), (1, 0, 2, 3))
+    def run(part_rows, ext, heads, base):
+        n = heads.stop - heads.start
+        ids = group_heads[heads]
+        allowed = window_mask(
+            block_lists, counts, ids, jnp.full((n,), base * blocks, jnp.int32), blocks
+        )
+        return attend(
+            part_rows[:, :n], ext[:, :n], ext[:, n:], allowed, logit_scale[heads], value_factor[heads]
+        )
+
+    line_out = run(line_rows, line_ext, lo, temporal_slot)
+    space_out = run(space_part, space_ext, hi, spatial_slot)
+
+    back = jnp.transpose(line_out.reshape(piece, frames, lines_per_group, width), (1, 0, 2, 3))
     returned = lax.all_to_all(back, "frame", split_axis=0, concat_axis=0, tiled=True)
-    returned = returned.reshape(rows, per_group, width)
-    frame_outputs = jnp.where(temporal[None, :, None], returned, outputs)
+    returned = returned.reshape(rows, lines_per_group, width)
+    frame_outputs = jnp.concatenate([returned, space_out], axis=1)
     merged = lax.all_to_all(
         frame_outputs.reshape(rows, 1, per_group, width),
         "ulysses",
@@ -139,6 +154,7 @@
         concat_axis=1,
         tiled=True,
     )
+    merged = jnp.take(merged.reshape(tokens_here, head_count, width), unslots, axis=1)
     return merged.reshape(tokens_here, head_count * width)
 
 

time: 333 us -> 249 us (0.75)
  the two profiles are of different devices: /device:TPU:48 before, /device:TPU:1 now
where the time goes in v2:
time: 249 us; the launch traced here: 244 us
  waiting for transfers between devices  96.9 us (39%)
  starting transfers between devices  79.3 us (32%)
  local copies, waits for them, and re-layouts  45.7 us (18%)
  other arithmetic  16 us (6%)
  matrix products  5.58 us (2%)
    ppermute x2, starting transfers between devices, with_halo(): upper = lax.ppermute(cells[:width], axes, [(b, a) for a, b in pairs])  41 us
    all_to_all x1, waiting for transfers between devices, shards(): lax.all_to_all(frame_outputs.reshape(rows, 1, per_group, width), 'ulysses...  35 us
    all_to_all x1, waiting for transfers between devices, shards(): lax.all_to_all(line_part.reshape(frames, piece, 3 * lines_per_group, widt...  23.9 us
    all_to_all x1, waiting for transfers between devices, shards(): lax.all_to_all(stacked, 'ulysses', split_axis=1, concat_axis=0, tiled=True)  23.5 us
    all_to_all x1, starting transfers between devices, shards(): lax.all_to_all(stacked, 'ulysses', split_axis=1, concat_axis=0, tiled=True)  13.4 us
    unnamed x59, local copies, waits for them, and re-layouts  13.4 us
    all_to_all x1, starting transfers between devices, shards(): lax.all_to_all(line_part.reshape(frames, piece, 3 * lines_per_group, widt...  9.82 us
    ppermute x2, waiting for transfers between devices, with_halo(): lower = lax.ppermute(cells[-width:], axes, pairs)  8.32 us
  transfers between devices with their start and end apart: 8, of which 5 were waited for; matrix products, arithmetic and copies ran while one was open for 13% of the time, Pallas kernels for 0%

profile of v2, /device:TPU:1, one launch (start us, length us, event | category | flops | bytes accessed | tf_op | source)
XLA Modules:
  0.0 244.2 jit_solution(9758885744973550119)
XLA Ops:
  0.7 2.0 sort.34
  3.4 1.0 copy-done.7
  6.1 2.3 copy_bitcast_fusion.1
  8.4 1.9 gather_fusion.10
  10.6 0.8 slice_dynamic-update-slice_fusion.5
  11.5 0.9 slice_dynamic-update-slice_fusion.4
  12.3 0.8 slice_dynamic-update-slice_fusion.3
  13.2 1.0 slice_dynamic-update-slice_fusion.2
  14.2 0.9 slice_dynamic-update-slice_fusion.1
  15.1 0.9 slice_dynamic-update-slice_fusion
  16.1 13.4 %all-to-all-start = ((bf16[96,8,15,128]{3,0,2,1:T(8,128)(2,1)}), bf16[96,8,15,128]{3,0,2,1:T(8,128)(2,1)}, u32[]{:S(2)}, u32[]{:S(2)}) async-start(bf16[96,8,15,128]{3,0,2,1:T(8,128)(2,1)} %slice_dynamic-update-slice_fusion), calls=%async_computation | async-start | bytes 5898240 | tf_op jit(solution)/shard_map/all_to_all | solution.py:109
  29.5 2.0 sort.35
  37.9 0.9 gather_fusion.5
  38.9 1.1 gather_fusion.7
  42.0 0.9 gather_fusion.6
  43.3 23.5 %all-to-all-done = bf16[96,8,15,128]{3,0,2,1:T(8,128)(2,1)} async-done(((bf16[96,8,15,128]{3,0,2,1:T(8,128)(2,1)}), bf16[96,8,15,128]{3,0,2,1:T(8,128)(2,1)}, u32[]{:S(2)}, u32[]{:S(2)}) %all-to-all-start) | async-done | bytes 2949152 | tf_op jit(solution)/shard_map/all_to_all | solution.py:109
  66.9 2.1 copy.141
  69.7 1.2 fusion.57
  70.9 35.1 %collective-permute-start.3 = (bf16[128,6,128]{2,0,1:T(8,128)(2,1)}, bf16[128,6,128]{2,0,1:T(8,128)(2,1)S(1)}, u32[]{:S(2)}, u32[]{:S(2)}) collective-permute-start(bf16[128,6,128]{2,0,1:T(8,128)(2,1)} %get-tuple-element.30), channel_id=1, source_target_pairs={{1,0},{2,1},{3,2},{4,3},{5,4},{6,5},{7,6},{8,7},{9,8},{10,9},{11,1... | collective-permute-start | bytes 589832 | tf_op jit(solution)/shard_map/ppermute | solution.py:18
  106.0 1.9 collective-permute-start.2
  107.9 1.1 copy.142
  109.0 9.8 %all-to-all-start.1 = ((bf16[16,48,6,128]{3,1,2,0:T(8,128)(2,1)}), bf16[16,48,6,128]{3,1,2,0:T(8,128)(2,1)}, u32[]{:S(2)}, u32[]{:S(2)}) async-start(bf16[16,48,6,128]{3,1,2,0:T(8,128)(2,1)} %copy.142), calls=%async_computation.1 | async-start | bytes 2359296 | tf_op jit(solution)/shard_map/all_to_all | solution.py:113
  118.9 0.9 fusion.58
  121.2 3.9 %fusion.44 = (bf16[768,3,128]{2,0,1:T(8,128)(2,1)S(1)}, bf16[768,3,128]{2,0,1:T(8,128)(2,1)}, bf16[768,3,128]{2,0,1:T(8,128)(2,1)S(1)}, bf16[768,3,128]{2,0,1:T(...) fusion(bf16[768,6,128]{2,0,1:T(8,128)(2,1)S(1)} %copy-done.6, ...), kind=kLoop, calls=%fused_computation.72 | loop fusion | flops 9437184 | bytes 6291456 | tf_op jit(solution)/shard_map/concatenate | solution.py:19
  125.6 1.6 copy-done.11
  127.2 1.0 fusion
  128.2 1.8 fusion.1
  130.7 23.9 %all-to-all-done.1 = bf16[16,48,6,128]{3,1,2,0:T(8,128)(2,1)} async-done(((bf16[16,48,6,128]{3,1,2,0:T(8,128)(2,1)}), bf16[16,48,6,128]{3,1,2,0:T(8,128)(2,1)}, u32[]{:S(2)}, u32[]{:S(2)}) %all-to-all-start.1) | async-done | bytes 1179680 | tf_op jit(solution)/shard_map/all_to_all | solution.py:113
  154.6 1.7 copy.143
  156.4 5.9 %collective-permute-start.1 = (bf16[128,4,128]{2,0,1:T(8,128)(2,1)S(1)}, bf16[128,4,128]{2,0,1:T(8,128)(2,1)S(1)}, u32[]{:S(2)}, u32[]{:S(2)}) collective-permute-start(bf16[128,4,128]{2,0,1:T(8,128)(2,1)S(1)} %get-tuple-element.43), channel_id=1, source_target_pairs={{4,0},{8,4},{12,8},{16,12},{20,16},{24,20},{28,24},{32,28},{36,32}... | collective-permute-start | bytes 393224 | tf_op jit(solution)/shard_map/ppermute | solution.py:18
  162.3 2.1 collective-permute-start
  164.6 8.3 %collective-permute-done = bf16[128,4,128]{2,0,1:T(8,128)(2,1)S(1)} collective-permute-done((bf16[128,4,128]{2,0,1:T(8,128)(2,1)S(1)}, bf16[128,4,128]{2,0,1:T(8,128)(2,1)S(1)}, u32[]{:S(2)}, u32[]{:S(2)}) %collective-permute-start) | collective-permute-done | bytes 131104 | tf_op jit(solution)/shard_map/ppermute | solution.py:17
  174.9 1.2 fusion.4
  176.4 0.8 fusion.37
  177.3 0.8 copy.156
  178.1 6.7 %all-to-all-start.2 = ((bf16[16,48,2,128]{3,1,2,0:T(8,128)(2,1)}), bf16[16,48,2,128]{3,1,2,0:T(8,128)(2,1)}, u32[]{:S(2)}, u32[]{:S(2)}) async-start(bf16[16,48,2,128]{3,1,2,0:T(8,128)(2,1)} %copy.156), calls=%async_computation.2 | async-start | bytes 786432 | tf_op jit(solution)/shard_map/all_to_all | solution.py:147
  184.9 1.9 constant_dynamic-update-slice_fusion.12
  186.8 0.7 copy.167
  187.6 1.9 constant_dynamic-update-slice_fusion.11
  189.5 0.9 constant_dynamic-update-slice_fusion.10
  190.3 3.0 %fusion.22 = bf16[12,64,3,128]{3,1,2,0:T(8,128)(2,1)S(1)} fusion(bf16[3,12,64,5,64]{2,4,3,1,0:T(8,128)(2,1)S(1)} %get-tuple-element.22, bf16[12,5,64,3,128]{4,2,0,3,1:T(8,128)(2,1)} %constant_dynamic-update-slice_fusion.10, f32[12,64,3]{1,2,0:T(4,128)S(1)} %copy.167), kind=kOutput, calls=%fused_computation.45 | convolution fusion | flops 189333504 | bytes 5022720 | tf_op jit(solution)/shard_map/hbqok,bokhd->bqhd/dot_general | solution.py:51
  193.4 6.1 %all-to-all-done.2 = bf16[16,48,2,128]{3,1,2,0:T(8,128)(2,1)} async-done(((bf16[16,48,2,128]{3,1,2,0:T(8,128)(2,1)}), bf16[16,48,2,128]{3,1,2,0:T(8,128)(2,1)}, u32[]{:S(2)}, u32[]{:S(2)}) %all-to-all-start.2) | async-done | bytes 393248 | tf_op jit(solution)/shard_map/all_to_all | solution.py:147
  199.5 1.0 copy.157
  200.7 1.9 copy.169
  202.6 4.2 %all-to-all-start.3 = ((bf16[768,1,5,128]{3,2,1,0:T(8,128)(2,1)}), bf16[768,1,5,128]{3,2,1,0:T(8,128)(2,1)S(1)}, u32[]{:S(2)}, u32[]{:S(2)}) async-start(bf16[768,1,5,128]{3,2,1,0:T(8,128)(2,1)} %copy.169), calls=%async_computation.3 | async-start | bytes 3145728 | tf_op jit(solution)/shard_map/all_to_all | solution.py:150
  206.8 35.0 %all-to-all-done.3 = bf16[768,1,5,128]{3,2,1,0:T(8,128)(2,1)S(1)} async-done(((bf16[768,1,5,128]{3,2,1,0:T(8,128)(2,1)}), bf16[768,1,5,128]{3,2,1,0:T(8,128)(2,1)S(1)}, u32[]{:S(2)}, u32[]{:S(2)}) %all-to-all-start.3) | async-done | bytes 983072 | tf_op jit(solution)/shard_map/all_to_all | solution.py:150
  242.0 1.0 gather_fusion.14
  243.0 1.2 copy_bitcast_fusion
  (137 shorter events, 17.9 us)
Async XLA Ops:
  0.0 3.2 %copy-start = (bf16[96,5120]{1,0:T(8,128)(2,1)S(1)}, bf16[96,5120]{1,0:T(8,128)(2,1)}, u32[]{:S(2)}) copy-start(bf16[96,5120]{1,0:T(8,128)(2,1)} %param.13) | copy-start | bytes 2949124
  3.2 1.2 copy-start.7
  16.1 15.6 %copy-start.10 = (s32[40,768]{1,0:T(8,128)S(1)}, s32[40,768]{1,0:T(8,128)}, u32[]{:S(2)}) copy-start(s32[40,768]{1,0:T(8,128)} %param.18) | copy-start | bytes 368644
  16.1 17.4 %copy-start.5 = (s32[40,768,5]{1,0,2:T(8,128)S(1)}, s32[40,768,5]{1,0,2:T(8,128)}, u32[]{:S(2)}) copy-start(s32[40,768,5]{1,0,2:T(8,128)} %param.17) | copy-start | bytes 1843204
  16.1 50.8 %all-to-all-start = ((bf16[96,8,15,128]{3,0,2,1:T(8,128)(2,1)}), bf16[96,8,15,128]{3,0,2,1:T(8,128)(2,1)}, u32[]{:S(2)}, u32[]{:S(2)}) async-start(bf16[96,8,15,128]{3,0,2,1:T(8,128)(2,1)} %slice_dynamic-update-slice_fusion), calls=%async_computation | async-start | bytes 5898240 | tf_op jit(solution)/shard_map/all_to_all | solution.py:109
  31.5 0.7 copy-start.17
  34.1 1.0 copy-start.2
  34.2 1.6 copy-start.3
  34.2 2.3 copy-start.4
  37.1 2.9 %copy-start.12 = (f32[5]{0:T(128)}, f32[5]{0:T(128)S(1)}, u32[]{:S(2)}) copy-start(f32[5]{0:T(128)S(1)} %get-tuple-element.62) | copy-start | bytes 64
  37.1 2.9 %copy-start.14 = (f32[5]{0:T(128)}, f32[5]{0:T(128)S(1)}, u32[]{:S(2)}) copy-start(f32[5]{0:T(128)S(1)} %get-tuple-element.61) | copy-start | bytes 64
  70.9 48.9 %collective-permute-start.3 = (bf16[128,6,128]{2,0,1:T(8,128)(2,1)}, bf16[128,6,128]{2,0,1:T(8,128)(2,1)S(1)}, u32[]{:S(2)}, u32[]{:S(2)}) collective-permute-start(bf16[128,6,128]{2,0,1:T(8,128)(2,1)} %get-tuple-element.30), channel_id=1, source_target_pairs={{1,0},{2,1},{3,2},{4,3},{5,4},{6,5},{7,6},{8,7},{9,8},{10,9},{11,1... | collective-permute-start | bytes 589832 | tf_op jit(solution)/shard_map/ppermute | solution.py:18
  106.0 13.8 %collective-permute-start.2 = (bf16[128,6,128]{2,0,1:T(8,128)(2,1)S(1)}, bf16[128,6,128]{2,0,1:T(8,128)(2,1)S(1)}, u32[]{:S(2)}, u32[]{:S(2)}) collective-permute-start(bf16[128,6,128]{2,0,1:T(8,128)(2,1)S(1)} %get-tuple-element.31), channel_id=1, source_target_pairs={{0,1},{1,2},{2,3},{3,4},{4,5},{5,6},{6,7},{7,8},{8,9},{9,10},{10,1... | collective-permute-start | bytes 589832 | tf_op jit(solution)/shard_map/ppermute | solution.py:17
  109.0 45.6 %all-to-all-start.1 = ((bf16[16,48,6,128]{3,1,2,0:T(8,128)(2,1)}), bf16[16,48,6,128]{3,1,2,0:T(8,128)(2,1)}, u32[]{:S(2)}, u32[]{:S(2)}) async-start(bf16[16,48,6,128]{3,1,2,0:T(8,128)(2,1)} %copy.142), calls=%async_computation.1 | async-start | bytes 2359296 | tf_op jit(solution)/shard_map/all_to_all | solution.py:113
  118.9 2.3 copy-start.6
  119.8 0.7 copy-start.8
  120.5 0.7 copy-start.9
  125.6 1.6 copy-start.11
  128.2 1.8 copy-start.16
  156.4 8.2 %collective-permute-start.1 = (bf16[128,4,128]{2,0,1:T(8,128)(2,1)S(1)}, bf16[128,4,128]{2,0,1:T(8,128)(2,1)S(1)}, u32[]{:S(2)}, u32[]{:S(2)}) collective-permute-start(bf16[128,4,128]{2,0,1:T(8,128)(2,1)S(1)} %get-tuple-element.43), channel_id=1, source_target_pairs={{4,0},{8,4},{12,8},{16,12},{20,16},{24,20},{28,24},{32,28},{36,32}... | collective-permute-start | bytes 393224 | tf_op jit(solution)/shard_map/ppermute | solution.py:18
  162.3 10.6 %collective-permute-start = (bf16[128,4,128]{2,0,1:T(8,128)(2,1)S(1)}, bf16[128,4,128]{2,0,1:T(8,128)(2,1)S(1)}, u32[]{:S(2)}, u32[]{:S(2)}) collective-permute-start(bf16[128,4,128]{2,0,1:T(8,128)(2,1)S(1)} %get-tuple-element.44), channel_id=1, source_target_pairs={{0,4},{4,8},{8,12},{12,16},{16,20},{20,24},{24,28},{28,32},{32,36}... | collective-permute-start | bytes 393224 | tf_op jit(solution)/shard_map/ppermute | solution.py:17
  173.5 0.6 copy-start.13
  174.8 1.2 copy-start.15
  178.1 21.4 %all-to-all-start.2 = ((bf16[16,48,2,128]{3,1,2,0:T(8,128)(2,1)}), bf16[16,48,2,128]{3,1,2,0:T(8,128)(2,1)}, u32[]{:S(2)}, u32[]{:S(2)}) async-start(bf16[16,48,2,128]{3,1,2,0:T(8,128)(2,1)} %copy.156), calls=%async_computation.2 | async-start | bytes 786432 | tf_op jit(solution)/shard_map/all_to_all | solution.py:147
  202.6 4.3 %copy-start.18 = (s32[40]{0:T(128)S(1)}, s32[40]{0:T(128)}, u32[]{:S(2)}) copy-start(s32[40]{0:T(128)} %copy-done.17) | copy-start | bytes 484
  202.6 39.2 %all-to-all-start.3 = ((bf16[768,1,5,128]{3,2,1,0:T(8,128)(2,1)}), bf16[768,1,5,128]{3,2,1,0:T(8,128)(2,1)S(1)}, u32[]{:S(2)}, u32[]{:S(2)}) async-start(bf16[768,1,5,128]{3,2,1,0:T(8,128)(2,1)} %copy.169), calls=%async_computation.3 | async-start | bytes 3145728 | tf_op jit(solution)/shard_map/all_to_all | solution.py:150
  242.0 2.2 copy-start.1

commit v3 on v2

--- a/solution.py
+++ b/solution.py
@@ -9,6 +9,7 @@
 MARGIN = 2
 BLOCK = 64
 TEMPORAL = 16
+HEAD_SPLIT = 4
 
 
 def with_halo(cells, axes, order):
@@ -67,10 +68,10 @@
     key_scale,
     value_scale,
 ):
-    groups = lax.axis_size("ulysses")
+    groups = lax.axis_size("x")
+    halves = lax.axis_size("zh")
     frames = lax.axis_size("frame")
     quarters = lax.axis_size("quarter")
-    devices_along = frames * quarters
     tokens_here = queries.shape[0]
     head_count = labels.shape[0]
     width = queries.shape[1] // head_count
@@ -80,12 +81,14 @@
     rows = tokens_here * groups
     blocks = rows // BLOCK
     piece = rows // frames
+    chunks = frames * quarters * halves
 
-    group_index = lax.axis_index("ulysses")
+    group_index = lax.axis_index("x")
+    half_index = lax.axis_index("zh")
     frame_index = lax.axis_index("frame")
     quarter_index = lax.axis_index("quarter")
-    spatial_slot = frame_index * quarters + quarter_index
-    temporal_slot = quarter_index * frames + frame_index
+    spatial_slot = (frame_index * quarters + quarter_index) * halves + half_index
+    temporal_slot = (quarter_index * halves + half_index) * frames + frame_index
 
     ranked = jnp.argsort(1 - labels, stable=True).astype(jnp.int32)
     slots = jnp.concatenate(
@@ -106,7 +109,7 @@
     stacked = jnp.concatenate(
         [gq[:, :, lo], gk[:, :, lo], gv[:, :, lo], gq[:, :, hi], gk[:, :, hi], gv[:, :, hi]], axis=2
     )
-    frame_rows = lax.all_to_all(stacked, "ulysses", split_axis=1, concat_axis=0, tiled=True)
+    frame_rows = lax.all_to_all(stacked, "x", split_axis=1, concat_axis=0, tiled=True)
     frame_rows = frame_rows.reshape(rows, 3 * per_group, width)
     line_part = frame_rows[:, : 3 * lines_per_group]
     space_part = frame_rows[:, 3 * lines_per_group :]
@@ -119,10 +122,18 @@
     )
     line_rows = jnp.transpose(moved, (1, 0, 2, 3)).reshape(rows, 3 * lines_per_group, width)
 
-    spatial_order = list(range(devices_along))
-    temporal_order = [(k % frames) * quarters + k // frames for k in range(devices_along)]
-    space_ext = with_halo(space_part[:, spaces_per_group:], ("frame", "quarter"), spatial_order)
-    line_ext = with_halo(line_rows[:, lines_per_group:], ("frame", "quarter"), temporal_order)
+    def linear(half, frame, quarter):
+        return (half * frames + frame) * quarters + quarter
+
+    spatial_order = [
+        linear(k % halves, k // (halves * quarters), (k // halves) % quarters) for k in range(chunks)
+    ]
+    temporal_order = [
+        linear((k // frames) % halves, k % frames, k // (frames * halves)) for k in range(chunks)
+    ]
+    along = ("zh", "frame", "quarter")
+    space_ext = with_halo(space_part[:, spaces_per_group:], along, spatial_order)
+    line_ext = with_halo(line_rows[:, lines_per_group:], along, temporal_order)
 
     group_heads = lax.dynamic_slice_in_dim(slots, group_index * per_group, per_group)
     logit_scale = (
@@ -149,7 +160,7 @@
     frame_outputs = jnp.concatenate([returned, space_out], axis=1)
     merged = lax.all_to_all(
         frame_outputs.reshape(rows, 1, per_group, width),
-        "ulysses",
+        "x",
         split_axis=0,
         concat_axis=1,
         tiled=True,
@@ -160,10 +171,12 @@
 
 def solution(mesh):
     ulysses, context = mesh.devices.shape
+    halves = mesh.devices.size // (context * HEAD_SPLIT)
     fine = Mesh(
-        mesh.devices.reshape(ulysses, FRAMES, context // FRAMES), ("ulysses", "frame", "quarter")
+        mesh.devices.reshape(halves, HEAD_SPLIT, FRAMES, context // FRAMES),
+        ("zh", "x", "frame", "quarter"),
     )
-    rows = P(("frame", "quarter", "ulysses"), None)
+    rows = P(("frame", "quarter", "zh", "x"), None)
     placed = (rows, rows, rows, P(), P(), P(), P(), P(), P())
     return jax.shard_map(
         shards,

time: 249 us -> 220 us (0.88); the launches traced: 244 us -> 218 us
  starting transfers between devices: 79.3 us -> 60.1 us
  waiting for transfers between devices: 96.9 us -> 90.5 us
    all_to_all x2, waiting for transfers between devices: 58.5 us -> 34.3 us  [the longest x1 19.5 us: shards(): lax.all_to_all(frame_outputs.reshape(rows, 1, per_group, width), 'x', spl...]
    ppermute x2, waiting for transfers between devices: 8.32 us -> 30.4 us  [with_halo(): lower = lax.ppermute(cells[-width:], axes, pairs)]
    all_to_all x2, starting transfers between devices: 17.7 us -> 8.67 us  [the longest x1 4.97 us: shards(): lax.all_to_all(stacked, 'x', split_axis=1, concat_axis=0, tiled=True)]
    ppermute x2, starting transfers between devices: 41 us -> 34.4 us  [with_halo(): upper = lax.ppermute(cells[:width], axes, [(b, a) for a, b in pairs])]
    all_to_all x1, waiting for transfers between devices: 23.9 us -> 19.6 us  [shards(): lax.all_to_all(line_part.reshape(frames, piece, 3 * lines_per_group, widt...]
    all_to_all x1, starting transfers between devices: 6.73 us -> 4.2 us  [shards(): lax.all_to_all(back, 'frame', split_axis=0, concat_axis=0, tiled=True)]
  transfers between devices with their start and end apart: 8 -> 8, of which waited for: 5 -> 7; matrix products, arithmetic and copies ran while one was open for 13% -> 15% of each run, Pallas kernels for 0% -> 0%
where the time goes in v3:
time: 220 us; the launch traced here: 218 us
  waiting for transfers between devices  90.5 us (41%)
  starting transfers between devices  60.1 us (27%)
  local copies, waits for them, and re-layouts  46.4 us (21%)
  other arithmetic  14.9 us (7%)
  matrix products  5.76 us (3%)
    ppermute x2, starting transfers between devices, with_halo(): upper = lax.ppermute(cells[:width], axes, [(b, a) for a, b in pairs])  34.4 us
    ppermute x2, waiting for transfers between devices, with_halo(): lower = lax.ppermute(cells[-width:], axes, pairs)  30.4 us
    all_to_all x1, waiting for transfers between devices, shards(): lax.all_to_all(line_part.reshape(frames, piece, 3 * lines_per_group, widt...  19.6 us
    all_to_all x1, waiting for transfers between devices, shards(): lax.all_to_all(frame_outputs.reshape(rows, 1, per_group, width), 'x', spl...  19.5 us
    all_to_all x1, waiting for transfers between devices, shards(): lax.all_to_all(stacked, 'x', split_axis=1, concat_axis=0, tiled=True)  14.8 us
    unnamed x59, local copies, waits for them, and re-layouts  12.7 us
    all_to_all x1, starting transfers between devices, shards(): lax.all_to_all(line_part.reshape(frames, piece, 3 * lines_per_group, widt...  8.79 us
    all_to_all x1, waiting for transfers between devices, shards(): lax.all_to_all(back, 'frame', split_axis=0, concat_axis=0, tiled=True)  5.07 us
  transfers between devices with their start and end apart: 8, of which 7 were waited for; matrix products, arithmetic and copies ran while one was open for 15% of the time, Pallas kernels for 0%

profile of v3, /device:TPU:1, one launch (start us, length us, event | category | flops | bytes accessed | tf_op | source)
XLA Modules:
  0.0 218.3 jit_solution(10774655429919809422)
XLA Ops:
  0.7 2.0 sort.34
  3.4 1.0 copy-done.7
  6.1 2.3 %copy_bitcast_fusion.1 = bf16[96,40,128]{2,0,1:T(8,128)(2,1)} fusion(bf16[96,5120]{1,0:T(8,128)(2,1)} %param.15), kind=kLoop, calls=%fused_computation.62 | loop fusion | bytes 1966080 | tf_op jit(solution)/shard_map/reshape | solution.py:104
  8.4 1.9 gather_fusion.10
  10.7 0.9 slice_dynamic-update-slice_fusion.5
  11.5 0.8 slice_dynamic-update-slice_fusion.4
  12.4 0.9 slice_dynamic-update-slice_fusion.3
  13.2 0.9 slice_dynamic-update-slice_fusion.2
  14.1 1.0 slice_dynamic-update-slice_fusion.1
  15.1 0.9 slice_dynamic-update-slice_fusion
  16.0 5.0 %all-to-all-start = ((bf16[96,4,30,128]{3,0,2,1:T(8,128)(2,1)}), bf16[96,4,30,128]{3,0,2,1:T(8,128)(2,1)}, u32[]{:S(2)}, u32[]{:S(2)}) async-start(bf16[96,4,30,128]{3,0,2,1:T(8,128)(2,1)} %slice_dynamic-update-slice_fusion), calls=%async_computation | async-start | bytes 5898240 | tf_op jit(solution)/shard_map/all_to_all | solution.py:112
  21.3 2.0 sort.35
  30.0 0.9 gather_fusion.5
  31.0 1.0 gather_fusion.7
  34.6 0.9 gather_fusion.6
  35.9 14.8 %all-to-all-done = bf16[96,4,30,128]{3,0,2,1:T(8,128)(2,1)} async-done(((bf16[96,4,30,128]{3,0,2,1:T(8,128)(2,1)}), bf16[96,4,30,128]{3,0,2,1:T(8,128)(2,1)}, u32[]{:S(2)}, u32[]{:S(2)}) %all-to-all-start) | async-done | bytes 2949152 | tf_op jit(solution)/shard_map/all_to_all | solution.py:112
  50.6 2.2 %copy.141 = bf16[4,96,1,30,128]{4,1,0,3,2:T(8,128)(2,1)S(1)} copy(bf16[4,96,1,30,128]{4,1,3,0,2:T(8,128)(2,1)} %bitcast.10) | data formatting | bytes 5898240 | tf_op jit(solution)/shard_map/all_to_all | solution.py:112
  52.9 0.9 fusion.61
  53.8 18.0 %collective-permute-start.3 = (bf16[128,12,128]{2,0,1:T(8,128)(2,1)}, bf16[128,12,128]{2,0,1:T(8,128)(2,1)S(1)}, u32[]{:S(2)}, u32[]{:S(2)}) collective-permute-start(bf16[128,12,128]{2,0,1:T(8,128)(2,1)} %get-tuple-element.30), channel_id=1, source_target_pairs={{256,0},{1,256},{257,1},{2,257},{258,2},{3,258},{259,3},{4,259},{2... | collective-permute-start | bytes 1179656 | tf_op jit(solution)/shard_map/ppermute | solution.py:19
  71.8 1.9 collective-permute-start.2
  73.7 1.2 fusion.59
  74.9 1.2 copy.142
  76.1 8.8 %all-to-all-start.1 = ((bf16[16,24,12,128]{3,1,2,0:T(8,128)(2,1)}), bf16[16,24,12,128]{3,1,2,0:T(8,128)(2,1)}, u32[]{:S(2)}, u32[]{:S(2)}) async-start(bf16[16,24,12,128]{3,1,2,0:T(8,128)(2,1)} %copy.142), calls=%async_computation.1 | async-start | bytes 2359296 | tf_op jit(solution)/shard_map/all_to_all | solution.py:116
  85.0 0.9 fusion.60
  85.9 15.6 %collective-permute-done.2 = bf16[128,12,128]{2,0,1:T(8,128)(2,1)} collective-permute-done((bf16[128,12,128]{2,0,1:T(8,128)(2,1)}, bf16[128,12,128]{2,0,1:T(8,128)(2,1)}, u32[]{:S(2)}, u32[]{:S(2)}) %collective-permute-start.2) | collective-permute-done | bytes 393248 | tf_op jit(solution)/shard_map/ppermute | solution.py:18
  101.5 3.4 %fusion.44 = (bf16[384,6,128]{2,0,1:T(8,128)(2,1)S(1)}, bf16[384,6,128]{2,0,1:T(8,128)(2,1)}, bf16[384,6,128]{2,0,1:T(8,128)(2,1)S(1)}, bf16[384,6,128]{2,0,1:T(...) fusion(bf16[384,12,128]{2,0,1:T(8,128)(2,1)S(1)} %copy-done.6, ...), kind=kLoop, calls=%fused_computation.72 | loop fusion | flops 9437184 | bytes 6684672 | tf_op jit(solution)/shard_map/concatenate | solution.py:20
  105.5 1.6 copy-done.10
  107.1 1.2 fusion
  108.3 1.9 fusion.1
  110.8 19.6 %all-to-all-done.1 = bf16[16,24,12,128]{3,1,2,0:T(8,128)(2,1)} async-done(((bf16[16,24,12,128]{3,1,2,0:T(8,128)(2,1)}), bf16[16,24,12,128]{3,1,2,0:T(8,128)(2,1)}, u32[]{:S(2)}, u32[]{:S(2)}) %all-to-all-start.1) | async-done | bytes 1179680 | tf_op jit(solution)/shard_map/all_to_all | solution.py:116
  130.4 1.7 copy.143
  132.3 16.4 %collective-permute-start.1 = (bf16[128,8,128]{2,0,1:T(8,128)(2,1)S(1)}, bf16[128,8,128]{2,0,1:T(8,128)(2,1)S(1)}, u32[]{:S(2)}, u32[]{:S(2)}) collective-permute-start(bf16[128,8,128]{2,0,1:T(8,128)(2,1)S(1)} %get-tuple-element.43), channel_id=1, source_target_pairs={{4,0},{8,4},{12,8},{16,12},{20,16},{24,20},{28,24},{32,28},{36,32}... | collective-permute-start | bytes 786440 | tf_op jit(solution)/shard_map/ppermute | solution.py:19
  148.7 2.1 collective-permute-start
  150.9 1.1 collective-permute-done.1
  152.0 14.7 %collective-permute-done = bf16[128,8,128]{2,0,1:T(8,128)(2,1)S(1)} collective-permute-done((bf16[128,8,128]{2,0,1:T(8,128)(2,1)S(1)}, bf16[128,8,128]{2,0,1:T(8,128)(2,1)S(1)}, u32[]{:S(2)}, u32[]{:S(2)}) %collective-permute-start) | collective-permute-done | bytes 262176 | tf_op jit(solution)/shard_map/ppermute | solution.py:18
  168.6 1.2 fusion.4
  171.1 0.8 copy.155
  171.9 4.2 %all-to-all-start.2 = ((bf16[16,24,4,128]{3,1,2,0:T(8,128)(2,1)}), bf16[16,24,4,128]{3,1,2,0:T(8,128)(2,1)}, u32[]{:S(2)}, u32[]{:S(2)}) async-start(bf16[16,24,4,128]{3,1,2,0:T(8,128)(2,1)} %copy.155), calls=%async_computation.2 | async-start | bytes 786432 | tf_op jit(solution)/shard_map/all_to_all | solution.py:158
  176.1 2.0 constant_dynamic-update-slice_fusion.12
  178.8 1.9 constant_dynamic-update-slice_fusion.11
  180.8 0.9 constant_dynamic-update-slice_fusion.10
  181.6 3.0 %fusion.22 = bf16[6,64,6,128]{3,1,2,0:T(8,128)(2,1)S(1)} fusion(bf16[6,6,64,5,64]{2,4,3,1,0:T(8,128)(2,1)S(1)} %get-tuple-element.22, bf16[6,5,64,6,128]{4,2,0,3,1:T(8,128)(2,1)} %constant_dynamic-update-slice_fusion.10, f32[6,64,6]{1,2,0:T(8,128)S(1)} %copy.166), kind=kOutput, calls=%fused_computation.51 | convolution fusion | flops 189333504 | bytes 5022720 | tf_op jit(solution)/shard_map/hbqok,bokhd->bqhd/dot_general | solution.py:52
  184.7 5.1 %all-to-all-done.2 = bf16[16,24,4,128]{3,1,2,0:T(8,128)(2,1)} async-done(((bf16[16,24,4,128]{3,1,2,0:T(8,128)(2,1)}), bf16[16,24,4,128]{3,1,2,0:T(8,128)(2,1)}, u32[]{:S(2)}, u32[]{:S(2)}) %all-to-all-start.2) | async-done | bytes 393248 | tf_op jit(solution)/shard_map/all_to_all | solution.py:158
  189.8 1.0 copy.156
  190.9 1.9 copy.168
  192.8 3.7 %all-to-all-start.3 = ((bf16[384,1,10,128]{3,2,1,0:T(8,128)(2,1)}), bf16[384,1,10,128]{3,2,1,0:T(8,128)(2,1)S(1)}, u32[]{:S(2)}, u32[]{:S(2)}) async-start(bf16[384,1,10,128]{3,2,1,0:T(8,128)(2,1)} %copy.168), calls=%async_computation.3 | async-start | bytes 3145728 | tf_op jit(solution)/shard_map/all_to_all | solution.py:161
  196.5 19.5 %all-to-all-done.3 = bf16[384,1,10,128]{3,2,1,0:T(8,128)(2,1)S(1)} async-done(((bf16[384,1,10,128]{3,2,1,0:T(8,128)(2,1)}), bf16[384,1,10,128]{3,2,1,0:T(8,128)(2,1)S(1)}, u32[]{:S(2)}, u32[]{:S(2)}) %all-to-all-start.3) | async-done | bytes 983072 | tf_op jit(solution)/shard_map/all_to_all | solution.py:161
  217.1 1.2 copy_bitcast_fusion
  (136 shorter events, 19.5 us)
Async XLA Ops:
  0.0 3.2 %copy-start = (bf16[96,5120]{1,0:T(8,128)(2,1)S(1)}, bf16[96,5120]{1,0:T(8,128)(2,1)}, u32[]{:S(2)}) copy-start(bf16[96,5120]{1,0:T(8,128)(2,1)} %param.13) | copy-start | bytes 2949124
  3.2 1.2 copy-start.7
  16.0 7.8 %copy-start.8 = (s32[40,768]{1,0:T(8,128)S(1)}, s32[40,768]{1,0:T(8,128)}, u32[]{:S(2)}) copy-start(s32[40,768]{1,0:T(8,128)} %param.18) | copy-start | bytes 368644
  16.0 8.9 %copy-start.2 = (s32[40,768,5]{1,0,2:T(8,128)S(1)}, s32[40,768,5]{1,0,2:T(8,128)}, u32[]{:S(2)}) copy-start(s32[40,768,5]{1,0,2:T(8,128)} %param.17) | copy-start | bytes 1843204
  16.0 34.6 %all-to-all-start = ((bf16[96,4,30,128]{3,0,2,1:T(8,128)(2,1)}), bf16[96,4,30,128]{3,0,2,1:T(8,128)(2,1)}, u32[]{:S(2)}, u32[]{:S(2)}) async-start(bf16[96,4,30,128]{3,0,2,1:T(8,128)(2,1)} %slice_dynamic-update-slice_fusion), calls=%async_computation | async-start | bytes 5898240 | tf_op jit(solution)/shard_map/all_to_all | solution.py:112
  23.3 0.5 copy-start.17
  25.7 1.0 copy-start.3
  25.7 1.6 copy-start.4
  25.7 2.3 %copy-start.5 = (f32[40]{0:T(128)S(1)}, f32[40]{0:T(128)}, u32[]{:S(2)}) copy-start(f32[40]{0:T(128)} %param.19) | copy-start | bytes 484
  28.7 3.3 %copy-start.11 = (f32[10]{0:T(128)}, f32[10]{0:T(128)S(1)}, u32[]{:S(2)}) copy-start(f32[10]{0:T(128)S(1)} %get-tuple-element.62) | copy-start | bytes 124
  28.7 3.3 %copy-start.14 = (f32[10]{0:T(128)}, f32[10]{0:T(128)S(1)}, u32[]{:S(2)}) copy-start(f32[10]{0:T(128)S(1)} %get-tuple-element.61) | copy-start | bytes 124
  53.8 32.1 %collective-permute-start.3 = (bf16[128,12,128]{2,0,1:T(8,128)(2,1)}, bf16[128,12,128]{2,0,1:T(8,128)(2,1)S(1)}, u32[]{:S(2)}, u32[]{:S(2)}) collective-permute-start(bf16[128,12,128]{2,0,1:T(8,128)(2,1)} %get-tuple-element.30), channel_id=1, source_target_pairs={{256,0},{1,256},{257,1},{2,257},{258,2},{3,258},{259,3},{4,259},{2... | collective-permute-start | bytes 1179656 | tf_op jit(solution)/shard_map/ppermute | solution.py:19
  71.8 29.7 %collective-permute-start.2 = (bf16[128,12,128]{2,0,1:T(8,128)(2,1)}, bf16[128,12,128]{2,0,1:T(8,128)(2,1)}, u32[]{:S(2)}, u32[]{:S(2)}) collective-permute-start(bf16[128,12,128]{2,0,1:T(8,128)(2,1)} %get-tuple-element.31), channel_id=1, source_target_pairs={{0,256},{256,1},{1,257},{257,2},{2,258},{258,3},{3,259},{259,4},{4... | collective-permute-start | bytes 1179656 | tf_op jit(solution)/shard_map/ppermute | solution.py:18
  76.1 54.3 %all-to-all-start.1 = ((bf16[16,24,12,128]{3,1,2,0:T(8,128)(2,1)}), bf16[16,24,12,128]{3,1,2,0:T(8,128)(2,1)}, u32[]{:S(2)}, u32[]{:S(2)}) async-start(bf16[16,24,12,128]{3,1,2,0:T(8,128)(2,1)} %copy.142), calls=%async_computation.1 | async-start | bytes 2359296 | tf_op jit(solution)/shard_map/all_to_all | solution.py:116
  84.9 16.6 %copy-start.6 = (bf16[384,12,128]{2,0,1:T(8,128)(2,1)S(1)}, bf16[384,12,128]{2,0,1:T(8,128)(2,1)}, u32[]{:S(2)}) copy-start(bf16[384,12,128]{2,0,1:T(8,128)(2,1)} %get-tuple-element.26) | copy-start | bytes 3538948
  85.9 15.6 %copy-start.9 = (bf16[128,12,128]{2,0,1:T(8,128)(2,1)}, bf16[128,12,128]{2,0,1:T(8,128)(2,1)S(1)}, u32[]{:S(2)}) copy-start(bf16[128,12,128]{2,0,1:T(8,128)(2,1)S(1)} %collective-permute-done.3) | copy-start | bytes 1179652
  105.2 1.9 copy-start.13
  105.5 1.6 copy-start.10
  108.2 1.9 copy-start.16
  132.3 19.7 %collective-permute-start.1 = (bf16[128,8,128]{2,0,1:T(8,128)(2,1)S(1)}, bf16[128,8,128]{2,0,1:T(8,128)(2,1)S(1)}, u32[]{:S(2)}, u32[]{:S(2)}) collective-permute-start(bf16[128,8,128]{2,0,1:T(8,128)(2,1)S(1)} %get-tuple-element.43), channel_id=1, source_target_pairs={{4,0},{8,4},{12,8},{16,12},{20,16},{24,20},{28,24},{32,28},{36,32}... | collective-permute-start | bytes 786440 | tf_op jit(solution)/shard_map/ppermute | solution.py:19
  148.7 18.0 %collective-permute-start = (bf16[128,8,128]{2,0,1:T(8,128)(2,1)S(1)}, bf16[128,8,128]{2,0,1:T(8,128)(2,1)S(1)}, u32[]{:S(2)}, u32[]{:S(2)}) collective-permute-start(bf16[128,8,128]{2,0,1:T(8,128)(2,1)S(1)} %get-tuple-element.44), channel_id=1, source_target_pairs={{0,4},{4,8},{8,12},{12,16},{16,20},{20,24},{24,28},{28,32},{32,36}... | collective-permute-start | bytes 786440 | tf_op jit(solution)/shard_map/ppermute | solution.py:18
  167.2 0.7 copy-start.12
  168.6 1.2 copy-start.15
  171.9 17.9 %all-to-all-start.2 = ((bf16[16,24,4,128]{3,1,2,0:T(8,128)(2,1)}), bf16[16,24,4,128]{3,1,2,0:T(8,128)(2,1)}, u32[]{:S(2)}, u32[]{:S(2)}) async-start(bf16[16,24,4,128]{3,1,2,0:T(8,128)(2,1)} %copy.155), calls=%async_computation.2 | async-start | bytes 786432 | tf_op jit(solution)/shard_map/all_to_all | solution.py:158
  192.8 3.7 %copy-start.18 = (s32[40]{0:T(128)S(1)}, s32[40]{0:T(128)}, u32[]{:S(2)}) copy-start(s32[40]{0:T(128)} %copy-done.17) | copy-start | bytes 484
  192.8 23.2 %all-to-all-start.3 = ((bf16[384,1,10,128]{3,2,1,0:T(8,128)(2,1)}), bf16[384,1,10,128]{3,2,1,0:T(8,128)(2,1)S(1)}, u32[]{:S(2)}, u32[]{:S(2)}) async-start(bf16[384,1,10,128]{3,2,1,0:T(8,128)(2,1)} %copy.168), calls=%async_computation.3 | async-start | bytes 3145728 | tf_op jit(solution)/shard_map/all_to_all | solution.py:161
  216.4 2.0 copy-start.1

commit v4 on v3

--- a/solution.py
+++ b/solution.py
@@ -88,7 +88,6 @@
     frame_index = lax.axis_index("frame")
     quarter_index = lax.axis_index("quarter")
     spatial_slot = (frame_index * quarters + quarter_index) * halves + half_index
-    temporal_slot = (quarter_index * halves + half_index) * frames + frame_index
 
     ranked = jnp.argsort(1 - labels, stable=True).astype(jnp.int32)
     slots = jnp.concatenate(
@@ -113,13 +112,18 @@
     frame_rows = frame_rows.reshape(rows, 3 * per_group, width)
     line_part = frame_rows[:, : 3 * lines_per_group]
     space_part = frame_rows[:, 3 * lines_per_group :]
+    piece_of = [j // 2 if j % 2 == 0 else frames - 1 - j // 2 for j in range(frames)]
+    holder_of = [piece_of.index(k) for k in range(frames)]
+    pieces = line_part.reshape(frames, piece, 3 * lines_per_group, width)
     moved = lax.all_to_all(
-        line_part.reshape(frames, piece, 3 * lines_per_group, width),
+        jnp.stack([pieces[k] for k in piece_of]),
         "frame",
         split_axis=0,
         concat_axis=0,
         tiled=True,
     )
+    space_kv = space_part[:, spaces_per_group:]
+    moved, space_kv = lax.optimization_barrier((moved, space_kv))
     line_rows = jnp.transpose(moved, (1, 0, 2, 3)).reshape(rows, 3 * lines_per_group, width)
 
     def linear(half, frame, quarter):
@@ -129,10 +133,11 @@
         linear(k % halves, k // (halves * quarters), (k // halves) % quarters) for k in range(chunks)
     ]
     temporal_order = [
-        linear((k // frames) % halves, k % frames, k // (frames * halves)) for k in range(chunks)
+        linear((k // frames) % halves, holder_of[k % frames], k // (frames * halves))
+        for k in range(chunks)
     ]
     along = ("zh", "frame", "quarter")
-    space_ext = with_halo(space_part[:, spaces_per_group:], along, spatial_order)
+    space_ext = with_halo(space_kv, along, spatial_order)
     line_ext = with_halo(line_rows[:, lines_per_group:], along, temporal_order)
 
     group_heads = lax.dynamic_slice_in_dim(slots, group_index * per_group, per_group)
@@ -151,12 +156,14 @@
             part_rows[:, :n], ext[:, :n], ext[:, n:], allowed, logit_scale[heads], value_factor[heads]
         )
 
+    own_piece = jnp.asarray(piece_of, jnp.int32)[frame_index]
+    temporal_slot = (quarter_index * halves + half_index) * frames + own_piece
     line_out = run(line_rows, line_ext, lo, temporal_slot)
     space_out = run(space_part, space_ext, hi, spatial_slot)
 
     back = jnp.transpose(line_out.reshape(piece, frames, lines_per_group, width), (1, 0, 2, 3))
     returned = lax.all_to_all(back, "frame", split_axis=0, concat_axis=0, tiled=True)
-    returned = returned.reshape(rows, lines_per_group, width)
+    returned = jnp.stack([returned[j] for j in holder_of]).reshape(rows, lines_per_group, width)
     frame_outputs = jnp.concatenate([returned, space_out], axis=1)
     merged = lax.all_to_all(
         frame_outputs.reshape(rows, 1, per_group, width),

time: 220 us -> 224 us (1.018)
  starting transfers between devices: 60.1 us -> 68.5 us
  local copies, waits for them, and re-layouts: 46.4 us -> 49.4 us
  waiting for transfers between devices: 90.5 us -> 87.6 us
  other arithmetic: 14.9 us -> 12.1 us
    ppermute x2, waiting for transfers between devices: 30.4 us -> 0.01 us  [with_halo(): lower = lax.ppermute(cells[-width:], axes, pairs)]
    ppermute x2, waiting for transfers between devices: 1.1 us -> 22.7 us  [with_halo(): upper = lax.ppermute(cells[:width], axes, [(b, a) for a, b in pairs])]
    ppermute x2, starting transfers between devices: 34.4 us -> 15.3 us  [with_halo(): upper = lax.ppermute(cells[:width], axes, [(b, a) for a, b in pairs])]
    all_to_all x1, starting transfers between devices: 4.2 us -> 17.3 us  [shards(): lax.all_to_all(back, 'frame', split_axis=0, concat_axis=0, tiled=True)]
    all_to_all x1, starting transfers between devices: 8.79 us -> 16.4 us  [shards(): lax.all_to_all(jnp.stack([pieces[k] for k in piece_of]), 'frame', split_a...]
    ppermute x2, starting transfers between devices: 4.02 us -> 11 us  [with_halo(): lower = lax.ppermute(cells[-width:], axes, pairs)]
    all_to_all x1, waiting for transfers between devices: 14.8 us -> 19.5 us  [shards(): lax.all_to_all(stacked, 'x', split_axis=1, concat_axis=0, tiled=True)]
    unnamed x59 -> x78, local copies, waits for them, and re-layouts: 12.7 us -> 16.9 us
  transfers between devices with their start and end apart: 8 -> 8, of which waited for: 7 -> 5; matrix products, arithmetic and copies ran while one was open for 15% -> 13% of each run, Pallas kernels for 0% -> 0%
where the time goes in v4:
time: 224 us; the launch traced here: 223 us
  waiting for transfers between devices  87.6 us (39%)
  starting transfers between devices  68.5 us (31%)
  local copies, waits for them, and re-layouts  49.4 us (22%)
  other arithmetic  12.1 us (5%)
  matrix products  3.92 us (2%)
    ppermute x2, waiting for transfers between devices, with_halo(): upper = lax.ppermute(cells[:width], axes, [(b, a) for a, b in pairs])  22.7 us
    all_to_all x1, waiting for transfers between devices, shards(): lax.all_to_all(jnp.stack([pieces[k] for k in piece_of]), 'frame', split_a...  20.6 us
    all_to_all x1, waiting for transfers between devices, shards(): lax.all_to_all(stacked, 'x', split_axis=1, concat_axis=0, tiled=True)  19.5 us
    all_to_all x1, waiting for transfers between devices, shards(): lax.all_to_all(frame_outputs.reshape(rows, 1, per_group, width), 'x', spl...  19.2 us
    all_to_all x1, starting transfers between devices, shards(): lax.all_to_all(back, 'frame', split_axis=0, concat_axis=0, tiled=True)  17.3 us
    unnamed x78, local copies, waits for them, and re-layouts  16.9 us
    all_to_all x1, starting transfers between devices, shards(): lax.all_to_all(jnp.stack([pieces[k] for k in piece_of]), 'frame', split_a...  16.4 us
    ppermute x2, starting transfers between devices, with_halo(): upper = lax.ppermute(cells[:width], axes, [(b, a) for a, b in pairs])  15.3 us
  transfers between devices with their start and end apart: 8, of which 5 were waited for; matrix products, arithmetic and copies ran while one was open for 13% of the time, Pallas kernels for 0%

profile of v4, /device:TPU:1, one launch (start us, length us, event | category | flops | bytes accessed | tf_op | source)
XLA Modules:
  0.0 223.1 jit_solution(7620989342147354865)
XLA Ops:
  0.0 0.8 broadcast_subtract_fusion
  0.8 2.0 sort.34
  3.7 0.7 gather_fusion.10
  4.4 0.7 gather_fusion.9
  5.1 1.4 copy_bitcast_fusion.3
  6.5 1.7 gather_fusion.8
  8.2 1.5 broadcast_select_fusion
  9.7 0.8 slice_dynamic-update-slice_fusion.5
  10.6 0.8 slice_dynamic-update-slice_fusion.4
  11.4 0.8 slice_dynamic-update-slice_fusion.3
  12.2 0.9 slice_dynamic-update-slice_fusion.2
  13.2 0.9 slice_dynamic-update-slice_fusion.1
  14.1 0.9 slice_dynamic-update-slice_fusion
  15.0 5.0 %all-to-all-start = ((bf16[96,4,30,128]{3,0,2,1:T(8,128)(2,1)}), bf16[96,4,30,128]{3,0,2,1:T(8,128)(2,1)}, u32[]{:S(2)}, u32[]{:S(2)}) async-start(bf16[96,4,30,128]{3,0,2,1:T(8,128)(2,1)} %slice_dynamic-update-slice_fusion), calls=%async_computation | async-start | bytes 5898240 | tf_op jit(solution)/shard_map/all_to_all | solution.py:111
  20.1 2.0 sort.35
  28.0 0.9 gather_fusion.6
  29.2 1.0 gather_fusion.7
  30.2 19.5 %all-to-all-done = bf16[96,4,30,128]{3,0,2,1:T(8,128)(2,1)} async-done(((bf16[96,4,30,128]{3,0,2,1:T(8,128)(2,1)}), bf16[96,4,30,128]{3,0,2,1:T(8,128)(2,1)}, u32[]{:S(2)}, u32[]{:S(2)}) %all-to-all-start) | async-done | bytes 2949152 | tf_op jit(solution)/shard_map/all_to_all | solution.py:111
  49.7 2.2 copy.195
  52.6 1.0 constant_dynamic-update-slice_fusion.14
  62.5 16.4 %all-to-all-start.1 = ((bf16[16,24,12,128]{3,1,2,0:T(8,128)(2,1)}), bf16[16,24,12,128]{3,1,2,0:T(8,128)(2,1)S(1)}, u32[]{:S(2)}, u32[]{:S(2)}) async-start(bf16[16,24,12,128]{3,1,2,0:T(8,128)(2,1)} %constant_dynamic-update-slice_fusion), calls=%async_computation.1 | async-start | bytes 2359296 | tf_op jit(solution)/shard_map/all_to_all | solution.py:118
  80.5 1.7 copy.202
  82.2 1.4 gather_fusion.4
  83.8 0.9 gather_fusion.5
  85.0 1.9 slice.544
  86.9 1.3 slice.506
  88.3 20.6 %all-to-all-done.1 = bf16[16,24,12,128]{3,1,2,0:T(8,128)(2,1)S(1)} async-done(((bf16[16,24,12,128]{3,1,2,0:T(8,128)(2,1)}), bf16[16,24,12,128]{3,1,2,0:T(8,128)(2,1)S(1)}, u32[]{:S(2)}, u32[]{:S(2)}) %all-to-all-start.1) | async-done | bytes 1179680 | tf_op jit(solution)/shard_map/all_to_all | solution.py:118
  108.9 1.0 fusion.58
  109.8 1.1 fusion.57
  111.5 9.0 %collective-permute-start.2 = (bf16[128,12,128]{2,0,1:T(8,128)(2,1)}, bf16[128,12,128]{2,0,1:T(8,128)(2,1)S(1)}, u32[]{:S(2)}, u32[]{:S(2)}) collective-permute-start(bf16[128,12,128]{2,0,1:T(8,128)(2,1)} %get-tuple-element.45), channel_id=1, source_target_pairs={{0,256},{256,1},{1,257},{257,2},{2,258},{258,3},{3,259},{259,4},{4... | collective-permute-start | bytes 1179656 | tf_op jit(solution)/shard_map/ppermute | solution.py:18
  120.6 8.3 %collective-permute-start.3 = (bf16[128,12,128]{2,0,1:T(8,128)(2,1)}, bf16[128,12,128]{2,0,1:T(8,128)(2,1)S(1)}, u32[]{:S(2)}, u32[]{:S(2)}) collective-permute-start(bf16[128,12,128]{2,0,1:T(8,128)(2,1)} %get-tuple-element.44), channel_id=1, source_target_pairs={{256,0},{1,256},{257,1},{2,257},{258,2},{3,258},{259,3},{4,259},{2... | collective-permute-start | bytes 1179656 | tf_op jit(solution)/shard_map/ppermute | solution.py:19
  128.9 7.0 %collective-permute-start.1 = (bf16[128,8,128]{2,0,1:T(8,128)(2,1)S(1)}, bf16[128,8,128]{2,0,1:T(8,128)(2,1)S(1)}, u32[]{:S(2)}, u32[]{:S(2)}) collective-permute-start(bf16[128,8,128]{2,0,1:T(8,128)(2,1)S(1)} %get-tuple-element.40), channel_id=1, source_target_pairs={{8,0},{16,8},{24,16},{32,24},{40,32},{48,40},{56,48},{60,56},{52,6... | collective-permute-start | bytes 786440 | tf_op jit(solution)/shard_map/ppermute | solution.py:19
  135.9 1.9 collective-permute-start
  137.9 22.7 %collective-permute-done.1 = bf16[128,8,128]{2,0,1:T(8,128)(2,1)S(1)} collective-permute-done((bf16[128,8,128]{2,0,1:T(8,128)(2,1)S(1)}, bf16[128,8,128]{2,0,1:T(8,128)(2,1)S(1)}, u32[]{:S(2)}, u32[]{:S(2)}) %collective-permute-start.1) | collective-permute-done | bytes 262176 | tf_op jit(solution)/shard_map/ppermute | solution.py:19
  161.4 0.7 fusion.3
  162.1 1.2 fusion.4
  163.6 0.8 fusion.37
  164.5 0.9 copy.208
  165.3 17.3 %all-to-all-start.2 = ((bf16[16,24,4,128]{3,1,2,0:T(8,128)(2,1)}), bf16[16,24,4,128]{3,1,2,0:T(8,128)(2,1)S(1)}, u32[]{:S(2)}, u32[]{:S(2)}) async-start(bf16[16,24,4,128]{3,1,2,0:T(8,128)(2,1)} %copy.208), calls=%async_computation.2 | async-start | bytes 786432 | tf_op jit(solution)/shard_map/all_to_all | solution.py:165
  184.1 0.9 copy-done.9
  185.3 1.2 fusion
  186.5 1.9 fusion.1
  188.9 1.2 fusion.22
  190.1 5.7 %all-to-all-done.2 = bf16[16,24,4,128]{3,1,2,0:T(8,128)(2,1)S(1)} async-done(((bf16[16,24,4,128]{3,1,2,0:T(8,128)(2,1)}), bf16[16,24,4,128]{3,1,2,0:T(8,128)(2,1)S(1)}, u32[]{:S(2)}, u32[]{:S(2)}) %all-to-all-start.2) | async-done | bytes 393248 | tf_op jit(solution)/shard_map/all_to_all | solution.py:165
  196.1 1.9 copy.235
  198.0 3.6 %all-to-all-start.3 = ((bf16[384,1,10,128]{3,2,1,0:T(8,128)(2,1)}), bf16[384,1,10,128]{3,2,1,0:T(8,128)(2,1)S(1)}, u32[]{:S(2)}, u32[]{:S(2)}) async-start(bf16[384,1,10,128]{3,2,1,0:T(8,128)(2,1)} %copy.235), calls=%async_computation.3 | async-start | bytes 3145728 | tf_op jit(solution)/shard_map/all_to_all | solution.py:168
  201.6 19.2 %all-to-all-done.3 = bf16[384,1,10,128]{3,2,1,0:T(8,128)(2,1)S(1)} async-done(((bf16[384,1,10,128]{3,2,1,0:T(8,128)(2,1)}), bf16[384,1,10,128]{3,2,1,0:T(8,128)(2,1)S(1)}, u32[]{:S(2)}, u32[]{:S(2)}) %all-to-all-start.3) | async-done | bytes 983072 | tf_op jit(solution)/shard_map/all_to_all | solution.py:168
  221.9 1.2 copy_bitcast_fusion
  (159 shorter events, 23.2 us)
Async XLA Ops:
  0.0 3.3 %copy-start = (bf16[96,5120]{1,0:T(8,128)(2,1)S(1)}, bf16[96,5120]{1,0:T(8,128)(2,1)}, u32[]{:S(2)}) copy-start(bf16[96,5120]{1,0:T(8,128)(2,1)} %param.16) | copy-start | bytes 2949124
  0.0 3.5 %copy-start.10 = (bf16[96,5120]{1,0:T(8,128)(2,1)S(1)}, bf16[96,5120]{1,0:T(8,128)(2,1)}, u32[]{:S(2)}) copy-start(bf16[96,5120]{1,0:T(8,128)(2,1)} %param.15) | copy-start | bytes 2949124
  15.0 7.2 %copy-start.2 = (s32[40,768,5]{1,0,2:T(8,128)S(1)}, s32[40,768,5]{1,0,2:T(8,128)}, u32[]{:S(2)}) copy-start(s32[40,768,5]{1,0,2:T(8,128)} %param.18) | copy-start | bytes 1843204
  15.0 34.7 %all-to-all-start = ((bf16[96,4,30,128]{3,0,2,1:T(8,128)(2,1)}), bf16[96,4,30,128]{3,0,2,1:T(8,128)(2,1)}, u32[]{:S(2)}, u32[]{:S(2)}) async-start(bf16[96,4,30,128]{3,0,2,1:T(8,128)(2,1)} %slice_dynamic-update-slice_fusion), calls=%async_computation | async-start | bytes 5898240 | tf_op jit(solution)/shard_map/all_to_all | solution.py:111
  22.2 0.9 copy-start.11
  23.7 1.3 copy-start.3
  23.7 2.0 copy-start.4
  23.8 2.6 %copy-start.5 = (f32[40]{0:T(128)S(1)}, f32[40]{0:T(128)}, u32[]{:S(2)}) copy-start(f32[40]{0:T(128)} %param.20) | copy-start | bytes 484
  51.9 9.9 %copy-start.6 = (bf16[4,96,1,30,128]{4,1,0,3,2:T(8,128)(2,1)}, bf16[4,96,1,30,128]{4,1,0,3,2:T(8,128)(2,1)S(1)}, u32[]{:S(2)}) copy-start(bf16[4,96,1,30,128]{4,1,0,3,2:T(8,128)(2,1)S(1)} %copy.195) | copy-start | bytes 8847364
  56.1 23.0 %copy-start.12 = (s32[16]{0:T(128)S(1)}, s32[16]{0:T(128)}, u32[]{:S(2)}) copy-start(s32[16]{0:T(128)} %constant.167.clone) | copy-start | bytes 196
  62.5 46.4 %all-to-all-start.1 = ((bf16[16,24,12,128]{3,1,2,0:T(8,128)(2,1)}), bf16[16,24,12,128]{3,1,2,0:T(8,128)(2,1)S(1)}, u32[]{:S(2)}, u32[]{:S(2)}) async-start(bf16[16,24,12,128]{3,1,2,0:T(8,128)(2,1)} %constant_dynamic-update-slice_fusion), calls=%async_computation.1 | async-start | bytes 2359296 | tf_op jit(solution)/shard_map/all_to_all | solution.py:118
  111.5 71.1 %collective-permute-start.2 = (bf16[128,12,128]{2,0,1:T(8,128)(2,1)}, bf16[128,12,128]{2,0,1:T(8,128)(2,1)S(1)}, u32[]{:S(2)}, u32[]{:S(2)}) collective-permute-start(bf16[128,12,128]{2,0,1:T(8,128)(2,1)} %get-tuple-element.45), channel_id=1, source_target_pairs={{0,256},{256,1},{1,257},{257,2},{2,258},{258,3},{3,259},{259,4},{4... | collective-permute-start | bytes 1179656 | tf_op jit(solution)/shard_map/ppermute | solution.py:18
  120.6 63.0 %collective-permute-start.3 = (bf16[128,12,128]{2,0,1:T(8,128)(2,1)}, bf16[128,12,128]{2,0,1:T(8,128)(2,1)S(1)}, u32[]{:S(2)}, u32[]{:S(2)}) collective-permute-start(bf16[128,12,128]{2,0,1:T(8,128)(2,1)} %get-tuple-element.44), channel_id=1, source_target_pairs={{256,0},{1,256},{257,1},{2,257},{258,2},{3,258},{259,3},{4,259},{2... | collective-permute-start | bytes 1179656 | tf_op jit(solution)/shard_map/ppermute | solution.py:19
  128.9 31.7 %collective-permute-start.1 = (bf16[128,8,128]{2,0,1:T(8,128)(2,1)S(1)}, bf16[128,8,128]{2,0,1:T(8,128)(2,1)S(1)}, u32[]{:S(2)}, u32[]{:S(2)}) collective-permute-start(bf16[128,8,128]{2,0,1:T(8,128)(2,1)S(1)} %get-tuple-element.40), channel_id=1, source_target_pairs={{8,0},{16,8},{24,16},{32,24},{40,32},{48,40},{56,48},{60,56},{52,6... | collective-permute-start | bytes 786440 | tf_op jit(solution)/shard_map/ppermute | solution.py:19
  135.9 24.7 %collective-permute-start = (bf16[128,8,128]{2,0,1:T(8,128)(2,1)S(1)}, bf16[128,8,128]{2,0,1:T(8,128)(2,1)S(1)}, u32[]{:S(2)}, u32[]{:S(2)}) collective-permute-start(bf16[128,8,128]{2,0,1:T(8,128)(2,1)S(1)} %get-tuple-element.41), channel_id=1, source_target_pairs={{0,8},{8,16},{16,24},{24,32},{32,40},{40,48},{48,56},{56,60},{60,5... | collective-permute-start | bytes 786440 | tf_op jit(solution)/shard_map/ppermute | solution.py:18
  165.3 30.4 %all-to-all-start.2 = ((bf16[16,24,4,128]{3,1,2,0:T(8,128)(2,1)}), bf16[16,24,4,128]{3,1,2,0:T(8,128)(2,1)S(1)}, u32[]{:S(2)}, u32[]{:S(2)}) async-start(bf16[16,24,4,128]{3,1,2,0:T(8,128)(2,1)} %copy.208), calls=%async_computation.2 | async-start | bytes 786432 | tf_op jit(solution)/shard_map/all_to_all | solution.py:165
  184.0 1.1 copy-start.9
  184.1 1.2 copy-start.7
  186.5 2.1 copy-start.8
  198.0 22.8 %all-to-all-start.3 = ((bf16[384,1,10,128]{3,2,1,0:T(8,128)(2,1)}), bf16[384,1,10,128]{3,2,1,0:T(8,128)(2,1)S(1)}, u32[]{:S(2)}, u32[]{:S(2)}) async-start(bf16[384,1,10,128]{3,2,1,0:T(8,128)(2,1)} %copy.235), calls=%async_computation.3 | async-start | bytes 3145728 | tf_op jit(solution)/shard_map/all_to_all | solution.py:168
  221.1 2.0 copy-start.1

commit v5 on v3

--- a/solution.py
+++ b/solution.py
@@ -90,15 +90,17 @@
     spatial_slot = (frame_index * quarters + quarter_index) * halves + half_index
     temporal_slot = (quarter_index * halves + half_index) * frames + frame_index
 
-    ranked = jnp.argsort(1 - labels, stable=True).astype(jnp.int32)
-    slots = jnp.concatenate(
-        [
-            ranked[:TEMPORAL].reshape(groups, lines_per_group),
-            ranked[TEMPORAL:].reshape(groups, spaces_per_group),
-        ],
-        axis=1,
-    ).reshape(head_count)
-    unslots = jnp.argsort(slots).astype(jnp.int32)
+    heads = jnp.arange(head_count, dtype=jnp.int32)
+    earlier = heads[None, :] < heads[:, None]
+    is_line = labels == 1
+    line_rank = jnp.sum(jnp.where(earlier, is_line[None, :], False), axis=1, dtype=jnp.int32)
+    space_rank = heads - line_rank
+    unslots = jnp.where(
+        is_line,
+        (line_rank // lines_per_group) * per_group + line_rank % lines_per_group,
+        (space_rank // spaces_per_group) * per_group + lines_per_group + space_rank % spaces_per_group,
+    )
+    slots = jnp.sum(jnp.where(unslots[None, :] == heads[:, None], heads[None, :], 0), axis=1)
 
     def grouped(array):
         picked = jnp.take(array.reshape(tokens_here, head_count, width), slots, axis=1)
@@ -120,6 +122,8 @@
         concat_axis=0,
         tiled=True,
     )
+    space_kv = space_part[:, spaces_per_group:]
+    moved, space_kv = lax.optimization_barrier((moved, space_kv))
     line_rows = jnp.transpose(moved, (1, 0, 2, 3)).reshape(rows, 3 * lines_per_group, width)
 
     def linear(half, frame, quarter):
@@ -132,7 +136,7 @@
         linear((k // frames) % halves, k % frames, k // (frames * halves)) for k in range(chunks)
     ]
     along = ("zh", "frame", "quarter")
-    space_ext = with_halo(space_part[:, spaces_per_group:], along, spatial_order)
+    space_ext = with_halo(space_kv, along, spatial_order)
     line_ext = with_halo(line_rows[:, lines_per_group:], along, temporal_order)
 
     group_heads = lax.dynamic_slice_in_dim(slots, group_index * per_group, per_group)
@@ -152,9 +156,10 @@
         )
 
     line_out = run(line_rows, line_ext, lo, temporal_slot)
+    back = jnp.transpose(line_out.reshape(piece, frames, lines_per_group, width), (1, 0, 2, 3))
+    back, space_ext = lax.optimization_barrier((back, space_ext))
     space_out = run(space_part, space_ext, hi, spatial_slot)
 
-    back = jnp.transpose(line_out.reshape(piece, frames, lines_per_group, width), (1, 0, 2, 3))
     returned = lax.all_to_all(back, "frame", split_axis=0, concat_axis=0, tiled=True)
     returned = returned.reshape(rows, lines_per_group, width)
     frame_outputs = jnp.concatenate([returned, space_out], axis=1)

time: 220 us -> 216 us (0.982); the launches traced: 218 us -> 212 us
  blocking collectives: 0 us -> 20 us
  waiting for transfers between devices: 90.5 us -> 79.8 us
  local copies, waits for them, and re-layouts: 46.4 us -> 36.9 us
  other arithmetic: 14.9 us -> 8.96 us
    all_to_all x0 -> x1, blocking collectives: none -> 20 us  [shards(): lax.all_to_all(frame_outputs.reshape(rows, 1, per_group, width), 'x', spl...]
    all_to_all x1 -> x0, waiting for transfers between devices: 19.5 us -> none  [shards(): lax.all_to_all(frame_outputs.reshape(rows, 1, per_group, width), 'x', spl...]
    ppermute x2, starting transfers between devices: 34.4 us -> 21.8 us  [with_halo(): upper = lax.ppermute(cells[:width], axes, [(b, a) for a, b in pairs])]
    all_to_all x1, starting transfers between devices: 4.2 us -> 14.7 us  [shards(): lax.all_to_all(back, 'frame', split_axis=0, concat_axis=0, tiled=True)]
    all_to_all x1, starting transfers between devices: 8.79 us -> 16.5 us  [shards(): lax.all_to_all(line_part.reshape(frames, piece, 3 * lines_per_group, widt...]
    all_to_all x1, waiting for transfers between devices: 14.8 us -> 20.8 us  [shards(): lax.all_to_all(stacked, 'x', split_axis=1, concat_axis=0, tiled=True)]
    unnamed x59 -> x43, local copies, waits for them, and re-layouts: 12.7 us -> 7.71 us
    sort x2 -> x0, other arithmetic: 4.08 us -> none  [the longest x1 2.04 us: shards(): ranked = jnp.argsort(1 - labels, stable=True).astype(jnp.int32)]
  transfers between devices with their start and end apart: 8 -> 7, of which waited for: 7 -> 5; matrix products, arithmetic and copies ran while one was open for 15% -> 12% of each run, Pallas kernels for 0% -> 0%
where the time goes in v5:
time: 216 us; the launch traced here: 212 us
  waiting for transfers between devices  79.8 us (37%)
  starting transfers between devices  61.8 us (29%)
  local copies, waits for them, and re-layouts  36.9 us (17%)
  blocking collectives  20 us (9%)
  other arithmetic  8.96 us (4%)
  matrix products  3.91 us (2%)
    ppermute x2, waiting for transfers between devices, with_halo(): lower = lax.ppermute(cells[-width:], axes, pairs)  29.5 us
    all_to_all x1, waiting for transfers between devices, shards(): lax.all_to_all(line_part.reshape(frames, piece, 3 * lines_per_group, widt...  23.5 us
    ppermute x2, starting transfers between devices, with_halo(): upper = lax.ppermute(cells[:width], axes, [(b, a) for a, b in pairs])  21.8 us
    all_to_all x1, waiting for transfers between devices, shards(): lax.all_to_all(stacked, 'x', split_axis=1, concat_axis=0, tiled=True)  20.8 us
    all_to_all x1, blocking collectives, shards(): lax.all_to_all(frame_outputs.reshape(rows, 1, per_group, width), 'x', spl...  20 us
    all_to_all x1, starting transfers between devices, shards(): lax.all_to_all(line_part.reshape(frames, piece, 3 * lines_per_group, widt...  16.5 us
    all_to_all x1, starting transfers between devices, shards(): lax.all_to_all(back, 'frame', split_axis=0, concat_axis=0, tiled=True)  14.7 us
    unnamed x43, local copies, waits for them, and re-layouts  7.71 us
  transfers between devices with their start and end apart: 7, of which 5 were waited for; matrix products, arithmetic and copies ran while one was open for 12% of the time, Pallas kernels for 0%

profile of v5, /device:TPU:1, one launch (start us, length us, event | category | flops | bytes accessed | tf_op | source)
XLA Modules:
  0.0 212.1 jit_solution(17367236024218428362)
XLA Ops:
  0.0 0.7 broadcast_compare_fusion.2
  0.9 0.7 compare_and_fusion
  1.9 1.4 copy_bitcast_fusion.2
  3.3 0.7 gather_fusion.8
  4.0 0.7 gather_fusion.9
  4.7 1.4 copy_bitcast_fusion.1
  6.1 1.7 gather_fusion.10
  7.8 1.5 broadcast_select_fusion
  9.3 0.9 slice_dynamic-update-slice_fusion.5
  10.2 0.8 slice_dynamic-update-slice_fusion.4
  11.0 0.9 slice_dynamic-update-slice_fusion.3
  11.9 0.9 slice_dynamic-update-slice_fusion.2
  12.8 1.0 slice_dynamic-update-slice_fusion.1
  13.8 0.9 slice_dynamic-update-slice_fusion
  14.7 5.0 %all-to-all-start = ((bf16[96,4,30,128]{3,0,2,1:T(8,128)(2,1)}), bf16[96,4,30,128]{3,0,2,1:T(8,128)(2,1)}, u32[]{:S(2)}, u32[]{:S(2)}) async-start(bf16[96,4,30,128]{3,0,2,1:T(8,128)(2,1)} %slice_dynamic-update-slice_fusion), calls=%async_computation | async-start | bytes 5898240 | tf_op jit(solution)/shard_map/all_to_all | solution.py:114
  21.0 0.7 gather_fusion
  21.8 0.7 gather_fusion.2
  25.0 0.9 gather_fusion.5
  26.0 1.0 gather_fusion.7
  27.6 0.7 gather_fusion.4
  28.5 20.8 %all-to-all-done = bf16[96,4,30,128]{3,0,2,1:T(8,128)(2,1)} async-done(((bf16[96,4,30,128]{3,0,2,1:T(8,128)(2,1)}), bf16[96,4,30,128]{3,0,2,1:T(8,128)(2,1)}, u32[]{:S(2)}, u32[]{:S(2)}) %all-to-all-start) | async-done | bytes 2949152 | tf_op jit(solution)/shard_map/all_to_all | solution.py:114
  49.3 2.2 %copy.141 = bf16[4,96,1,30,128]{4,1,0,3,2:T(8,128)(2,1)S(1)} copy(bf16[4,96,1,30,128]{4,1,3,0,2:T(8,128)(2,1)} %bitcast.10) | data formatting | bytes 5898240 | tf_op jit(solution)/shard_map/all_to_all | solution.py:114
  51.6 1.6 copy-done.6
  53.3 1.4 copy.142
  54.7 16.5 %all-to-all-start.1 = ((bf16[16,24,12,128]{3,1,2,0:T(8,128)(2,1)}), bf16[16,24,12,128]{3,1,2,0:T(8,128)(2,1)S(1)}, u32[]{:S(2)}, u32[]{:S(2)}) async-start(bf16[16,24,12,128]{3,1,2,0:T(8,128)(2,1)} %copy.142), calls=%async_computation.1 | async-start | bytes 2359296 | tf_op jit(solution)/shard_map/all_to_all | solution.py:118
  71.5 2.2 %copy.162 = s32[6,768,5]{2,1,0:T(8,128)} copy(s32[6,768,5]{1,0,2:T(8,128)S(1)} %broadcast_select_fusion.3) | data formatting | bytes 184320 | tf_op jit(solution)/shard_map/jit(_take)/select_n | solution.py:26
  73.6 1.7 gather_fusion.6
  75.7 1.9 slice.281
  77.6 23.5 %all-to-all-done.1 = bf16[16,24,12,128]{3,1,2,0:T(8,128)(2,1)S(1)} async-done(((bf16[16,24,12,128]{3,1,2,0:T(8,128)(2,1)}), bf16[16,24,12,128]{3,1,2,0:T(8,128)(2,1)S(1)}, u32[]{:S(2)}, u32[]{:S(2)}) %all-to-all-start.1) | async-done | bytes 1179680 | tf_op jit(solution)/shard_map/all_to_all | solution.py:118
  101.7 14.3 %collective-permute-start.1 = (bf16[128,8,128]{2,0,1:T(8,128)(2,1)S(1)}, bf16[128,8,128]{2,0,1:T(8,128)(2,1)S(1)}, u32[]{:S(2)}, u32[]{:S(2)}) collective-permute-start(bf16[128,8,128]{2,0,1:T(8,128)(2,1)S(1)} %get-tuple-element.48), channel_id=1, source_target_pairs={{4,0},{8,4},{12,8},{16,12},{20,16},{24,20},{28,24},{32,28},{36,32}... | collective-permute-start | bytes 786440 | tf_op jit(solution)/shard_map/ppermute | solution.py:19
  116.0 1.9 collective-permute-start
  118.0 1.9 collective-permute-start.2
  119.9 7.5 %collective-permute-start.3 = (bf16[128,12,128]{2,0,1:T(8,128)(2,1)S(1)}, bf16[128,12,128]{2,0,1:T(8,128)(2,1)S(1)}, u32[]{:S(2)}, u32[]{:S(2)}) collective-permute-start(bf16[128,12,128]{2,0,1:T(8,128)(2,1)S(1)} %get-tuple-element.44), channel_id=1, source_target_pairs={{256,0},{1,256},{257,1},{2,257},{258,2},{3,258},{259,3},{4,259},{2... | collective-permute-start | bytes 1179656 | tf_op jit(solution)/shard_map/ppermute | solution.py:19
  127.6 4.6 %collective-permute-done = bf16[128,8,128]{2,0,1:T(8,128)(2,1)S(1)} collective-permute-done((bf16[128,8,128]{2,0,1:T(8,128)(2,1)S(1)}, bf16[128,8,128]{2,0,1:T(8,128)(2,1)S(1)}, u32[]{:S(2)}, u32[]{:S(2)}) %collective-permute-start) | collective-permute-done | bytes 262176 | tf_op jit(solution)/shard_map/ppermute | solution.py:18
  133.0 0.7 fusion.3
  133.8 1.2 fusion.4
  135.3 0.8 fusion.37
  136.2 24.9 %collective-permute-done.2 = bf16[128,12,128]{2,0,1:T(8,128)(2,1)S(1)} collective-permute-done((bf16[128,12,128]{2,0,1:T(8,128)(2,1)S(1)}, bf16[128,12,128]{2,0,1:T(8,128)(2,1)S(1)}, u32[]{:S(2)}, u32[]{:S(2)}) %collective-permute-start.2) | collective-permute-done | bytes 393248 | tf_op jit(solution)/shard_map/ppermute | solution.py:18
  161.2 0.8 copy.155
  162.1 14.7 %all-to-all-start.2 = ((bf16[16,24,4,128]{3,1,2,0:T(8,128)(2,1)}), bf16[16,24,4,128]{3,1,2,0:T(8,128)(2,1)S(1)}, u32[]{:S(2)}, u32[]{:S(2)}) async-start(bf16[16,24,4,128]{3,1,2,0:T(8,128)(2,1)} %copy.155), calls=%async_computation.2 | async-start | bytes 786432 | tf_op jit(solution)/shard_map/all_to_all | solution.py:163
  178.2 1.2 fusion
  179.4 1.9 fusion.1
  181.7 1.2 fusion.22
  183.0 5.9 %all-to-all-done.2 = bf16[16,24,4,128]{3,1,2,0:T(8,128)(2,1)S(1)} async-done(((bf16[16,24,4,128]{3,1,2,0:T(8,128)(2,1)}), bf16[16,24,4,128]{3,1,2,0:T(8,128)(2,1)S(1)}, u32[]{:S(2)}, u32[]{:S(2)}) %all-to-all-start.2) | async-done | bytes 393248 | tf_op jit(solution)/shard_map/all_to_all | solution.py:163
  189.0 0.7 copy.168
  189.8 20.0 %all_to_all.40 = bf16[384,1,10,128]{3,2,1,0:T(8,128)(2,1)S(1)} all-to-all(bf16[384,1,10,128]{3,2,1,0:T(8,128)(2,1)S(1)} %copy.168), channel_id=1, replica_groups=mesh['zh'=2,'x'=4,'frame'=16,'quarter'=4] {'x'}, dimensions={0} | all-to-all | bytes 1966080 | tf_op jit(solution)/shard_map/all_to_all | solution.py:166
  210.1 0.7 gather_fusion.14
  210.9 1.2 copy_bitcast_fusion
  (113 shorter events, 10.2 us)
Async XLA Ops:
  0.0 1.7 copy-start
  14.7 5.1 %copy-start.10 = (s32[40,768]{1,0:T(8,128)S(1)}, s32[40,768]{1,0:T(8,128)}, u32[]{:S(2)}) copy-start(s32[40,768]{1,0:T(8,128)} %param.18) | copy-start | bytes 368644
  14.7 6.3 %copy-start.2 = (s32[40,768,5]{1,0,2:T(8,128)S(1)}, s32[40,768,5]{1,0,2:T(8,128)}, u32[]{:S(2)}) copy-start(s32[40,768,5]{1,0,2:T(8,128)} %param.17) | copy-start | bytes 1843204
  14.7 34.6 %all-to-all-start = ((bf16[96,4,30,128]{3,0,2,1:T(8,128)(2,1)}), bf16[96,4,30,128]{3,0,2,1:T(8,128)(2,1)}, u32[]{:S(2)}, u32[]{:S(2)}) async-start(bf16[96,4,30,128]{3,0,2,1:T(8,128)(2,1)} %slice_dynamic-update-slice_fusion), calls=%async_computation | async-start | bytes 5898240 | tf_op jit(solution)/shard_map/all_to_all | solution.py:114
  21.7 1.0 copy-start.3
  21.7 1.7 copy-start.4
  21.8 2.3 %copy-start.5 = (f32[40]{0:T(128)S(1)}, f32[40]{0:T(128)}, u32[]{:S(2)}) copy-start(f32[40]{0:T(128)} %param.19) | copy-start | bytes 484
  51.5 1.6 copy-start.6
  53.3 64.6 %copy-start.7 = (bf16[384,12,128]{2,0,1:T(8,128)(2,1)}, bf16[384,12,128]{2,0,1:T(8,128)(2,1)S(1)}, u32[]{:S(2)}) copy-start(bf16[384,12,128]{2,0,1:T(8,128)(2,1)S(1)} %get-tuple-element.12) | copy-start | bytes 3538948
  54.7 46.5 %all-to-all-start.1 = ((bf16[16,24,12,128]{3,1,2,0:T(8,128)(2,1)}), bf16[16,24,12,128]{3,1,2,0:T(8,128)(2,1)S(1)}, u32[]{:S(2)}, u32[]{:S(2)}) async-start(bf16[16,24,12,128]{3,1,2,0:T(8,128)(2,1)} %copy.142), calls=%async_computation.1 | async-start | bytes 2359296 | tf_op jit(solution)/shard_map/all_to_all | solution.py:118
  101.7 25.9 %collective-permute-start.1 = (bf16[128,8,128]{2,0,1:T(8,128)(2,1)S(1)}, bf16[128,8,128]{2,0,1:T(8,128)(2,1)S(1)}, u32[]{:S(2)}, u32[]{:S(2)}) collective-permute-start(bf16[128,8,128]{2,0,1:T(8,128)(2,1)S(1)} %get-tuple-element.48), channel_id=1, source_target_pairs={{4,0},{8,4},{12,8},{16,12},{20,16},{24,20},{28,24},{32,28},{36,32}... | collective-permute-start | bytes 786440 | tf_op jit(solution)/shard_map/ppermute | solution.py:19
  116.0 16.2 %collective-permute-start = (bf16[128,8,128]{2,0,1:T(8,128)(2,1)S(1)}, bf16[128,8,128]{2,0,1:T(8,128)(2,1)S(1)}, u32[]{:S(2)}, u32[]{:S(2)}) collective-permute-start(bf16[128,8,128]{2,0,1:T(8,128)(2,1)S(1)} %get-tuple-element.49), channel_id=1, source_target_pairs={{0,4},{4,8},{8,12},{12,16},{16,20},{20,24},{24,28},{28,32},{32,36}... | collective-permute-start | bytes 786440 | tf_op jit(solution)/shard_map/ppermute | solution.py:18
  118.0 43.1 %collective-permute-start.2 = (bf16[128,12,128]{2,0,1:T(8,128)(2,1)S(1)}, bf16[128,12,128]{2,0,1:T(8,128)(2,1)S(1)}, u32[]{:S(2)}, u32[]{:S(2)}) collective-permute-start(bf16[128,12,128]{2,0,1:T(8,128)(2,1)S(1)} %get-tuple-element.43), channel_id=1, source_target_pairs={{0,256},{256,1},{1,257},{257,2},{2,258},{258,3},{3,259},{259,4},{4... | collective-permute-start | bytes 1179656 | tf_op jit(solution)/shard_map/ppermute | solution.py:18
  119.9 41.1 %collective-permute-start.3 = (bf16[128,12,128]{2,0,1:T(8,128)(2,1)S(1)}, bf16[128,12,128]{2,0,1:T(8,128)(2,1)S(1)}, u32[]{:S(2)}, u32[]{:S(2)}) collective-permute-start(bf16[128,12,128]{2,0,1:T(8,128)(2,1)S(1)} %get-tuple-element.44), channel_id=1, source_target_pairs={{256,0},{1,256},{257,1},{2,257},{258,2},{3,258},{259,3},{4,259},{2... | collective-permute-start | bytes 1179656 | tf_op jit(solution)/shard_map/ppermute | solution.py:19
  135.3 25.8 %copy-start.8 = (bf16[384,12,128]{2,0,1:T(8,128)(2,1)S(1)}, bf16[384,12,128]{2,0,1:T(8,128)(2,1)}, u32[]{:S(2)}) copy-start(bf16[384,12,128]{2,0,1:T(8,128)(2,1)} %copy-done.7) | copy-start | bytes 3538948
  162.1 26.8 %all-to-all-start.2 = ((bf16[16,24,4,128]{3,1,2,0:T(8,128)(2,1)}), bf16[16,24,4,128]{3,1,2,0:T(8,128)(2,1)S(1)}, u32[]{:S(2)}, u32[]{:S(2)}) async-start(bf16[16,24,4,128]{3,1,2,0:T(8,128)(2,1)} %copy.155), calls=%async_computation.2 | async-start | bytes 786432 | tf_op jit(solution)/shard_map/all_to_all | solution.py:163
  177.2 1.1 copy-start.9
  210.0 2.0 copy-start.1

commit v6 on v5

--- a/solution.py
+++ b/solution.py
@@ -88,7 +88,8 @@
     frame_index = lax.axis_index("frame")
     quarter_index = lax.axis_index("quarter")
     spatial_slot = (frame_index * quarters + quarter_index) * halves + half_index
-    temporal_slot = (quarter_index * halves + half_index) * frames + frame_index
+    own_piece = (frame_index % 2) * (frames // 2) + frame_index // 2
+    temporal_slot = (quarter_index * halves + half_index) * frames + own_piece
 
     heads = jnp.arange(head_count, dtype=jnp.int32)
     earlier = heads[None, :] < heads[:, None]
@@ -102,21 +103,32 @@
     )
     slots = jnp.sum(jnp.where(unslots[None, :] == heads[:, None], heads[None, :], 0), axis=1)
 
-    def grouped(array):
-        picked = jnp.take(array.reshape(tokens_here, head_count, width), slots, axis=1)
-        return picked.reshape(tokens_here, groups, per_group, width)
-
-    gq, gk, gv = grouped(queries), grouped(key_vectors), grouped(value_vectors)
+    columns = jnp.concatenate(
+        [
+            queries.reshape(tokens_here, head_count, width),
+            key_vectors.reshape(tokens_here, head_count, width),
+            value_vectors.reshape(tokens_here, head_count, width),
+        ],
+        axis=1,
+    )
+    grid = slots.reshape(groups, per_group)
     lo, hi = slice(0, lines_per_group), slice(lines_per_group, per_group)
-    stacked = jnp.concatenate(
-        [gq[:, :, lo], gk[:, :, lo], gv[:, :, lo], gq[:, :, hi], gk[:, :, hi], gv[:, :, hi]], axis=2
+    order = jnp.concatenate(
+        [grid[:, lo] + t * head_count for t in range(3)] + [grid[:, hi] + t * head_count for t in range(3)],
+        axis=1,
+    )
+    stacked = jnp.take(columns, order.reshape(-1), axis=1).reshape(
+        tokens_here, groups, 3 * per_group, width
     )
     frame_rows = lax.all_to_all(stacked, "x", split_axis=1, concat_axis=0, tiled=True)
     frame_rows = frame_rows.reshape(rows, 3 * per_group, width)
     line_part = frame_rows[:, : 3 * lines_per_group]
     space_part = frame_rows[:, 3 * lines_per_group :]
+    pairs = 2
+    rings = frames // pairs
+    pieces = line_part.reshape(pairs, rings, piece, 3 * lines_per_group, width)
     moved = lax.all_to_all(
-        line_part.reshape(frames, piece, 3 * lines_per_group, width),
+        jnp.transpose(pieces, (1, 0, 2, 3, 4)).reshape(frames, piece, 3 * lines_per_group, width),
         "frame",
         split_axis=0,
         concat_axis=0,
@@ -133,7 +145,8 @@
         linear(k % halves, k // (halves * quarters), (k // halves) % quarters) for k in range(chunks)
     ]
     temporal_order = [
-        linear((k // frames) % halves, k % frames, k // (frames * halves)) for k in range(chunks)
+        linear((k // frames) % halves, (k % rings) * pairs + (k % frames) // rings, k // (frames * halves))
+        for k in range(chunks)
     ]
     along = ("zh", "frame", "quarter")
     space_ext = with_halo(space_kv, along, spatial_order)
@@ -161,7 +174,9 @@
     space_out = run(space_part, space_ext, hi, spatial_slot)
 
     returned = lax.all_to_all(back, "frame", split_axis=0, concat_axis=0, tiled=True)
-    returned = returned.reshape(rows, lines_per_group, width)
+    returned = jnp.transpose(
+        returned.reshape(rings, pairs, piece, lines_per_group, width), (1, 0, 2, 3, 4)
+    ).reshape(rows, lines_per_group, width)
     frame_outputs = jnp.concatenate([returned, space_out], axis=1)
     merged = lax.all_to_all(
         frame_outputs.reshape(rows, 1, per_group, width),

time: 216 us -> 203 us (0.940)
  blocking collectives: 20 us -> 0 us
  starting transfers between devices: 61.8 us -> 68.8 us
  other arithmetic: 8.96 us -> 13.2 us
  local copies, waits for them, and re-layouts: 36.9 us -> 33 us
    all_to_all x1 -> x0, blocking collectives: 20 us -> none  [shards(): lax.all_to_all(frame_outputs.reshape(rows, 1, per_group, width), 'x', spl...]
    ppermute x2, waiting for transfers between devices: 29.5 us -> 12 us  [with_halo(): lower = lax.ppermute(cells[-width:], axes, pairs)]
    all_to_all x1 -> x2, waiting for transfers between devices: 23.5 us -> 40.6 us  [the longest x1 23.6 us: shards(): lax.all_to_all(jnp.transpose(pieces, (1, 0, 2, 3, 4)).reshape(frames, pie...]
    unnamed x43 -> x38, local copies, waits for them, and re-layouts: 7.71 us -> 1.81 us
    all_to_all x1 -> x2, starting transfers between devices: 16.5 us -> 20 us  [the longest x1 16.4 us: shards(): lax.all_to_all(jnp.transpose(pieces, (1, 0, 2, 3, 4)).reshape(frames, pie...]
    all_to_all x1, starting transfers between devices: 14.7 us -> 18.2 us  [shards(): lax.all_to_all(back, 'frame', split_axis=0, concat_axis=0, tiled=True)]
    select_n x2, other arithmetic: 1.53 us -> 3.8 us  [shards(): jnp.take(columns, order.reshape(-1), axis=1)]
    gather x3 -> x1, local copies, waits for them, and re-layouts: 3.15 us -> 4.34 us  [shards(): jnp.take(columns, order.reshape(-1), axis=1)]
  transfers between devices with their start and end apart: 7 -> 8, of which waited for: 5 -> 7; matrix products, arithmetic and copies ran while one was open for 12% -> 12% of each run, Pallas kernels for 0% -> 0%
where the time goes in v6:
time: 203 us; the launch traced here: 200 us
  waiting for transfers between devices  80.7 us (40%)
  starting transfers between devices  68.8 us (34%)
  local copies, waits for them, and re-layouts  33 us (16%)
  other arithmetic  13.2 us (7%)
  matrix products  3.91 us (2%)
    all_to_all x1, waiting for transfers between devices, shards(): lax.all_to_all(jnp.transpose(pieces, (1, 0, 2, 3, 4)).reshape(frames, pie...  23.6 us
    ppermute x2, starting transfers between devices, with_halo(): upper = lax.ppermute(cells[:width], axes, [(b, a) for a, b in pairs])  21.7 us
    all_to_all x1, waiting for transfers between devices, shards(): lax.all_to_all(stacked, 'x', split_axis=1, concat_axis=0, tiled=True)  20.8 us
    all_to_all x1, starting transfers between devices, shards(): lax.all_to_all(back, 'frame', split_axis=0, concat_axis=0, tiled=True)  18.2 us
    all_to_all x1, waiting for transfers between devices, shards(): lax.all_to_all(frame_outputs.reshape(rows, 1, per_group, width), 'x', spl...  17.1 us
    all_to_all x1, starting transfers between devices, shards(): lax.all_to_all(jnp.transpose(pieces, (1, 0, 2, 3, 4)).reshape(frames, pie...  16.4 us
    ppermute x2, waiting for transfers between devices, with_halo(): lower = lax.ppermute(cells[-width:], axes, pairs)  12 us
    all_to_all x1, waiting for transfers between devices, shards(): lax.all_to_all(back, 'frame', split_axis=0, concat_axis=0, tiled=True)  6.77 us
  transfers between devices with their start and end apart: 8, of which 7 were waited for; matrix products, arithmetic and copies ran while one was open for 12% of the time, Pallas kernels for 0%

profile of v6, /device:TPU:1, one launch (start us, length us, event | category | flops | bytes accessed | tf_op | source)
XLA Modules:
  0.0 200.2 jit_solution(7968970071008990141)
XLA Ops:
  0.0 0.7 broadcast_compare_fusion.2
  0.9 0.7 compare_and_fusion.4
  2.0 1.4 copy_bitcast_fusion.2
  3.4 1.5 copy_bitcast_fusion
  5.0 1.9 pad_maximum_fusion
  6.9 4.3 %gather_fusion = bf16[120,96,128]{2,1,0:T(8,128)(2,1)} fusion(bf16[96,120,128]{2,0,1:T(8,128)(2,1)} %pad_maximum_fusion, s32[1024]{0:T(1024)S(1)} %pad_clamp_fusion.4), kind=kCustom, calls=%fused_computation.3 | custom fusion | bytes 5898720 | tf_op jit(solution)/shard_map/jit(_take)/gather | solution.py:120
  11.3 3.8 %broadcast_select_fusion = bf16[96,4,30,128]{3,0,2,1:T(8,128)(2,1)} fusion(bf16[96,4,30,128]{3,0,2,1:T(8,128)(2,1)} %bitcast.120, pred[4,30]{1,0:T(4,128)(4,1)S(1)} %compare_and_fusion.3), kind=kLoop, calls=%fused_computation.27 | loop fusion | flops 1474560 | bytes 5898360 | tf_op jit(solution)/shard_map/jit(_take)/select_n | solution.py:120
  15.1 5.0 %all-to-all-start = ((bf16[96,4,30,128]{3,0,2,1:T(8,128)(2,1)}), bf16[96,4,30,128]{3,0,2,1:T(8,128)(2,1)}, u32[]{:S(2)}, u32[]{:S(2)}) async-start(bf16[96,4,30,128]{3,0,2,1:T(8,128)(2,1)} %broadcast_select_fusion), calls=%async_computation | async-start | bytes 5898240 | tf_op jit(solution)/shard_map/all_to_all | solution.py:123
  20.1 0.6 gather_fusion.2
  20.8 0.6 gather_fusion.4
  21.4 0.7 gather_fusion.1
  22.1 0.7 gather_fusion.3
  23.1 0.7 gather_fusion.12
  23.8 0.7 gather_fusion.11
  24.4 0.7 gather_fusion.10
  25.3 0.9 gather_fusion.7
  26.4 1.0 gather_fusion.9
  27.5 0.5 copy.200
  28.0 0.7 gather_fusion.6
  28.9 20.8 %all-to-all-done = bf16[96,4,30,128]{3,0,2,1:T(8,128)(2,1)} async-done(((bf16[96,4,30,128]{3,0,2,1:T(8,128)(2,1)}), bf16[96,4,30,128]{3,0,2,1:T(8,128)(2,1)}, u32[]{:S(2)}, u32[]{:S(2)}) %all-to-all-start) | async-done | bytes 2949152 | tf_op jit(solution)/shard_map/all_to_all | solution.py:123
  49.7 2.2 %copy.192 = bf16[4,96,1,30,128]{4,1,0,3,2:T(8,128)(2,1)S(1)} copy(bf16[4,96,1,30,128]{4,1,3,0,2:T(8,128)(2,1)} %bitcast.5) | data formatting | bytes 5898240 | tf_op jit(solution)/shard_map/all_to_all | solution.py:123
  52.1 1.6 copy.193
  53.9 16.4 %all-to-all-start.1 = ((bf16[16,24,12,128]{3,1,2,0:T(8,128)(2,1)}), bf16[16,24,12,128]{3,1,2,0:T(8,128)(2,1)S(1)}, u32[]{:S(2)}, u32[]{:S(2)}) async-start(bf16[16,24,12,128]{3,1,2,0:T(8,128)(2,1)} %bitcast.125), calls=%async_computation.1 | async-start | bytes 2359296 | tf_op jit(solution)/shard_map/all_to_all | solution.py:130
  70.6 2.2 %copy.213 = s32[6,768,5]{2,1,0:T(8,128)} copy(s32[6,768,5]{1,0,2:T(8,128)S(1)} %broadcast_select_fusion.1) | data formatting | bytes 184320 | tf_op jit(solution)/shard_map/jit(_take)/select_n | solution.py:26
  72.8 1.6 gather_fusion.8
  74.8 1.9 slice.259
  76.7 23.6 %all-to-all-done.1 = bf16[16,24,12,128]{3,1,2,0:T(8,128)(2,1)S(1)} async-done(((bf16[16,24,12,128]{3,1,2,0:T(8,128)(2,1)}), bf16[16,24,12,128]{3,1,2,0:T(8,128)(2,1)S(1)}, u32[]{:S(2)}, u32[]{:S(2)}) %all-to-all-start.1) | async-done | bytes 1179680 | tf_op jit(solution)/shard_map/all_to_all | solution.py:130
  100.8 14.3 %collective-permute-start.1 = (bf16[128,8,128]{2,0,1:T(8,128)(2,1)S(1)}, bf16[128,8,128]{2,0,1:T(8,128)(2,1)S(1)}, u32[]{:S(2)}, u32[]{:S(2)}) collective-permute-start(bf16[128,8,128]{2,0,1:T(8,128)(2,1)S(1)} %get-tuple-element.47), channel_id=1, source_target_pairs={{8,0},{16,8},{24,16},{32,24},{40,32},{48,40},{56,48},{4,56},{12,4}... | collective-permute-start | bytes 786440 | tf_op jit(solution)/shard_map/ppermute | solution.py:19
  115.1 1.9 collective-permute-start
  117.1 2.0 %collective-permute-start.2 = (bf16[128,12,128]{2,0,1:T(8,128)(2,1)S(1)}, bf16[128,12,128]{2,0,1:T(8,128)(2,1)S(1)}, u32[]{:S(2)}, u32[]{:S(2)}) collective-permute-start(bf16[128,12,128]{2,0,1:T(8,128)(2,1)S(1)} %get-tuple-element.42), channel_id=1, source_target_pairs={{0,256},{256,1},{1,257},{257,2},{2,258},{258,3},{3,259},{259,4},{4... | collective-permute-start | bytes 1179656 | tf_op jit(solution)/shard_map/ppermute | solution.py:18
  119.2 7.5 %collective-permute-start.3 = (bf16[128,12,128]{2,0,1:T(8,128)(2,1)S(1)}, bf16[128,12,128]{2,0,1:T(8,128)(2,1)S(1)}, u32[]{:S(2)}, u32[]{:S(2)}) collective-permute-start(bf16[128,12,128]{2,0,1:T(8,128)(2,1)S(1)} %get-tuple-element.43), channel_id=1, source_target_pairs={{256,0},{1,256},{257,1},{2,257},{258,2},{3,258},{259,3},{4,259},{2... | collective-permute-start | bytes 1179656 | tf_op jit(solution)/shard_map/ppermute | solution.py:19
  126.7 6.0 %collective-permute-done = bf16[128,8,128]{2,0,1:T(8,128)(2,1)S(1)} collective-permute-done((bf16[128,8,128]{2,0,1:T(8,128)(2,1)S(1)}, bf16[128,8,128]{2,0,1:T(8,128)(2,1)S(1)}, u32[]{:S(2)}, u32[]{:S(2)}) %collective-permute-start) | collective-permute-done | bytes 262176 | tf_op jit(solution)/shard_map/ppermute | solution.py:18
  133.5 0.7 fusion.3
  134.2 1.2 fusion.4
  135.8 0.8 fusion.37
  136.6 6.0 %collective-permute-done.2 = bf16[128,12,128]{2,0,1:T(8,128)(2,1)S(1)} collective-permute-done((bf16[128,12,128]{2,0,1:T(8,128)(2,1)S(1)}, bf16[128,12,128]{2,0,1:T(8,128)(2,1)S(1)}, u32[]{:S(2)}, u32[]{:S(2)}) %collective-permute-start.2) | collective-permute-done | bytes 393248 | tf_op jit(solution)/shard_map/ppermute | solution.py:18
  143.3 0.8 copy.206
  144.1 18.2 %all-to-all-start.2 = ((bf16[16,24,4,128]{3,1,2,0:T(8,128)(2,1)}), bf16[16,24,4,128]{3,1,2,0:T(8,128)(2,1)S(1)}, u32[]{:S(2)}, u32[]{:S(2)}) async-start(bf16[16,24,4,128]{3,1,2,0:T(8,128)(2,1)} %copy.206), calls=%async_computation.2 | async-start | bytes 786432 | tf_op jit(solution)/shard_map/all_to_all | solution.py:176
  163.1 0.7 copy-done.9
  163.8 1.2 fusion
  164.9 1.9 fusion.1
  167.3 1.2 fusion.22
  168.5 6.8 %all-to-all-done.2 = bf16[16,24,4,128]{3,1,2,0:T(8,128)(2,1)S(1)} async-done(((bf16[16,24,4,128]{3,1,2,0:T(8,128)(2,1)}), bf16[16,24,4,128]{3,1,2,0:T(8,128)(2,1)S(1)}, u32[]{:S(2)}, u32[]{:S(2)}) %all-to-all-start.2) | async-done | bytes 393248 | tf_op jit(solution)/shard_map/all_to_all | solution.py:176
  175.4 1.9 copy.219
  177.3 3.6 %all-to-all-start.3 = ((bf16[384,1,10,128]{3,2,1,0:T(8,128)(2,1)}), bf16[384,1,10,128]{3,2,1,0:T(8,128)(2,1)S(1)}, u32[]{:S(2)}, u32[]{:S(2)}) async-start(bf16[384,1,10,128]{3,2,1,0:T(8,128)(2,1)} %copy.219), calls=%async_computation.3 | async-start | bytes 3145728 | tf_op jit(solution)/shard_map/all_to_all | solution.py:181
  180.9 17.1 %all-to-all-done.3 = bf16[384,1,10,128]{3,2,1,0:T(8,128)(2,1)S(1)} async-done(((bf16[384,1,10,128]{3,2,1,0:T(8,128)(2,1)}), bf16[384,1,10,128]{3,2,1,0:T(8,128)(2,1)S(1)}, u32[]{:S(2)}, u32[]{:S(2)}) %all-to-all-start.3) | async-done | bytes 983072 | tf_op jit(solution)/shard_map/all_to_all | solution.py:181
  198.4 0.7 gather_fusion.5
  199.1 1.1 bitcast_select_fusion
  (112 shorter events, 6.8 us)
Async XLA Ops:
  0.0 3.4 %copy-start = (bf16[96,5120]{1,0:T(8,128)(2,1)S(1)}, bf16[96,5120]{1,0:T(8,128)(2,1)}, u32[]{:S(2)}) copy-start(bf16[96,5120]{1,0:T(8,128)(2,1)} %param.12) | copy-start | bytes 2949124
  15.0 5.1 %copy-start.10 = (s32[40,768]{1,0:T(8,128)S(1)}, s32[40,768]{1,0:T(8,128)}, u32[]{:S(2)}) copy-start(s32[40,768]{1,0:T(8,128)} %param.16) | copy-start | bytes 368644
  15.1 6.3 %copy-start.2 = (s32[40,768,5]{1,0,2:T(8,128)S(1)}, s32[40,768,5]{1,0,2:T(8,128)}, u32[]{:S(2)}) copy-start(s32[40,768,5]{1,0,2:T(8,128)} %param.15) | copy-start | bytes 1843204
  15.1 34.6 %all-to-all-start = ((bf16[96,4,30,128]{3,0,2,1:T(8,128)(2,1)}), bf16[96,4,30,128]{3,0,2,1:T(8,128)(2,1)}, u32[]{:S(2)}, u32[]{:S(2)}) async-start(bf16[96,4,30,128]{3,0,2,1:T(8,128)(2,1)} %broadcast_select_fusion), calls=%async_computation | async-start | bytes 5898240 | tf_op jit(solution)/shard_map/all_to_all | solution.py:123
  22.1 1.0 copy-start.3
  22.1 1.7 copy-start.4
  22.1 2.3 %copy-start.5 = (f32[40]{0:T(128)S(1)}, f32[40]{0:T(128)}, u32[]{:S(2)}) copy-start(f32[40]{0:T(128)} %param.17) | copy-start | bytes 484
  51.9 2.0 copy-start.6
  52.1 64.9 %copy-start.7 = (bf16[384,12,128]{2,0,1:T(8,128)(2,1)}, bf16[384,12,128]{2,0,1:T(8,128)(2,1)S(1)}, u32[]{:S(2)}) copy-start(bf16[384,12,128]{2,0,1:T(8,128)(2,1)S(1)} %get-tuple-element.11) | copy-start | bytes 3538948
  53.9 46.4 %all-to-all-start.1 = ((bf16[16,24,12,128]{3,1,2,0:T(8,128)(2,1)}), bf16[16,24,12,128]{3,1,2,0:T(8,128)(2,1)S(1)}, u32[]{:S(2)}, u32[]{:S(2)}) async-start(bf16[16,24,12,128]{3,1,2,0:T(8,128)(2,1)} %bitcast.125), calls=%async_computation.1 | async-start | bytes 2359296 | tf_op jit(solution)/shard_map/all_to_all | solution.py:130
  100.8 25.9 %collective-permute-start.1 = (bf16[128,8,128]{2,0,1:T(8,128)(2,1)S(1)}, bf16[128,8,128]{2,0,1:T(8,128)(2,1)S(1)}, u32[]{:S(2)}, u32[]{:S(2)}) collective-permute-start(bf16[128,8,128]{2,0,1:T(8,128)(2,1)S(1)} %get-tuple-element.47), channel_id=1, source_target_pairs={{8,0},{16,8},{24,16},{32,24},{40,32},{48,40},{56,48},{4,56},{12,4}... | collective-permute-start | bytes 786440 | tf_op jit(solution)/shard_map/ppermute | solution.py:19
  115.1 17.6 %collective-permute-start = (bf16[128,8,128]{2,0,1:T(8,128)(2,1)S(1)}, bf16[128,8,128]{2,0,1:T(8,128)(2,1)S(1)}, u32[]{:S(2)}, u32[]{:S(2)}) collective-permute-start(bf16[128,8,128]{2,0,1:T(8,128)(2,1)S(1)} %get-tuple-element.48), channel_id=1, source_target_pairs={{0,8},{8,16},{16,24},{24,32},{32,40},{40,48},{48,56},{56,4},{4,12}... | collective-permute-start | bytes 786440 | tf_op jit(solution)/shard_map/ppermute | solution.py:18
  117.1 25.5 %collective-permute-start.2 = (bf16[128,12,128]{2,0,1:T(8,128)(2,1)S(1)}, bf16[128,12,128]{2,0,1:T(8,128)(2,1)S(1)}, u32[]{:S(2)}, u32[]{:S(2)}) collective-permute-start(bf16[128,12,128]{2,0,1:T(8,128)(2,1)S(1)} %get-tuple-element.42), channel_id=1, source_target_pairs={{0,256},{256,1},{1,257},{257,2},{2,258},{258,3},{3,259},{259,4},{4... | collective-permute-start | bytes 1179656 | tf_op jit(solution)/shard_map/ppermute | solution.py:18
  119.2 23.9 %collective-permute-start.3 = (bf16[128,12,128]{2,0,1:T(8,128)(2,1)S(1)}, bf16[128,12,128]{2,0,1:T(8,128)(2,1)S(1)}, u32[]{:S(2)}, u32[]{:S(2)}) collective-permute-start(bf16[128,12,128]{2,0,1:T(8,128)(2,1)S(1)} %get-tuple-element.43), channel_id=1, source_target_pairs={{256,0},{1,256},{257,1},{2,257},{258,2},{3,258},{259,3},{4,259},{2... | collective-permute-start | bytes 1179656 | tf_op jit(solution)/shard_map/ppermute | solution.py:19
  135.8 7.3 %copy-start.8 = (bf16[384,12,128]{2,0,1:T(8,128)(2,1)S(1)}, bf16[384,12,128]{2,0,1:T(8,128)(2,1)}, u32[]{:S(2)}) copy-start(bf16[384,12,128]{2,0,1:T(8,128)(2,1)} %copy-done.7) | copy-start | bytes 3538948
  144.1 31.2 %all-to-all-start.2 = ((bf16[16,24,4,128]{3,1,2,0:T(8,128)(2,1)}), bf16[16,24,4,128]{3,1,2,0:T(8,128)(2,1)S(1)}, u32[]{:S(2)}, u32[]{:S(2)}) async-start(bf16[16,24,4,128]{3,1,2,0:T(8,128)(2,1)} %copy.206), calls=%async_computation.2 | async-start | bytes 786432 | tf_op jit(solution)/shard_map/all_to_all | solution.py:176
  162.7 1.1 copy-start.9
  177.3 20.7 %all-to-all-start.3 = ((bf16[384,1,10,128]{3,2,1,0:T(8,128)(2,1)}), bf16[384,1,10,128]{3,2,1,0:T(8,128)(2,1)S(1)}, u32[]{:S(2)}, u32[]{:S(2)}) async-start(bf16[384,1,10,128]{3,2,1,0:T(8,128)(2,1)} %copy.219), calls=%async_computation.3 | async-start | bytes 3145728 | tf_op jit(solution)/shard_map/all_to_all | solution.py:181
  198.3 2.0 copy-start.1

commit v7 on v6

--- a/solution.py
+++ b/solution.py
@@ -117,9 +117,12 @@
         [grid[:, lo] + t * head_count for t in range(3)] + [grid[:, hi] + t * head_count for t in range(3)],
         axis=1,
     )
-    stacked = jnp.take(columns, order.reshape(-1), axis=1).reshape(
-        tokens_here, groups, 3 * per_group, width
-    )
+    picks = (
+        order.reshape(-1)[:, None] == jnp.arange(3 * head_count, dtype=jnp.int32)[None, :]
+    ).astype(jnp.bfloat16)
+    stacked = jnp.einsum(
+        "sh,thd->tsd", picks, columns, preferred_element_type=jnp.bfloat16
+    ).reshape(tokens_here, groups, 3 * per_group, width)
     frame_rows = lax.all_to_all(stacked, "x", split_axis=1, concat_axis=0, tiled=True)
     frame_rows = frame_rows.reshape(rows, 3 * per_group, width)
     line_part = frame_rows[:, : 3 * lines_per_group]

time: 203 us -> 196 us (0.966)
  other arithmetic: 13.2 us -> 7.5 us
  local copies, waits for them, and re-layouts: 33 us -> 29.3 us
    gather x1 -> x0, local copies, waits for them, and re-layouts: 4.34 us -> none  [shards(): jnp.take(columns, order.reshape(-1), axis=1)]
    select_n x2 -> x0, other arithmetic: 3.8 us -> none  [shards(): jnp.take(columns, order.reshape(-1), axis=1)]
    reshape x3 -> x0, local copies, waits for them, and re-layouts: 3 us -> none  [the longest x1 1.54 us: shards(): value_vectors.reshape(tokens_here, head_count, width)]
    unnamed x38 -> x39, local copies, waits for them, and re-layouts: 1.81 us -> 4.15 us
    transpose x0 -> x1, local copies, waits for them, and re-layouts: none -> 2.09 us  [shards(): jnp.einsum('sh,thd->tsd', picks, columns, preferred_element_type=jnp.bflo...]
where the time goes in v7:
time: 196 us; the launch traced here: 194 us
  waiting for transfers between devices  82.1 us (42%)
  starting transfers between devices  68.7 us (35%)
  local copies, waits for them, and re-layouts  29.3 us (15%)
  other arithmetic  7.5 us (4%)
  matrix products  5.16 us (3%)
    all_to_all x1, waiting for transfers between devices, shards(): lax.all_to_all(jnp.transpose(pieces, (1, 0, 2, 3, 4)).reshape(frames, pie...  24.4 us
    ppermute x2, starting transfers between devices, with_halo(): upper = lax.ppermute(cells[:width], axes, [(b, a) for a, b in pairs])  21.7 us
    all_to_all x1, waiting for transfers between devices, shards(): lax.all_to_all(stacked, 'x', split_axis=1, concat_axis=0, tiled=True)  20.8 us
    all_to_all x1, starting transfers between devices, shards(): lax.all_to_all(back, 'frame', split_axis=0, concat_axis=0, tiled=True)  18.1 us
    all_to_all x1, waiting for transfers between devices, shards(): lax.all_to_all(frame_outputs.reshape(rows, 1, per_group, width), 'x', spl...  17.1 us
    all_to_all x1, starting transfers between devices, shards(): lax.all_to_all(jnp.transpose(pieces, (1, 0, 2, 3, 4)).reshape(frames, pie...  16.4 us
    ppermute x2, waiting for transfers between devices, with_halo(): lower = lax.ppermute(cells[-width:], axes, pairs)  12 us
    all_to_all x1, waiting for transfers between devices, shards(): lax.all_to_all(back, 'frame', split_axis=0, concat_axis=0, tiled=True)  7.43 us
  transfers between devices with their start and end apart: 8, of which 7 were waited for; matrix products, arithmetic and copies ran while one was open for 12% of the time, Pallas kernels for 0%

profile of v7, /device:TPU:1, one launch (start us, length us, event | category | flops | bytes accessed | tf_op | source)
XLA Modules:
  0.0 193.5 jit_solution(12954270695801630087)
XLA Ops:
  0.0 0.8 broadcast_compare_fusion.2
  0.9 0.7 compare_and_fusion.3
  2.0 1.4 copy.196
  3.4 1.4 copy.197
  5.0 1.2 fusion.18
  6.3 2.1 %copy.153 = bf16[96,120,128]{2,0,1:T(8,128)(2,1)} copy(bf16[96,120,128]{2,1,0:T(8,128)(2,1)S(1)} %fusion.18) | data formatting | bytes 5898240 | tf_op jit(solution)/shard_map/sh,thd->tsd/transpose | solution.py:123
  8.3 5.0 %all-to-all-start = ((bf16[96,4,30,128]{3,0,2,1:T(8,128)(2,1)}), bf16[96,4,30,128]{3,0,2,1:T(8,128)(2,1)}, u32[]{:S(2)}, u32[]{:S(2)}) async-start(bf16[96,4,30,128]{3,0,2,1:T(8,128)(2,1)} %bitcast.110), calls=%async_computation | async-start | bytes 5898240 | tf_op jit(solution)/shard_map/all_to_all | solution.py:126
  13.4 0.6 gather_fusion.1
  14.1 0.6 gather_fusion.3
  14.7 0.7 gather_fusion
  15.4 0.7 gather_fusion.2
  16.4 0.7 gather_fusion.11
  17.1 0.7 gather_fusion.10
  17.7 0.7 gather_fusion.9
  18.6 0.9 gather_fusion.6
  19.6 1.0 gather_fusion.8
  20.8 0.5 copy.162
  21.3 0.7 gather_fusion.5
  22.2 20.8 %all-to-all-done = bf16[96,4,30,128]{3,0,2,1:T(8,128)(2,1)} async-done(((bf16[96,4,30,128]{3,0,2,1:T(8,128)(2,1)}), bf16[96,4,30,128]{3,0,2,1:T(8,128)(2,1)}, u32[]{:S(2)}, u32[]{:S(2)}) %all-to-all-start) | async-done | bytes 2949152 | tf_op jit(solution)/shard_map/all_to_all | solution.py:126
  43.0 2.2 %copy.154 = bf16[4,96,1,30,128]{4,1,0,3,2:T(8,128)(2,1)S(1)} copy(bf16[4,96,1,30,128]{4,1,3,0,2:T(8,128)(2,1)} %bitcast.5) | data formatting | bytes 5898240 | tf_op jit(solution)/shard_map/all_to_all | solution.py:126
  45.4 1.6 copy.155
  47.1 16.4 %all-to-all-start.1 = ((bf16[16,24,12,128]{3,1,2,0:T(8,128)(2,1)}), bf16[16,24,12,128]{3,1,2,0:T(8,128)(2,1)S(1)}, u32[]{:S(2)}, u32[]{:S(2)}) async-start(bf16[16,24,12,128]{3,1,2,0:T(8,128)(2,1)} %bitcast.117), calls=%async_computation.1 | async-start | bytes 2359296 | tf_op jit(solution)/shard_map/all_to_all | solution.py:133
  63.9 2.2 %copy.175 = s32[6,768,5]{2,1,0:T(8,128)} copy(s32[6,768,5]{1,0,2:T(8,128)S(1)} %broadcast_select_fusion) | data formatting | bytes 184320 | tf_op jit(solution)/shard_map/jit(_take)/select_n | solution.py:26
  66.1 1.6 gather_fusion.7
  68.1 1.1 slice.257
  69.2 24.4 %all-to-all-done.1 = bf16[16,24,12,128]{3,1,2,0:T(8,128)(2,1)S(1)} async-done(((bf16[16,24,12,128]{3,1,2,0:T(8,128)(2,1)}), bf16[16,24,12,128]{3,1,2,0:T(8,128)(2,1)S(1)}, u32[]{:S(2)}, u32[]{:S(2)}) %all-to-all-start.1) | async-done | bytes 1179680 | tf_op jit(solution)/shard_map/all_to_all | solution.py:133
  93.6 0.5 copy.156
  94.1 14.3 %collective-permute-start.1 = (bf16[128,8,128]{2,0,1:T(8,128)(2,1)S(1)}, bf16[128,8,128]{2,0,1:T(8,128)(2,1)S(1)}, u32[]{:S(2)}, u32[]{:S(2)}) collective-permute-start(bf16[128,8,128]{2,0,1:T(8,128)(2,1)S(1)} %get-tuple-element.47), channel_id=1, source_target_pairs={{8,0},{16,8},{24,16},{32,24},{40,32},{48,40},{56,48},{4,56},{12,4}... | collective-permute-start | bytes 786440 | tf_op jit(solution)/shard_map/ppermute | solution.py:19
  108.4 1.9 collective-permute-start
  110.4 2.0 %collective-permute-start.2 = (bf16[128,12,128]{2,0,1:T(8,128)(2,1)S(1)}, bf16[128,12,128]{2,0,1:T(8,128)(2,1)S(1)}, u32[]{:S(2)}, u32[]{:S(2)}) collective-permute-start(bf16[128,12,128]{2,0,1:T(8,128)(2,1)S(1)} %get-tuple-element.42), channel_id=1, source_target_pairs={{0,256},{256,1},{1,257},{257,2},{2,258},{258,3},{3,259},{259,4},{4... | collective-permute-start | bytes 1179656 | tf_op jit(solution)/shard_map/ppermute | solution.py:18
  112.4 7.5 %collective-permute-start.3 = (bf16[128,12,128]{2,0,1:T(8,128)(2,1)S(1)}, bf16[128,12,128]{2,0,1:T(8,128)(2,1)S(1)}, u32[]{:S(2)}, u32[]{:S(2)}) collective-permute-start(bf16[128,12,128]{2,0,1:T(8,128)(2,1)S(1)} %get-tuple-element.43), channel_id=1, source_target_pairs={{256,0},{1,256},{257,1},{2,257},{258,2},{3,258},{259,3},{4,259},{2... | collective-permute-start | bytes 1179656 | tf_op jit(solution)/shard_map/ppermute | solution.py:19
  120.0 6.0 %collective-permute-done = bf16[128,8,128]{2,0,1:T(8,128)(2,1)S(1)} collective-permute-done((bf16[128,8,128]{2,0,1:T(8,128)(2,1)S(1)}, bf16[128,8,128]{2,0,1:T(8,128)(2,1)S(1)}, u32[]{:S(2)}, u32[]{:S(2)}) %collective-permute-start) | collective-permute-done | bytes 262176 | tf_op jit(solution)/shard_map/ppermute | solution.py:18
  126.0 0.5 fusion.53
  126.8 0.7 fusion.3
  127.5 1.2 fusion.4
  129.1 0.8 fusion.46
  129.9 6.1 %collective-permute-done.2 = bf16[128,12,128]{2,0,1:T(8,128)(2,1)S(1)} collective-permute-done((bf16[128,12,128]{2,0,1:T(8,128)(2,1)S(1)}, bf16[128,12,128]{2,0,1:T(8,128)(2,1)S(1)}, u32[]{:S(2)}, u32[]{:S(2)}) %collective-permute-start.2) | collective-permute-done | bytes 393248 | tf_op jit(solution)/shard_map/ppermute | solution.py:18
  136.6 0.8 copy.168
  137.4 18.1 %all-to-all-start.2 = ((bf16[16,24,4,128]{3,1,2,0:T(8,128)(2,1)}), bf16[16,24,4,128]{3,1,2,0:T(8,128)(2,1)S(1)}, u32[]{:S(2)}, u32[]{:S(2)}) async-start(bf16[16,24,4,128]{3,1,2,0:T(8,128)(2,1)} %copy.168), calls=%async_computation.2 | async-start | bytes 786432 | tf_op jit(solution)/shard_map/all_to_all | solution.py:179
  156.4 1.2 fusion
  157.6 1.9 fusion.1
  159.9 1.2 fusion.31
  161.2 7.4 %all-to-all-done.2 = bf16[16,24,4,128]{3,1,2,0:T(8,128)(2,1)S(1)} async-done(((bf16[16,24,4,128]{3,1,2,0:T(8,128)(2,1)}), bf16[16,24,4,128]{3,1,2,0:T(8,128)(2,1)S(1)}, u32[]{:S(2)}, u32[]{:S(2)}) %all-to-all-start.2) | async-done | bytes 393248 | tf_op jit(solution)/shard_map/all_to_all | solution.py:179
  168.7 1.9 copy.181
  170.6 3.6 %all-to-all-start.3 = ((bf16[384,1,10,128]{3,2,1,0:T(8,128)(2,1)}), bf16[384,1,10,128]{3,2,1,0:T(8,128)(2,1)S(1)}, u32[]{:S(2)}, u32[]{:S(2)}) async-start(bf16[384,1,10,128]{3,2,1,0:T(8,128)(2,1)} %copy.181), calls=%async_computation.3 | async-start | bytes 3145728 | tf_op jit(solution)/shard_map/all_to_all | solution.py:184
  174.3 17.1 %all-to-all-done.3 = bf16[384,1,10,128]{3,2,1,0:T(8,128)(2,1)S(1)} async-done(((bf16[384,1,10,128]{3,2,1,0:T(8,128)(2,1)}), bf16[384,1,10,128]{3,2,1,0:T(8,128)(2,1)S(1)}, u32[]{:S(2)}, u32[]{:S(2)}) %all-to-all-start.3) | async-done | bytes 983072 | tf_op jit(solution)/shard_map/all_to_all | solution.py:184
  191.7 0.7 gather_fusion.4
  192.4 1.1 bitcast_select_fusion
  (107 shorter events, 6.0 us)
Async XLA Ops:
  0.0 14.6 %copy-start = (s32[40,768,5]{1,0,2:T(8,128)S(1)}, s32[40,768,5]{1,0,2:T(8,128)}, u32[]{:S(2)}) copy-start(s32[40,768,5]{1,0,2:T(8,128)} %param.15) | copy-start | bytes 1843204
  0.0 4.8 %copy-start.8 = (bf16[96,5120]{1,0:T(8,128)(2,1)S(1)}, bf16[96,5120]{1,0:T(8,128)(2,1)}, u32[]{:S(2)}) copy-start(bf16[96,5120]{1,0:T(8,128)(2,1)} %param.13) | copy-start | bytes 2949124
  8.3 5.1 %copy-start.9 = (s32[40,768]{1,0:T(8,128)S(1)}, s32[40,768]{1,0:T(8,128)}, u32[]{:S(2)}) copy-start(s32[40,768]{1,0:T(8,128)} %param.16) | copy-start | bytes 368644
  8.3 34.6 %all-to-all-start = ((bf16[96,4,30,128]{3,0,2,1:T(8,128)(2,1)}), bf16[96,4,30,128]{3,0,2,1:T(8,128)(2,1)}, u32[]{:S(2)}, u32[]{:S(2)}) async-start(bf16[96,4,30,128]{3,0,2,1:T(8,128)(2,1)} %bitcast.110), calls=%async_computation | async-start | bytes 5898240 | tf_op jit(solution)/shard_map/all_to_all | solution.py:126
  15.4 1.0 copy-start.2
  15.4 1.7 copy-start.3
  15.4 2.3 %copy-start.4 = (f32[40]{0:T(128)S(1)}, f32[40]{0:T(128)}, u32[]{:S(2)}) copy-start(f32[40]{0:T(128)} %param.17) | copy-start | bytes 484
  45.2 2.0 %copy-start.5 = (bf16[4,96,1,30,128]{4,1,0,3,2:T(8,128)(2,1)}, bf16[4,96,1,30,128]{4,1,0,3,2:T(8,128)(2,1)S(1)}, u32[]{:S(2)}) copy-start(bf16[4,96,1,30,128]{4,1,0,3,2:T(8,128)(2,1)S(1)} %copy.154) | copy-start | bytes 8847364
  45.4 65.0 %copy-start.6 = (bf16[384,12,128]{2,0,1:T(8,128)(2,1)}, bf16[384,12,128]{2,0,1:T(8,128)(2,1)S(1)}, u32[]{:S(2)}) copy-start(bf16[384,12,128]{2,0,1:T(8,128)(2,1)S(1)} %get-tuple-element.11) | copy-start | bytes 3538948
  47.1 46.4 %all-to-all-start.1 = ((bf16[16,24,12,128]{3,1,2,0:T(8,128)(2,1)}), bf16[16,24,12,128]{3,1,2,0:T(8,128)(2,1)S(1)}, u32[]{:S(2)}, u32[]{:S(2)}) async-start(bf16[16,24,12,128]{3,1,2,0:T(8,128)(2,1)} %bitcast.117), calls=%async_computation.1 | async-start | bytes 2359296 | tf_op jit(solution)/shard_map/all_to_all | solution.py:133
  94.1 25.9 %collective-permute-start.1 = (bf16[128,8,128]{2,0,1:T(8,128)(2,1)S(1)}, bf16[128,8,128]{2,0,1:T(8,128)(2,1)S(1)}, u32[]{:S(2)}, u32[]{:S(2)}) collective-permute-start(bf16[128,8,128]{2,0,1:T(8,128)(2,1)S(1)} %get-tuple-element.47), channel_id=1, source_target_pairs={{8,0},{16,8},{24,16},{32,24},{40,32},{48,40},{56,48},{4,56},{12,4}... | collective-permute-start | bytes 786440 | tf_op jit(solution)/shard_map/ppermute | solution.py:19
  108.4 17.5 %collective-permute-start = (bf16[128,8,128]{2,0,1:T(8,128)(2,1)S(1)}, bf16[128,8,128]{2,0,1:T(8,128)(2,1)S(1)}, u32[]{:S(2)}, u32[]{:S(2)}) collective-permute-start(bf16[128,8,128]{2,0,1:T(8,128)(2,1)S(1)} %get-tuple-element.48), channel_id=1, source_target_pairs={{0,8},{8,16},{16,24},{24,32},{32,40},{40,48},{48,56},{56,4},{4,12}... | collective-permute-start | bytes 786440 | tf_op jit(solution)/shard_map/ppermute | solution.py:18
  110.4 25.6 %collective-permute-start.2 = (bf16[128,12,128]{2,0,1:T(8,128)(2,1)S(1)}, bf16[128,12,128]{2,0,1:T(8,128)(2,1)S(1)}, u32[]{:S(2)}, u32[]{:S(2)}) collective-permute-start(bf16[128,12,128]{2,0,1:T(8,128)(2,1)S(1)} %get-tuple-element.42), channel_id=1, source_target_pairs={{0,256},{256,1},{1,257},{257,2},{2,258},{258,3},{3,259},{259,4},{4... | collective-permute-start | bytes 1179656 | tf_op jit(solution)/shard_map/ppermute | solution.py:18
  112.4 24.0 %collective-permute-start.3 = (bf16[128,12,128]{2,0,1:T(8,128)(2,1)S(1)}, bf16[128,12,128]{2,0,1:T(8,128)(2,1)S(1)}, u32[]{:S(2)}, u32[]{:S(2)}) collective-permute-start(bf16[128,12,128]{2,0,1:T(8,128)(2,1)S(1)} %get-tuple-element.43), channel_id=1, source_target_pairs={{256,0},{1,256},{257,1},{2,257},{258,2},{3,258},{259,3},{4,259},{2... | collective-permute-start | bytes 1179656 | tf_op jit(solution)/shard_map/ppermute | solution.py:19
  129.1 7.4 %copy-start.7 = (bf16[384,12,128]{2,0,1:T(8,128)(2,1)S(1)}, bf16[384,12,128]{2,0,1:T(8,128)(2,1)}, u32[]{:S(2)}) copy-start(bf16[384,12,128]{2,0,1:T(8,128)(2,1)} %copy-done.6) | copy-start | bytes 3538948
  137.4 31.1 %all-to-all-start.2 = ((bf16[16,24,4,128]{3,1,2,0:T(8,128)(2,1)}), bf16[16,24,4,128]{3,1,2,0:T(8,128)(2,1)S(1)}, u32[]{:S(2)}, u32[]{:S(2)}) async-start(bf16[16,24,4,128]{3,1,2,0:T(8,128)(2,1)} %copy.168), calls=%async_computation.2 | async-start | bytes 786432 | tf_op jit(solution)/shard_map/all_to_all | solution.py:179
  170.6 20.7 %all-to-all-start.3 = ((bf16[384,1,10,128]{3,2,1,0:T(8,128)(2,1)}), bf16[384,1,10,128]{3,2,1,0:T(8,128)(2,1)S(1)}, u32[]{:S(2)}, u32[]{:S(2)}) async-start(bf16[384,1,10,128]{3,2,1,0:T(8,128)(2,1)} %copy.181), calls=%async_computation.3 | async-start | bytes 3145728 | tf_op jit(solution)/shard_map/all_to_all | solution.py:184
  191.6 2.0 %copy-start.1 = (s32[40,768,5]{1,0,2:T(8,128)S(1)}, s32[40,768,5]{1,0,2:T(8,128)}, u32[]{:S(2)}) copy-start(s32[40,768,5]{1,0,2:T(8,128)} %param.15) | copy-start | bytes 1843204

commit v8 on v7

--- a/solution.py
+++ b/solution.py
@@ -173,7 +173,6 @@
 
     line_out = run(line_rows, line_ext, lo, temporal_slot)
     back = jnp.transpose(line_out.reshape(piece, frames, lines_per_group, width), (1, 0, 2, 3))
-    back, space_ext = lax.optimization_barrier((back, space_ext))
     space_out = run(space_part, space_ext, hi, spatial_slot)
 
     returned = lax.all_to_all(back, "frame", split_axis=0, concat_axis=0, tiled=True)

time: 196 us -> 197 us (level)
  starting transfers between devices: 68.7 us -> 54.5 us
  waiting for transfers between devices: 82.1 us -> 90.4 us
  local copies, waits for them, and re-layouts: 29.3 us -> 36.4 us
    all_to_all x1, starting transfers between devices: 18.1 us -> 3.73 us  [shards(): lax.all_to_all(back, 'frame', split_axis=0, concat_axis=0, tiled=True)]
    ppermute x2, starting transfers between devices: 3.94 us -> 11 us  [with_halo(): lower = lax.ppermute(cells[-width:], axes, pairs)]
    ppermute x2, starting transfers between devices: 21.7 us -> 15 us  [with_halo(): upper = lax.ppermute(cells[:width], axes, [(b, a) for a, b in pairs])]
    ppermute x2, waiting for transfers between devices: 12 us -> 16.7 us  [with_halo(): lower = lax.ppermute(cells[-width:], axes, pairs)]
    all_to_all x1, waiting for transfers between devices: 17.1 us -> 20.5 us  [shards(): lax.all_to_all(frame_outputs.reshape(rows, 1, per_group, width), 'x', spl...]
    unnamed x39 -> x41, local copies, waits for them, and re-layouts: 4.15 us -> 7.26 us
  transfers between devices with their start and end apart: 8 -> 8, of which waited for: 7 -> 6; matrix products, arithmetic and copies ran while one was open for 12% -> 14% of each run, Pallas kernels for 0% -> 0%
where the time goes in v8:
time: 197 us; the launch traced here: 196 us
  waiting for transfers between devices  90.4 us (46%)
  starting transfers between devices  54.5 us (28%)
  local copies, waits for them, and re-layouts  36.4 us (18%)
  other arithmetic  7.37 us (4%)
  matrix products  6.4 us (3%)
    all_to_all x1, waiting for transfers between devices, shards(): lax.all_to_all(jnp.transpose(pieces, (1, 0, 2, 3, 4)).reshape(frames, pie...  24 us
    all_to_all x1, waiting for transfers between devices, shards(): lax.all_to_all(frame_outputs.reshape(rows, 1, per_group, width), 'x', spl...  20.5 us
    all_to_all x1, waiting for transfers between devices, shards(): lax.all_to_all(stacked, 'x', split_axis=1, concat_axis=0, tiled=True)  19.3 us
    ppermute x2, waiting for transfers between devices, with_halo(): lower = lax.ppermute(cells[-width:], axes, pairs)  16.7 us
    all_to_all x1, starting transfers between devices, shards(): lax.all_to_all(jnp.transpose(pieces, (1, 0, 2, 3, 4)).reshape(frames, pie...  16.4 us
    ppermute x2, starting transfers between devices, with_halo(): upper = lax.ppermute(cells[:width], axes, [(b, a) for a, b in pairs])  15 us
    ppermute x2, starting transfers between devices, with_halo(): lower = lax.ppermute(cells[-width:], axes, pairs)  11 us
    all_to_all x1, waiting for transfers between devices, shards(): lax.all_to_all(back, 'frame', split_axis=0, concat_axis=0, tiled=True)  7.57 us
  transfers between devices with their start and end apart: 8, of which 6 were waited for; matrix products, arithmetic and copies ran while one was open for 14% of the time, Pallas kernels for 0%

profile of v8, /device:TPU:1, one launch (start us, length us, event | category | flops | bytes accessed | tf_op | source)
XLA Modules:
  0.0 195.7 jit_solution(9552787548753667366)
XLA Ops:
  0.0 0.8 broadcast_compare_fusion.2
  0.9 0.7 compare_and_fusion.3
  1.9 1.4 copy.198
  3.3 2.3 %copy.197 = bf16[12,8,40,128]{3,2,1,0:T(8,128)(2,1)} copy(bf16[12,8,40,128]{3,1,2,0:T(8,128)(2,1)} %bitcast.148) | data formatting | bytes 1966080
  5.6 1.1 copy.196
  6.9 2.5 %fusion.18 = bf16[96,120,128]{2,1,0:T(8,128)(2,1)S(1)} fusion(bf16[96,40,128]{2,1,0:T(8,128)(2,1)S(1)} %bitcast.150, bf16[96,40,128]{2,1,0:T(8,128)(2,1)} %bitcast.151, bf16[96,40,128]{2,1,0:T(8,128)(2,1)} %bitcast.152, s32[120]{0:T(128)S(1)} %eq.67), kind=kOutput, calls=%fused_computation.34 | convolution fusion | flops 362756160 | bytes 5898720 | tf_op jit(solution)/shard_map/sh,thd->tsd/dot_general | solution.py:123
  9.4 2.1 %copy.153 = bf16[96,120,128]{2,0,1:T(8,128)(2,1)} copy(bf16[96,120,128]{2,1,0:T(8,128)(2,1)S(1)} %fusion.18) | data formatting | bytes 5898240 | tf_op jit(solution)/shard_map/sh,thd->tsd/transpose | solution.py:123
  11.5 4.8 %all-to-all-start = ((bf16[96,4,30,128]{3,0,2,1:T(8,128)(2,1)}), bf16[96,4,30,128]{3,0,2,1:T(8,128)(2,1)}, u32[]{:S(2)}, u32[]{:S(2)}) async-start(bf16[96,4,30,128]{3,0,2,1:T(8,128)(2,1)} %bitcast.110), calls=%async_computation | async-start | bytes 5898240 | tf_op jit(solution)/shard_map/all_to_all | solution.py:126
  16.5 0.7 gather_fusion.2
  18.0 0.7 gather_fusion
  19.3 0.7 gather_fusion.11
  20.0 0.7 gather_fusion.10
  20.6 0.7 gather_fusion.9
  21.5 2.1 %copy.175 = s32[6,768,5]{2,1,0:T(8,128)} copy(s32[6,768,5]{1,0,2:T(8,128)S(1)} %broadcast_select_fusion) | data formatting | bytes 184320 | tf_op jit(solution)/shard_map/jit(_take)/select_n | solution.py:26
  23.7 1.6 gather_fusion.7
  25.6 1.0 gather_fusion.8
  26.6 19.3 %all-to-all-done = bf16[96,4,30,128]{3,0,2,1:T(8,128)(2,1)} async-done(((bf16[96,4,30,128]{3,0,2,1:T(8,128)(2,1)}), bf16[96,4,30,128]{3,0,2,1:T(8,128)(2,1)}, u32[]{:S(2)}, u32[]{:S(2)}) %all-to-all-start) | async-done | bytes 2949152 | tf_op jit(solution)/shard_map/all_to_all | solution.py:126
  46.0 2.2 %copy.154 = bf16[4,96,1,30,128]{4,1,0,3,2:T(8,128)(2,1)S(1)} copy(bf16[4,96,1,30,128]{4,1,3,0,2:T(8,128)(2,1)} %bitcast.5) | data formatting | bytes 5898240 | tf_op jit(solution)/shard_map/all_to_all | solution.py:126
  48.4 1.6 copy.155
  50.2 16.4 %all-to-all-start.1 = ((bf16[16,24,12,128]{3,1,2,0:T(8,128)(2,1)}), bf16[16,24,12,128]{3,1,2,0:T(8,128)(2,1)S(1)}, u32[]{:S(2)}, u32[]{:S(2)}) async-start(bf16[16,24,12,128]{3,1,2,0:T(8,128)(2,1)} %bitcast.117), calls=%async_computation.1 | async-start | bytes 2359296 | tf_op jit(solution)/shard_map/all_to_all | solution.py:133
  67.0 1.7 copy.162
  68.7 1.4 gather_fusion.5
  70.4 0.9 gather_fusion.6
  71.5 1.1 slice.271
  72.6 24.0 %all-to-all-done.1 = bf16[16,24,12,128]{3,1,2,0:T(8,128)(2,1)S(1)} async-done(((bf16[16,24,12,128]{3,1,2,0:T(8,128)(2,1)}), bf16[16,24,12,128]{3,1,2,0:T(8,128)(2,1)S(1)}, u32[]{:S(2)}, u32[]{:S(2)}) %all-to-all-start.1) | async-done | bytes 1179680 | tf_op jit(solution)/shard_map/all_to_all | solution.py:133
  96.6 0.8 fusion.77
  97.4 1.1 fusion.76
  99.1 9.1 %collective-permute-start.2 = (bf16[128,12,128]{2,0,1:T(8,128)(2,1)}, bf16[128,12,128]{2,0,1:T(8,128)(2,1)S(1)}, u32[]{:S(2)}, u32[]{:S(2)}) collective-permute-start(bf16[128,12,128]{2,0,1:T(8,128)(2,1)} %get-tuple-element.44), channel_id=1, source_target_pairs={{0,256},{256,1},{1,257},{257,2},{2,258},{258,3},{3,259},{259,4},{4... | collective-permute-start | bytes 1179656 | tf_op jit(solution)/shard_map/ppermute | solution.py:18
  108.1 8.3 %collective-permute-start.3 = (bf16[128,12,128]{2,0,1:T(8,128)(2,1)S(1)}, bf16[128,12,128]{2,0,1:T(8,128)(2,1)S(1)}, u32[]{:S(2)}, u32[]{:S(2)}) collective-permute-start(bf16[128,12,128]{2,0,1:T(8,128)(2,1)S(1)} %get-tuple-element.43), channel_id=1, source_target_pairs={{256,0},{1,256},{257,1},{2,257},{258,2},{3,258},{259,3},{4,259},{2... | collective-permute-start | bytes 1179656 | tf_op jit(solution)/shard_map/ppermute | solution.py:19
  116.5 6.6 %collective-permute-start.1 = (bf16[128,8,128]{2,0,1:T(8,128)(2,1)S(1)}, bf16[128,8,128]{2,0,1:T(8,128)(2,1)S(1)}, u32[]{:S(2)}, u32[]{:S(2)}) collective-permute-start(bf16[128,8,128]{2,0,1:T(8,128)(2,1)S(1)} %get-tuple-element.39), channel_id=1, source_target_pairs={{8,0},{16,8},{24,16},{32,24},{40,32},{48,40},{56,48},{4,56},{12,4}... | collective-permute-start | bytes 786440 | tf_op jit(solution)/shard_map/ppermute | solution.py:19
  123.1 1.9 collective-permute-start
  125.2 2.3 %collective-permute-done.1 = bf16[128,8,128]{2,0,1:T(8,128)(2,1)S(1)} collective-permute-done((bf16[128,8,128]{2,0,1:T(8,128)(2,1)S(1)}, bf16[128,8,128]{2,0,1:T(8,128)(2,1)S(1)}, u32[]{:S(2)}, u32[]{:S(2)}) %collective-permute-start.1) | collective-permute-done | bytes 262176 | tf_op jit(solution)/shard_map/ppermute | solution.py:19
  127.4 16.7 %collective-permute-done = bf16[128,8,128]{2,0,1:T(8,128)(2,1)S(1)} collective-permute-done((bf16[128,8,128]{2,0,1:T(8,128)(2,1)S(1)}, bf16[128,8,128]{2,0,1:T(8,128)(2,1)S(1)}, u32[]{:S(2)}, u32[]{:S(2)}) %collective-permute-start) | collective-permute-done | bytes 262176 | tf_op jit(solution)/shard_map/ppermute | solution.py:18
  144.9 0.7 fusion.3
  145.6 1.2 fusion.4
  147.2 0.8 fusion.46
  148.1 0.9 copy.168
  148.9 3.7 %all-to-all-start.2 = ((bf16[16,24,4,128]{3,1,2,0:T(8,128)(2,1)}), bf16[16,24,4,128]{3,1,2,0:T(8,128)(2,1)S(1)}, u32[]{:S(2)}, u32[]{:S(2)}) async-start(bf16[16,24,4,128]{3,1,2,0:T(8,128)(2,1)} %copy.168), calls=%async_computation.2 | async-start | bytes 786432 | tf_op jit(solution)/shard_map/all_to_all | solution.py:178
  154.1 0.6 copy-done.7
  155.0 1.2 fusion
  156.2 1.9 fusion.1
  158.5 1.2 fusion.31
  159.7 7.6 %all-to-all-done.2 = bf16[16,24,4,128]{3,1,2,0:T(8,128)(2,1)S(1)} async-done(((bf16[16,24,4,128]{3,1,2,0:T(8,128)(2,1)}), bf16[16,24,4,128]{3,1,2,0:T(8,128)(2,1)S(1)}, u32[]{:S(2)}, u32[]{:S(2)}) %all-to-all-start.2) | async-done | bytes 393248 | tf_op jit(solution)/shard_map/all_to_all | solution.py:178
  167.4 1.9 copy.181
  169.3 3.6 %all-to-all-start.3 = ((bf16[384,1,10,128]{3,2,1,0:T(8,128)(2,1)}), bf16[384,1,10,128]{3,2,1,0:T(8,128)(2,1)S(1)}, u32[]{:S(2)}, u32[]{:S(2)}) async-start(bf16[384,1,10,128]{3,2,1,0:T(8,128)(2,1)} %copy.181), calls=%async_computation.3 | async-start | bytes 3145728 | tf_op jit(solution)/shard_map/all_to_all | solution.py:183
  173.0 20.5 %all-to-all-done.3 = bf16[384,1,10,128]{3,2,1,0:T(8,128)(2,1)S(1)} async-done(((bf16[384,1,10,128]{3,2,1,0:T(8,128)(2,1)}), bf16[384,1,10,128]{3,2,1,0:T(8,128)(2,1)S(1)}, u32[]{:S(2)}, u32[]{:S(2)}) %all-to-all-start.3) | async-done | bytes 983072 | tf_op jit(solution)/shard_map/all_to_all | solution.py:183
  193.8 0.7 gather_fusion.4
  194.6 1.1 bitcast_select_fusion
  (111 shorter events, 8.3 us)
Async XLA Ops:
  0.0 16.5 %copy-start = (s32[40,768,5]{1,0,2:T(8,128)S(1)}, s32[40,768,5]{1,0,2:T(8,128)}, u32[]{:S(2)}) copy-start(s32[40,768,5]{1,0,2:T(8,128)} %param.15) | copy-start | bytes 1843204
  0.0 5.6 %copy-start.8 = (bf16[96,5120]{1,0:T(8,128)(2,1)S(1)}, bf16[96,5120]{1,0:T(8,128)(2,1)}, u32[]{:S(2)}) copy-start(bf16[96,5120]{1,0:T(8,128)(2,1)} %param.11) | copy-start | bytes 2949124
  11.5 34.5 %all-to-all-start = ((bf16[96,4,30,128]{3,0,2,1:T(8,128)(2,1)}), bf16[96,4,30,128]{3,0,2,1:T(8,128)(2,1)}, u32[]{:S(2)}, u32[]{:S(2)}) async-start(bf16[96,4,30,128]{3,0,2,1:T(8,128)(2,1)} %bitcast.110), calls=%async_computation | async-start | bytes 5898240 | tf_op jit(solution)/shard_map/all_to_all | solution.py:126
  16.5 0.9 copy-start.9
  18.0 1.3 copy-start.2
  18.0 2.0 %copy-start.3 = (f32[40]{0:T(128)S(1)}, f32[40]{0:T(128)}, u32[]{:S(2)}) copy-start(f32[40]{0:T(128)} %param.18) | copy-start | bytes 484
  18.0 2.6 %copy-start.4 = (f32[40]{0:T(128)S(1)}, f32[40]{0:T(128)}, u32[]{:S(2)}) copy-start(f32[40]{0:T(128)} %param.17) | copy-start | bytes 484
  48.2 2.0 %copy-start.5 = (bf16[4,96,1,30,128]{4,1,0,3,2:T(8,128)(2,1)}, bf16[4,96,1,30,128]{4,1,0,3,2:T(8,128)(2,1)S(1)}, u32[]{:S(2)}) copy-start(bf16[4,96,1,30,128]{4,1,0,3,2:T(8,128)(2,1)S(1)} %copy.154) | copy-start | bytes 8847364
  50.2 46.4 %all-to-all-start.1 = ((bf16[16,24,12,128]{3,1,2,0:T(8,128)(2,1)}), bf16[16,24,12,128]{3,1,2,0:T(8,128)(2,1)S(1)}, u32[]{:S(2)}, u32[]{:S(2)}) async-start(bf16[16,24,12,128]{3,1,2,0:T(8,128)(2,1)} %bitcast.117), calls=%async_computation.1 | async-start | bytes 2359296 | tf_op jit(solution)/shard_map/all_to_all | solution.py:133
  99.1 53.6 %collective-permute-start.2 = (bf16[128,12,128]{2,0,1:T(8,128)(2,1)}, bf16[128,12,128]{2,0,1:T(8,128)(2,1)S(1)}, u32[]{:S(2)}, u32[]{:S(2)}) collective-permute-start(bf16[128,12,128]{2,0,1:T(8,128)(2,1)} %get-tuple-element.44), channel_id=1, source_target_pairs={{0,256},{256,1},{1,257},{257,2},{2,258},{258,3},{3,259},{259,4},{4... | collective-permute-start | bytes 1179656 | tf_op jit(solution)/shard_map/ppermute | solution.py:18
  108.1 45.4 %collective-permute-start.3 = (bf16[128,12,128]{2,0,1:T(8,128)(2,1)S(1)}, bf16[128,12,128]{2,0,1:T(8,128)(2,1)S(1)}, u32[]{:S(2)}, u32[]{:S(2)}) collective-permute-start(bf16[128,12,128]{2,0,1:T(8,128)(2,1)S(1)} %get-tuple-element.43), channel_id=1, source_target_pairs={{256,0},{1,256},{257,1},{2,257},{258,2},{3,258},{259,3},{4,259},{2... | collective-permute-start | bytes 1179656 | tf_op jit(solution)/shard_map/ppermute | solution.py:19
  116.5 10.9 %collective-permute-start.1 = (bf16[128,8,128]{2,0,1:T(8,128)(2,1)S(1)}, bf16[128,8,128]{2,0,1:T(8,128)(2,1)S(1)}, u32[]{:S(2)}, u32[]{:S(2)}) collective-permute-start(bf16[128,8,128]{2,0,1:T(8,128)(2,1)S(1)} %get-tuple-element.39), channel_id=1, source_target_pairs={{8,0},{16,8},{24,16},{32,24},{40,32},{48,40},{56,48},{4,56},{12,4}... | collective-permute-start | bytes 786440 | tf_op jit(solution)/shard_map/ppermute | solution.py:19
  123.1 21.0 %collective-permute-start = (bf16[128,8,128]{2,0,1:T(8,128)(2,1)S(1)}, bf16[128,8,128]{2,0,1:T(8,128)(2,1)S(1)}, u32[]{:S(2)}, u32[]{:S(2)}) collective-permute-start(bf16[128,8,128]{2,0,1:T(8,128)(2,1)S(1)} %get-tuple-element.40), channel_id=1, source_target_pairs={{0,8},{8,16},{16,24},{24,32},{32,40},{40,48},{48,56},{56,4},{4,12}... | collective-permute-start | bytes 786440 | tf_op jit(solution)/shard_map/ppermute | solution.py:18
  148.9 18.4 %all-to-all-start.2 = ((bf16[16,24,4,128]{3,1,2,0:T(8,128)(2,1)}), bf16[16,24,4,128]{3,1,2,0:T(8,128)(2,1)S(1)}, u32[]{:S(2)}, u32[]{:S(2)}) async-start(bf16[16,24,4,128]{3,1,2,0:T(8,128)(2,1)} %copy.168), calls=%async_computation.2 | async-start | bytes 786432 | tf_op jit(solution)/shard_map/all_to_all | solution.py:178
  153.6 1.1 copy-start.7
  156.2 2.1 %copy-start.6 = (bf16[384,6,128]{2,0,1:T(8,128)(2,1)S(1)}, bf16[384,6,128]{2,0,1:T(8,128)(2,1)}, u32[]{:S(2)}) copy-start(bf16[384,6,128]{2,0,1:T(8,128)(2,1)} %get-tuple-element.41) | copy-start | bytes 1769476
  169.3 24.2 %all-to-all-start.3 = ((bf16[384,1,10,128]{3,2,1,0:T(8,128)(2,1)}), bf16[384,1,10,128]{3,2,1,0:T(8,128)(2,1)S(1)}, u32[]{:S(2)}, u32[]{:S(2)}) async-start(bf16[384,1,10,128]{3,2,1,0:T(8,128)(2,1)} %copy.181), calls=%async_computation.3 | async-start | bytes 3145728 | tf_op jit(solution)/shard_map/all_to_all | solution.py:183
  193.7 2.0 %copy-start.1 = (s32[40,768,5]{1,0,2:T(8,128)S(1)}, s32[40,768,5]{1,0,2:T(8,128)}, u32[]{:S(2)}) copy-start(s32[40,768,5]{1,0,2:T(8,128)} %param.15) | copy-start | bytes 1843204

commit v9 on v8

--- a/solution.py
+++ b/solution.py
@@ -152,8 +152,9 @@
         for k in range(chunks)
     ]
     along = ("zh", "frame", "quarter")
+    line_ext = with_halo(line_rows[:, lines_per_group:], along, temporal_order)
+    line_ext, space_kv = lax.optimization_barrier((line_ext, space_kv))
     space_ext = with_halo(space_kv, along, spatial_order)
-    line_ext = with_halo(line_rows[:, lines_per_group:], along, temporal_order)
 
     group_heads = lax.dynamic_slice_in_dim(slots, group_index * per_group, per_group)
     logit_scale = (

time: 197 us -> 209 us (1.061); the launches traced: 196 us -> 206 us
  waiting for transfers between devices: 90.4 us -> 99.6 us
  starting transfers between devices: 54.5 us -> 57.8 us
    ppermute x2, waiting for transfers between devices: 2.28 us -> 30 us  [with_halo(): upper = lax.ppermute(cells[:width], axes, [(b, a) for a, b in pairs])]
    ppermute x2, waiting for transfers between devices: 16.7 us -> 3.39 us  [with_halo(): lower = lax.ppermute(cells[-width:], axes, pairs)]
    all_to_all x1, starting transfers between devices: 3.73 us -> 12.8 us  [shards(): lax.all_to_all(back, 'frame', split_axis=0, concat_axis=0, tiled=True)]
    all_to_all x1, waiting for transfers between devices: 19.3 us -> 27.1 us  [shards(): lax.all_to_all(stacked, 'x', split_axis=1, concat_axis=0, tiled=True)]
    all_to_all x1, waiting for transfers between devices: 7.57 us -> 0.01 us  [shards(): lax.all_to_all(back, 'frame', split_axis=0, concat_axis=0, tiled=True)]
    all_to_all x1, waiting for transfers between devices: 24 us -> 18.8 us  [shards(): lax.all_to_all(jnp.transpose(pieces, (1, 0, 2, 3, 4)).reshape(frames, pie...]
    ppermute x2, starting transfers between devices: 15 us -> 11.3 us  [with_halo(): upper = lax.ppermute(cells[:width], axes, [(b, a) for a, b in pairs])]
    unnamed x41, local copies, waits for them, and re-layouts: 7.26 us -> 4.61 us
  transfers between devices with their start and end apart: 8 -> 8, of which waited for: 6 -> 5; matrix products, arithmetic and copies ran while one was open for 14% -> 12% of each run, Pallas kernels for 0% -> 0%
where the time goes in v9:
time: 209 us; the launch traced here: 206 us
  waiting for transfers between devices  99.6 us (48%)
  starting transfers between devices  57.8 us (28%)
  local copies, waits for them, and re-layouts  35.3 us (17%)
  other arithmetic  7.02 us (3%)
  matrix products  5.16 us (2%)
    ppermute x2, waiting for transfers between devices, with_halo(): upper = lax.ppermute(cells[:width], axes, [(b, a) for a, b in pairs])  30 us
    all_to_all x1, waiting for transfers between devices, shards(): lax.all_to_all(stacked, 'x', split_axis=1, concat_axis=0, tiled=True)  27.1 us
    all_to_all x1, waiting for transfers between devices, shards(): lax.all_to_all(frame_outputs.reshape(rows, 1, per_group, width), 'x', spl...  20.2 us
    all_to_all x1, waiting for transfers between devices, shards(): lax.all_to_all(jnp.transpose(pieces, (1, 0, 2, 3, 4)).reshape(frames, pie...  18.8 us
    all_to_all x1, starting transfers between devices, shards(): lax.all_to_all(jnp.transpose(pieces, (1, 0, 2, 3, 4)).reshape(frames, pie...  16.4 us
    all_to_all x1, starting transfers between devices, shards(): lax.all_to_all(back, 'frame', split_axis=0, concat_axis=0, tiled=True)  12.8 us
    ppermute x2, starting transfers between devices, with_halo(): upper = lax.ppermute(cells[:width], axes, [(b, a) for a, b in pairs])  11.3 us
    ppermute x2, starting transfers between devices, with_halo(): lower = lax.ppermute(cells[-width:], axes, pairs)  8.94 us
  transfers between devices with their start and end apart: 8, of which 5 were waited for; matrix products, arithmetic and copies ran while one was open for 12% of the time, Pallas kernels for 0%

profile of v9, /device:TPU:1, one launch (start us, length us, event | category | flops | bytes accessed | tf_op | source)
XLA Modules:
  0.0 205.5 jit_solution(2603996933479420351)
XLA Ops:
  0.0 0.8 broadcast_compare_fusion.2
  0.9 0.7 compare_and_fusion.3
  2.1 1.4 copy.196
  3.9 1.2 fusion.18
  5.1 2.1 %copy.153 = bf16[96,120,128]{2,0,1:T(8,128)(2,1)} copy(bf16[96,120,128]{2,1,0:T(8,128)(2,1)S(1)} %fusion.18) | data formatting | bytes 5898240 | tf_op jit(solution)/shard_map/sh,thd->tsd/transpose | solution.py:123
  7.2 4.8 %all-to-all-start = ((bf16[96,4,30,128]{3,0,2,1:T(8,128)(2,1)}), bf16[96,4,30,128]{3,0,2,1:T(8,128)(2,1)}, u32[]{:S(2)}, u32[]{:S(2)}) async-start(bf16[96,4,30,128]{3,0,2,1:T(8,128)(2,1)} %bitcast.110), calls=%async_computation | async-start | bytes 5898240 | tf_op jit(solution)/shard_map/all_to_all | solution.py:126
  12.2 0.7 gather_fusion
  13.0 0.6 gather_fusion.1
  13.7 0.6 gather_fusion.3
  14.6 27.1 %all-to-all-done = bf16[96,4,30,128]{3,0,2,1:T(8,128)(2,1)} async-done(((bf16[96,4,30,128]{3,0,2,1:T(8,128)(2,1)}), bf16[96,4,30,128]{3,0,2,1:T(8,128)(2,1)}, u32[]{:S(2)}, u32[]{:S(2)}) %all-to-all-start) | async-done | bytes 2949152 | tf_op jit(solution)/shard_map/all_to_all | solution.py:126
  41.7 2.2 %copy.154 = bf16[4,96,1,30,128]{4,1,0,3,2:T(8,128)(2,1)S(1)} copy(bf16[4,96,1,30,128]{4,1,3,0,2:T(8,128)(2,1)} %bitcast.5) | data formatting | bytes 5898240 | tf_op jit(solution)/shard_map/all_to_all | solution.py:126
  44.1 1.5 copy.155
  45.9 16.4 %all-to-all-start.1 = ((bf16[16,24,12,128]{3,1,2,0:T(8,128)(2,1)}), bf16[16,24,12,128]{3,1,2,0:T(8,128)(2,1)S(1)}, u32[]{:S(2)}, u32[]{:S(2)}) async-start(bf16[16,24,12,128]{3,1,2,0:T(8,128)(2,1)} %bitcast.117), calls=%async_computation.1 | async-start | bytes 2359296 | tf_op jit(solution)/shard_map/all_to_all | solution.py:133
  62.3 0.7 gather_fusion.2
  63.1 1.7 copy.162
  64.8 1.4 gather_fusion.5
  66.3 0.9 gather_fusion.6
  67.4 1.0 gather_fusion.8
  68.5 2.2 %copy.175 = s32[6,768,5]{2,1,0:T(8,128)} copy(s32[6,768,5]{1,0,2:T(8,128)S(1)} %broadcast_select_fusion) | data formatting | bytes 184320 | tf_op jit(solution)/shard_map/jit(_take)/select_n | solution.py:26
  70.7 2.4 %gather_fusion.7 = s32[36,5]{1,0:T(8,128)S(1)} fusion(s32[6,768,5]{2,1,0:T(8,128)} %copy.175, s32[36]{0:T(128)S(1)} %reshape.498), kind=kCustom, calls=%fused_computation.10 | custom fusion | bytes 1728 | tf_op jit(solution)/shard_map/jit(take_along_axis)/gather | solution.py:29
  73.4 18.8 %all-to-all-done.1 = bf16[16,24,12,128]{3,1,2,0:T(8,128)(2,1)S(1)} async-done(((bf16[16,24,12,128]{3,1,2,0:T(8,128)(2,1)}), bf16[16,24,12,128]{3,1,2,0:T(8,128)(2,1)S(1)}, u32[]{:S(2)}, u32[]{:S(2)}) %all-to-all-start.1) | async-done | bytes 1179680 | tf_op jit(solution)/shard_map/all_to_all | solution.py:133
  92.3 1.0 copy-done.6
  93.3 1.7 copy.156
  95.0 0.8 fusion.71
  95.9 7.0 %collective-permute-start = (bf16[128,8,128]{2,0,1:T(8,128)(2,1)}, bf16[128,8,128]{2,0,1:T(8,128)(2,1)S(1)}, u32[]{:S(2)}, u32[]{:S(2)}) collective-permute-start(bf16[128,8,128]{2,0,1:T(8,128)(2,1)} %get-tuple-element.56), channel_id=1, source_target_pairs={{0,8},{8,16},{16,24},{24,32},{32,40},{40,48},{48,56},{56,4},{4,12}... | collective-permute-start | bytes 786440 | tf_op jit(solution)/shard_map/ppermute | solution.py:18
  102.9 9.2 %collective-permute-start.1 = (bf16[128,8,128]{2,0,1:T(8,128)(2,1)}, bf16[128,8,128]{2,0,1:T(8,128)(2,1)S(1)}, u32[]{:S(2)}, u32[]{:S(2)}) collective-permute-start(bf16[128,8,128]{2,0,1:T(8,128)(2,1)} %get-tuple-element.57), channel_id=1, source_target_pairs={{8,0},{16,8},{24,16},{32,24},{40,32},{48,40},{56,48},{4,56},{12,4}... | collective-permute-start | bytes 786440 | tf_op jit(solution)/shard_map/ppermute | solution.py:19
  112.2 0.7 gather_fusion.9
  112.9 0.7 gather_fusion.10
  113.6 0.7 gather_fusion.11
  114.5 1.1 slice.245
  115.7 3.4 %collective-permute-done = bf16[128,8,128]{2,0,1:T(8,128)(2,1)S(1)} collective-permute-done((bf16[128,8,128]{2,0,1:T(8,128)(2,1)}, bf16[128,8,128]{2,0,1:T(8,128)(2,1)S(1)}, u32[]{:S(2)}, u32[]{:S(2)}) %collective-permute-start) | collective-permute-done | bytes 262176 | tf_op jit(solution)/shard_map/ppermute | solution.py:18
  119.9 0.7 fusion.3
  120.6 1.2 fusion.4
  122.0 1.9 collective-permute-start.2
  124.2 0.8 fusion.46
  125.1 0.8 copy.168
  125.9 12.8 %all-to-all-start.2 = ((bf16[16,24,4,128]{3,1,2,0:T(8,128)(2,1)}), bf16[16,24,4,128]{3,1,2,0:T(8,128)(2,1)S(1)}, u32[]{:S(2)}, u32[]{:S(2)}) async-start(bf16[16,24,4,128]{3,1,2,0:T(8,128)(2,1)} %copy.168), calls=%async_computation.2 | async-start | bytes 786432 | tf_op jit(solution)/shard_map/all_to_all | solution.py:179
  138.7 2.1 %collective-permute-start.3 = (bf16[128,12,128]{2,0,1:T(8,128)(2,1)S(1)}, bf16[128,12,128]{2,0,1:T(8,128)(2,1)S(1)}, u32[]{:S(2)}, u32[]{:S(2)}) collective-permute-start(bf16[128,12,128]{2,0,1:T(8,128)(2,1)S(1)} %get-tuple-element.52), channel_id=1, source_target_pairs={{256,0},{1,256},{257,1},{2,257},{258,2},{3,258},{259,3},{4,259},{2... | collective-permute-start | bytes 1179656 | tf_op jit(solution)/shard_map/ppermute | solution.py:19
  141.3 0.4 fusion.67
  141.8 30.0 %collective-permute-done.3 = bf16[128,12,128]{2,0,1:T(8,128)(2,1)S(1)} collective-permute-done((bf16[128,12,128]{2,0,1:T(8,128)(2,1)S(1)}, bf16[128,12,128]{2,0,1:T(8,128)(2,1)S(1)}, u32[]{:S(2)}, u32[]{:S(2)}) %collective-permute-start.3) | collective-permute-done | bytes 393248 | tf_op jit(solution)/shard_map/ppermute | solution.py:19
  172.7 1.2 fusion
  173.9 1.9 fusion.1
  176.2 1.2 fusion.31
  177.6 1.9 copy.181
  179.4 3.6 %all-to-all-start.3 = ((bf16[384,1,10,128]{3,2,1,0:T(8,128)(2,1)}), bf16[384,1,10,128]{3,2,1,0:T(8,128)(2,1)S(1)}, u32[]{:S(2)}, u32[]{:S(2)}) async-start(bf16[384,1,10,128]{3,2,1,0:T(8,128)(2,1)} %copy.181), calls=%async_computation.3 | async-start | bytes 3145728 | tf_op jit(solution)/shard_map/all_to_all | solution.py:184
  183.1 20.2 %all-to-all-done.3 = bf16[384,1,10,128]{3,2,1,0:T(8,128)(2,1)S(1)} async-done(((bf16[384,1,10,128]{3,2,1,0:T(8,128)(2,1)}), bf16[384,1,10,128]{3,2,1,0:T(8,128)(2,1)S(1)}, u32[]{:S(2)}, u32[]{:S(2)}) %all-to-all-start.3) | async-done | bytes 983072 | tf_op jit(solution)/shard_map/all_to_all | solution.py:184
  203.6 0.7 gather_fusion.4
  204.4 1.1 bitcast_select_fusion
  (112 shorter events, 6.8 us)
Async XLA Ops:
  0.0 12.1 %copy-start = (s32[40,768,5]{1,0,2:T(8,128)S(1)}, s32[40,768,5]{1,0,2:T(8,128)}, u32[]{:S(2)}) copy-start(s32[40,768,5]{1,0,2:T(8,128)} %param.15) | copy-start | bytes 1843204
  0.0 3.5 %copy-start.7 = (bf16[96,5120]{1,0:T(8,128)(2,1)S(1)}, bf16[96,5120]{1,0:T(8,128)(2,1)}, u32[]{:S(2)}) copy-start(bf16[96,5120]{1,0:T(8,128)(2,1)} %param.12) | copy-start | bytes 2949124
  0.0 3.7 %copy-start.8 = (bf16[96,5120]{1,0:T(8,128)(2,1)S(1)}, bf16[96,5120]{1,0:T(8,128)(2,1)}, u32[]{:S(2)}) copy-start(bf16[96,5120]{1,0:T(8,128)(2,1)} %param.13) | copy-start | bytes 2949124
  7.2 34.5 %all-to-all-start = ((bf16[96,4,30,128]{3,0,2,1:T(8,128)(2,1)}), bf16[96,4,30,128]{3,0,2,1:T(8,128)(2,1)}, u32[]{:S(2)}, u32[]{:S(2)}) async-start(bf16[96,4,30,128]{3,0,2,1:T(8,128)(2,1)} %bitcast.110), calls=%async_computation | async-start | bytes 5898240 | tf_op jit(solution)/shard_map/all_to_all | solution.py:126
  12.1 0.9 copy-start.9
  43.9 1.9 copy-start.5
  45.9 46.4 %all-to-all-start.1 = ((bf16[16,24,12,128]{3,1,2,0:T(8,128)(2,1)}), bf16[16,24,12,128]{3,1,2,0:T(8,128)(2,1)S(1)}, u32[]{:S(2)}, u32[]{:S(2)}) async-start(bf16[16,24,12,128]{3,1,2,0:T(8,128)(2,1)} %bitcast.117), calls=%async_computation.1 | async-start | bytes 2359296 | tf_op jit(solution)/shard_map/all_to_all | solution.py:133
  68.5 43.8 %copy-start.2 = (f32[40]{0:T(128)S(1)}, f32[40]{0:T(128)}, u32[]{:S(2)}) copy-start(f32[40]{0:T(128)} %param.17) | copy-start | bytes 484
  70.7 42.2 %copy-start.3 = (f32[40]{0:T(128)S(1)}, f32[40]{0:T(128)}, u32[]{:S(2)}) copy-start(f32[40]{0:T(128)} %param.18) | copy-start | bytes 484
  70.7 42.9 %copy-start.4 = (f32[40]{0:T(128)S(1)}, f32[40]{0:T(128)}, u32[]{:S(2)}) copy-start(f32[40]{0:T(128)} %param.19) | copy-start | bytes 484
  92.3 1.0 copy-start.6
  95.9 23.3 %collective-permute-start = (bf16[128,8,128]{2,0,1:T(8,128)(2,1)}, bf16[128,8,128]{2,0,1:T(8,128)(2,1)S(1)}, u32[]{:S(2)}, u32[]{:S(2)}) collective-permute-start(bf16[128,8,128]{2,0,1:T(8,128)(2,1)} %get-tuple-element.56), channel_id=1, source_target_pairs={{0,8},{8,16},{16,24},{24,32},{32,40},{40,48},{48,56},{56,4},{4,12}... | collective-permute-start | bytes 786440 | tf_op jit(solution)/shard_map/ppermute | solution.py:18
  102.9 16.2 %collective-permute-start.1 = (bf16[128,8,128]{2,0,1:T(8,128)(2,1)}, bf16[128,8,128]{2,0,1:T(8,128)(2,1)S(1)}, u32[]{:S(2)}, u32[]{:S(2)}) collective-permute-start(bf16[128,8,128]{2,0,1:T(8,128)(2,1)} %get-tuple-element.57), channel_id=1, source_target_pairs={{8,0},{16,8},{24,16},{32,24},{40,32},{48,40},{56,48},{4,56},{12,4}... | collective-permute-start | bytes 786440 | tf_op jit(solution)/shard_map/ppermute | solution.py:19
  122.0 18.9 %collective-permute-start.2 = (bf16[128,12,128]{2,0,1:T(8,128)(2,1)S(1)}, bf16[128,12,128]{2,0,1:T(8,128)(2,1)S(1)}, u32[]{:S(2)}, u32[]{:S(2)}) collective-permute-start(bf16[128,12,128]{2,0,1:T(8,128)(2,1)S(1)} %get-tuple-element.53), channel_id=1, source_target_pairs={{0,256},{256,1},{1,257},{257,2},{2,258},{258,3},{3,259},{259,4},{4... | collective-permute-start | bytes 1179656 | tf_op jit(solution)/shard_map/ppermute | solution.py:18
  125.9 51.5 %all-to-all-start.2 = ((bf16[16,24,4,128]{3,1,2,0:T(8,128)(2,1)}), bf16[16,24,4,128]{3,1,2,0:T(8,128)(2,1)S(1)}, u32[]{:S(2)}, u32[]{:S(2)}) async-start(bf16[16,24,4,128]{3,1,2,0:T(8,128)(2,1)} %copy.168), calls=%async_computation.2 | async-start | bytes 786432 | tf_op jit(solution)/shard_map/all_to_all | solution.py:179
  138.7 33.1 %collective-permute-start.3 = (bf16[128,12,128]{2,0,1:T(8,128)(2,1)S(1)}, bf16[128,12,128]{2,0,1:T(8,128)(2,1)S(1)}, u32[]{:S(2)}, u32[]{:S(2)}) collective-permute-start(bf16[128,12,128]{2,0,1:T(8,128)(2,1)S(1)} %get-tuple-element.52), channel_id=1, source_target_pairs={{256,0},{1,256},{257,1},{2,257},{258,2},{3,258},{259,3},{4,259},{2... | collective-permute-start | bytes 1179656 | tf_op jit(solution)/shard_map/ppermute | solution.py:19
  179.4 23.8 %all-to-all-start.3 = ((bf16[384,1,10,128]{3,2,1,0:T(8,128)(2,1)}), bf16[384,1,10,128]{3,2,1,0:T(8,128)(2,1)S(1)}, u32[]{:S(2)}, u32[]{:S(2)}) async-start(bf16[384,1,10,128]{3,2,1,0:T(8,128)(2,1)} %copy.181), calls=%async_computation.3 | async-start | bytes 3145728 | tf_op jit(solution)/shard_map/all_to_all | solution.py:184
  203.5 2.0 copy-start.1

commit v10 on v8

--- a/solution.py
+++ b/solution.py
@@ -118,12 +118,10 @@
         axis=1,
     )
     picks = (
-        order.reshape(-1)[:, None] == jnp.arange(3 * head_count, dtype=jnp.int32)[None, :]
+        order[:, :, None] == jnp.arange(3 * head_count, dtype=jnp.int32)[None, None, :]
     ).astype(jnp.bfloat16)
-    stacked = jnp.einsum(
-        "sh,thd->tsd", picks, columns, preferred_element_type=jnp.bfloat16
-    ).reshape(tokens_here, groups, 3 * per_group, width)
-    frame_rows = lax.all_to_all(stacked, "x", split_axis=1, concat_axis=0, tiled=True)
+    stacked = jnp.einsum("gsh,thd->gtsd", picks, columns, preferred_element_type=jnp.bfloat16)
+    frame_rows = lax.all_to_all(stacked, "x", split_axis=0, concat_axis=0, tiled=True)
     frame_rows = frame_rows.reshape(rows, 3 * per_group, width)
     line_part = frame_rows[:, : 3 * lines_per_group]
     space_part = frame_rows[:, 3 * lines_per_group :]
@@ -181,13 +179,16 @@
     ).reshape(rows, lines_per_group, width)
     frame_outputs = jnp.concatenate([returned, space_out], axis=1)
     merged = lax.all_to_all(
-        frame_outputs.reshape(rows, 1, per_group, width),
+        frame_outputs.reshape(groups, tokens_here, per_group, width),
         "x",
         split_axis=0,
-        concat_axis=1,
+        concat_axis=0,
         tiled=True,
     )
-    merged = jnp.take(merged.reshape(tokens_here, head_count, width), unslots, axis=1)
+    places = (
+        unslots[:, None] == jnp.arange(head_count, dtype=jnp.int32)[None, :]
+    ).astype(jnp.bfloat16).reshape(head_count, groups, per_group)
+    merged = jnp.einsum("hgs,gtsd->thd", places, merged, preferred_element_type=jnp.bfloat16)
     return merged.reshape(tokens_here, head_count * width)
 
 

time: 197 us -> 190 us (0.964)
  waiting for transfers between devices: 90.4 us -> 84 us
    all_to_all x2, waiting for transfers between devices: 39.9 us -> 33.5 us  [the longest x1 19.3 us: shards(): lax.all_to_all(stacked, 'x', split_axis=0, concat_axis=0, tiled=True)]
    unnamed x41 -> x42, local copies, waits for them, and re-layouts: 7.26 us -> 8.23 us
where the time goes in v10:
time: 190 us; the launch traced here: 189 us
  waiting for transfers between devices  84 us (44%)
  starting transfers between devices  54.5 us (29%)
  local copies, waits for them, and re-layouts  37 us (19%)
  matrix products  7.03 us (4%)
  other arithmetic  6.23 us (3%)
    all_to_all x1, waiting for transfers between devices, shards(): lax.all_to_all(jnp.transpose(pieces, (1, 0, 2, 3, 4)).reshape(frames, pie...  24 us
    all_to_all x1, waiting for transfers between devices, shards(): lax.all_to_all(stacked, 'x', split_axis=0, concat_axis=0, tiled=True)  19.3 us
    ppermute x2, waiting for transfers between devices, with_halo(): lower = lax.ppermute(cells[-width:], axes, pairs)  16.7 us
    all_to_all x1, starting transfers between devices, shards(): lax.all_to_all(jnp.transpose(pieces, (1, 0, 2, 3, 4)).reshape(frames, pie...  16.4 us
    ppermute x2, starting transfers between devices, with_halo(): upper = lax.ppermute(cells[:width], axes, [(b, a) for a, b in pairs])  15 us
    all_to_all x1, waiting for transfers between devices, shards(): lax.all_to_all(frame_outputs.reshape(groups, tokens_here, per_group, widt...  14.2 us
    ppermute x2, starting transfers between devices, with_halo(): lower = lax.ppermute(cells[-width:], axes, pairs)  11.2 us
    unnamed x42, local copies, waits for them, and re-layouts  8.23 us
  transfers between devices with their start and end apart: 8, of which 6 were waited for; matrix products, arithmetic and copies ran while one was open for 14% of the time, Pallas kernels for 0%

profile of v10, /device:TPU:1, one launch (start us, length us, event | category | flops | bytes accessed | tf_op | source)
XLA Modules:
  0.0 189.4 jit_solution(639307485822694599)
XLA Ops:
  0.0 0.8 broadcast_compare_fusion.2
  0.9 0.7 fusion.67
  1.9 1.4 copy.193
  3.2 2.3 %copy.192 = bf16[12,8,40,128]{3,2,1,0:T(8,128)(2,1)} copy(bf16[12,8,40,128]{3,1,2,0:T(8,128)(2,1)} %bitcast.146) | data formatting | bytes 1966080
  5.6 1.1 copy.191
  6.8 2.5 %fusion.17 = bf16[4,96,30,128]{3,2,0,1:T(8,128)(2,1)S(1)} fusion(bf16[96,40,128]{2,1,0:T(8,128)(2,1)S(1)} %bitcast.148, bf16[96,40,128]{2,1,0:T(8,128)(2,1)} %bitcast.149, bf16[96,40,128]{2,1,0:T(8,128)(2,1)} %bitcast.150, s32[4,30]{1,0:T(4,128)S(1)} %concatenate.41), kind=kOutput, calls=%fused_computation.33 | convolution fusion | flops 362756160 | bytes 5898720 | tf_op jit(solution)/shard_map/gsh,thd->gtsd/dot_general | solution.py:123
  9.3 3.5 %copy.149 = bf16[4,96,30,128]{3,1,2,0:T(8,128)(2,1)} copy(bf16[4,96,30,128]{3,2,0,1:T(8,128)(2,1)S(1)} %fusion.17) | data formatting | bytes 5898240 | tf_op jit(solution)/shard_map/gsh,thd->gtsd/transpose | solution.py:123
  12.9 4.8 %all-to-all-start = ((bf16[4,96,30,128]{3,1,2,0:T(8,128)(2,1)}), bf16[4,96,30,128]{3,1,2,0:T(8,128)(2,1)}, u32[]{:S(2)}, u32[]{:S(2)}) async-start(bf16[4,96,30,128]{3,1,2,0:T(8,128)(2,1)} %copy.149), calls=%async_computation | async-start | bytes 5898240 | tf_op jit(solution)/shard_map/all_to_all | solution.py:124
  17.9 0.7 gather_fusion.2
  19.4 0.7 gather_fusion
  20.1 0.6 gather_fusion.1
  20.7 0.7 gather_fusion.10
  21.3 0.7 gather_fusion.9
  22.0 0.7 gather_fusion.8
  22.8 2.1 %copy.171 = s32[6,768,5]{2,1,0:T(8,128)} copy(s32[6,768,5]{1,0,2:T(8,128)S(1)} %broadcast_select_fusion) | data formatting | bytes 184320 | tf_op jit(solution)/shard_map/jit(_take)/select_n | solution.py:26
  25.1 1.6 gather_fusion.6
  27.0 1.0 gather_fusion.7
  28.0 19.3 %all-to-all-done = bf16[4,96,30,128]{3,1,2,0:T(8,128)(2,1)} async-done(((bf16[4,96,30,128]{3,1,2,0:T(8,128)(2,1)}), bf16[4,96,30,128]{3,1,2,0:T(8,128)(2,1)}, u32[]{:S(2)}, u32[]{:S(2)}) %all-to-all-start) | async-done | bytes 2949152 | tf_op jit(solution)/shard_map/all_to_all | solution.py:124
  47.3 2.2 %copy.150 = bf16[4,96,30,128]{3,1,0,2:T(8,128)(2,1)S(1)} copy(bf16[4,96,30,128]{3,1,2,0:T(8,128)(2,1)} %all-to-all-done) | data formatting | bytes 5898240 | tf_op jit(solution)/shard_map/all_to_all | solution.py:124
  49.8 1.6 copy.151
  51.6 16.4 %all-to-all-start.1 = ((bf16[16,24,12,128]{3,1,2,0:T(8,128)(2,1)}), bf16[16,24,12,128]{3,1,2,0:T(8,128)(2,1)S(1)}, u32[]{:S(2)}, u32[]{:S(2)}) async-start(bf16[16,24,12,128]{3,1,2,0:T(8,128)(2,1)} %bitcast.116), calls=%async_computation.1 | async-start | bytes 2359296 | tf_op jit(solution)/shard_map/all_to_all | solution.py:131
  68.4 1.7 copy.158
  70.2 1.4 gather_fusion.4
  71.8 0.9 gather_fusion.5
  72.9 1.1 slice.269
  74.0 24.0 %all-to-all-done.1 = bf16[16,24,12,128]{3,1,2,0:T(8,128)(2,1)S(1)} async-done(((bf16[16,24,12,128]{3,1,2,0:T(8,128)(2,1)}), bf16[16,24,12,128]{3,1,2,0:T(8,128)(2,1)S(1)}, u32[]{:S(2)}, u32[]{:S(2)}) %all-to-all-start.1) | async-done | bytes 1179680 | tf_op jit(solution)/shard_map/all_to_all | solution.py:131
  98.0 0.8 fusion.79
  98.8 1.1 fusion.78
  100.5 9.1 %collective-permute-start.2 = (bf16[128,12,128]{2,0,1:T(8,128)(2,1)}, bf16[128,12,128]{2,0,1:T(8,128)(2,1)S(1)}, u32[]{:S(2)}, u32[]{:S(2)}) collective-permute-start(bf16[128,12,128]{2,0,1:T(8,128)(2,1)} %get-tuple-element.42), channel_id=1, source_target_pairs={{0,256},{256,1},{1,257},{257,2},{2,258},{258,3},{3,259},{259,4},{4... | collective-permute-start | bytes 1179656 | tf_op jit(solution)/shard_map/ppermute | solution.py:18
  109.6 8.3 %collective-permute-start.3 = (bf16[128,12,128]{2,0,1:T(8,128)(2,1)S(1)}, bf16[128,12,128]{2,0,1:T(8,128)(2,1)S(1)}, u32[]{:S(2)}, u32[]{:S(2)}) collective-permute-start(bf16[128,12,128]{2,0,1:T(8,128)(2,1)S(1)} %get-tuple-element.41), channel_id=1, source_target_pairs={{256,0},{1,256},{257,1},{2,257},{258,2},{3,258},{259,3},{4,259},{2... | collective-permute-start | bytes 1179656 | tf_op jit(solution)/shard_map/ppermute | solution.py:19
  117.9 6.6 %collective-permute-start.1 = (bf16[128,8,128]{2,0,1:T(8,128)(2,1)S(1)}, bf16[128,8,128]{2,0,1:T(8,128)(2,1)S(1)}, u32[]{:S(2)}, u32[]{:S(2)}) collective-permute-start(bf16[128,8,128]{2,0,1:T(8,128)(2,1)S(1)} %get-tuple-element.37), channel_id=1, source_target_pairs={{8,0},{16,8},{24,16},{32,24},{40,32},{48,40},{56,48},{4,56},{12,4}... | collective-permute-start | bytes 786440 | tf_op jit(solution)/shard_map/ppermute | solution.py:19
  124.5 2.1 %collective-permute-start = (bf16[128,8,128]{2,0,1:T(8,128)(2,1)S(1)}, bf16[128,8,128]{2,0,1:T(8,128)(2,1)S(1)}, u32[]{:S(2)}, u32[]{:S(2)}) collective-permute-start(bf16[128,8,128]{2,0,1:T(8,128)(2,1)S(1)} %get-tuple-element.38), channel_id=1, source_target_pairs={{0,8},{8,16},{16,24},{24,32},{32,40},{40,48},{48,56},{56,4},{4,12}... | collective-permute-start | bytes 786440 | tf_op jit(solution)/shard_map/ppermute | solution.py:18
  126.7 2.1 %collective-permute-done.1 = bf16[128,8,128]{2,0,1:T(8,128)(2,1)S(1)} collective-permute-done((bf16[128,8,128]{2,0,1:T(8,128)(2,1)S(1)}, bf16[128,8,128]{2,0,1:T(8,128)(2,1)S(1)}, u32[]{:S(2)}, u32[]{:S(2)}) %collective-permute-start.1) | collective-permute-done | bytes 262176 | tf_op jit(solution)/shard_map/ppermute | solution.py:19
  128.8 16.7 %collective-permute-done = bf16[128,8,128]{2,0,1:T(8,128)(2,1)S(1)} collective-permute-done((bf16[128,8,128]{2,0,1:T(8,128)(2,1)S(1)}, bf16[128,8,128]{2,0,1:T(8,128)(2,1)S(1)}, u32[]{:S(2)}, u32[]{:S(2)}) %collective-permute-start) | collective-permute-done | bytes 262176 | tf_op jit(solution)/shard_map/ppermute | solution.py:18
  146.3 0.7 fusion.3
  147.1 1.2 fusion.4
  148.6 0.8 fusion.45
  149.5 0.9 copy.164
  150.4 3.6 %all-to-all-start.2 = ((bf16[16,24,4,128]{3,1,2,0:T(8,128)(2,1)}), bf16[16,24,4,128]{3,1,2,0:T(8,128)(2,1)S(1)}, u32[]{:S(2)}, u32[]{:S(2)}) async-start(bf16[16,24,4,128]{3,1,2,0:T(8,128)(2,1)} %copy.164), calls=%async_computation.2 | async-start | bytes 786432 | tf_op jit(solution)/shard_map/all_to_all | solution.py:176
  156.3 1.2 fusion
  157.5 1.9 fusion.1
  159.8 1.2 fusion.30
  161.0 7.7 %all-to-all-done.2 = bf16[16,24,4,128]{3,1,2,0:T(8,128)(2,1)S(1)} async-done(((bf16[16,24,4,128]{3,1,2,0:T(8,128)(2,1)}), bf16[16,24,4,128]{3,1,2,0:T(8,128)(2,1)S(1)}, u32[]{:S(2)}, u32[]{:S(2)}) %all-to-all-start.2) | async-done | bytes 393248 | tf_op jit(solution)/shard_map/all_to_all | solution.py:176
  168.9 1.0 copy.177
  169.9 3.5 %all-to-all-start.3 = ((bf16[4,96,10,128]{3,1,2,0:T(8,128)(2,1)}), bf16[4,96,10,128]{3,1,2,0:T(8,128)(2,1)S(1)}, u32[]{:S(2)}, u32[]{:S(2)}) async-start(bf16[4,96,10,128]{3,1,2,0:T(8,128)(2,1)} %copy.177), calls=%async_computation.3 | async-start | bytes 1966080 | tf_op jit(solution)/shard_map/all_to_all | solution.py:181
  173.5 14.2 %all-to-all-done.3 = bf16[4,96,10,128]{3,1,2,0:T(8,128)(2,1)S(1)} async-done(((bf16[4,96,10,128]{3,1,2,0:T(8,128)(2,1)}), bf16[4,96,10,128]{3,1,2,0:T(8,128)(2,1)S(1)}, u32[]{:S(2)}, u32[]{:S(2)}) %all-to-all-start.3) | async-done | bytes 983072 | tf_op jit(solution)/shard_map/all_to_all | solution.py:181
  187.7 0.6 fusion.18
  188.3 1.1 copy.230
  (107 shorter events, 7.9 us)
Async XLA Ops:
  0.0 17.9 %copy-start = (s32[40,768,5]{1,0,2:T(8,128)S(1)}, s32[40,768,5]{1,0,2:T(8,128)}, u32[]{:S(2)}) copy-start(s32[40,768,5]{1,0,2:T(8,128)} %param.15) | copy-start | bytes 1843204
  0.0 5.6 %copy-start.8 = (bf16[96,5120]{1,0:T(8,128)(2,1)S(1)}, bf16[96,5120]{1,0:T(8,128)(2,1)}, u32[]{:S(2)}) copy-start(bf16[96,5120]{1,0:T(8,128)(2,1)} %param.11) | copy-start | bytes 2949124
  12.9 34.5 %all-to-all-start = ((bf16[4,96,30,128]{3,1,2,0:T(8,128)(2,1)}), bf16[4,96,30,128]{3,1,2,0:T(8,128)(2,1)}, u32[]{:S(2)}, u32[]{:S(2)}) async-start(bf16[4,96,30,128]{3,1,2,0:T(8,128)(2,1)} %copy.149), calls=%async_computation | async-start | bytes 5898240 | tf_op jit(solution)/shard_map/all_to_all | solution.py:124
  17.9 0.9 copy-start.9
  19.4 1.3 copy-start.2
  19.4 2.0 %copy-start.3 = (f32[40]{0:T(128)S(1)}, f32[40]{0:T(128)}, u32[]{:S(2)}) copy-start(f32[40]{0:T(128)} %param.18) | copy-start | bytes 484
  19.4 2.6 %copy-start.4 = (f32[40]{0:T(128)S(1)}, f32[40]{0:T(128)}, u32[]{:S(2)}) copy-start(f32[40]{0:T(128)} %param.17) | copy-start | bytes 484
  49.6 2.0 %copy-start.5 = (bf16[4,96,30,128]{3,1,0,2:T(8,128)(2,1)}, bf16[4,96,30,128]{3,1,0,2:T(8,128)(2,1)S(1)}, u32[]{:S(2)}) copy-start(bf16[4,96,30,128]{3,1,0,2:T(8,128)(2,1)S(1)} %copy.150) | copy-start | bytes 8847364
  51.6 46.4 %all-to-all-start.1 = ((bf16[16,24,12,128]{3,1,2,0:T(8,128)(2,1)}), bf16[16,24,12,128]{3,1,2,0:T(8,128)(2,1)S(1)}, u32[]{:S(2)}, u32[]{:S(2)}) async-start(bf16[16,24,12,128]{3,1,2,0:T(8,128)(2,1)} %bitcast.116), calls=%async_computation.1 | async-start | bytes 2359296 | tf_op jit(solution)/shard_map/all_to_all | solution.py:131
  100.5 53.4 %collective-permute-start.2 = (bf16[128,12,128]{2,0,1:T(8,128)(2,1)}, bf16[128,12,128]{2,0,1:T(8,128)(2,1)S(1)}, u32[]{:S(2)}, u32[]{:S(2)}) collective-permute-start(bf16[128,12,128]{2,0,1:T(8,128)(2,1)} %get-tuple-element.42), channel_id=1, source_target_pairs={{0,256},{256,1},{1,257},{257,2},{2,258},{258,3},{3,259},{259,4},{4... | collective-permute-start | bytes 1179656 | tf_op jit(solution)/shard_map/ppermute | solution.py:18
  109.6 45.3 %collective-permute-start.3 = (bf16[128,12,128]{2,0,1:T(8,128)(2,1)S(1)}, bf16[128,12,128]{2,0,1:T(8,128)(2,1)S(1)}, u32[]{:S(2)}, u32[]{:S(2)}) collective-permute-start(bf16[128,12,128]{2,0,1:T(8,128)(2,1)S(1)} %get-tuple-element.41), channel_id=1, source_target_pairs={{256,0},{1,256},{257,1},{2,257},{258,2},{3,258},{259,3},{4,259},{2... | collective-permute-start | bytes 1179656 | tf_op jit(solution)/shard_map/ppermute | solution.py:19
  117.9 10.9 %collective-permute-start.1 = (bf16[128,8,128]{2,0,1:T(8,128)(2,1)S(1)}, bf16[128,8,128]{2,0,1:T(8,128)(2,1)S(1)}, u32[]{:S(2)}, u32[]{:S(2)}) collective-permute-start(bf16[128,8,128]{2,0,1:T(8,128)(2,1)S(1)} %get-tuple-element.37), channel_id=1, source_target_pairs={{8,0},{16,8},{24,16},{32,24},{40,32},{48,40},{56,48},{4,56},{12,4}... | collective-permute-start | bytes 786440 | tf_op jit(solution)/shard_map/ppermute | solution.py:19
  124.5 21.0 %collective-permute-start = (bf16[128,8,128]{2,0,1:T(8,128)(2,1)S(1)}, bf16[128,8,128]{2,0,1:T(8,128)(2,1)S(1)}, u32[]{:S(2)}, u32[]{:S(2)}) collective-permute-start(bf16[128,8,128]{2,0,1:T(8,128)(2,1)S(1)} %get-tuple-element.38), channel_id=1, source_target_pairs={{0,8},{8,16},{16,24},{24,32},{32,40},{40,48},{48,56},{56,4},{4,12}... | collective-permute-start | bytes 786440 | tf_op jit(solution)/shard_map/ppermute | solution.py:18
  150.4 18.4 %all-to-all-start.2 = ((bf16[16,24,4,128]{3,1,2,0:T(8,128)(2,1)}), bf16[16,24,4,128]{3,1,2,0:T(8,128)(2,1)S(1)}, u32[]{:S(2)}, u32[]{:S(2)}) async-start(bf16[16,24,4,128]{3,1,2,0:T(8,128)(2,1)} %copy.164), calls=%async_computation.2 | async-start | bytes 786432 | tf_op jit(solution)/shard_map/all_to_all | solution.py:176
  154.9 1.1 copy-start.7
  157.5 2.1 %copy-start.6 = (bf16[384,6,128]{2,0,1:T(8,128)(2,1)S(1)}, bf16[384,6,128]{2,0,1:T(8,128)(2,1)}, u32[]{:S(2)}) copy-start(bf16[384,6,128]{2,0,1:T(8,128)(2,1)} %get-tuple-element.39) | copy-start | bytes 1769476
  168.9 20.5 %copy-start.1 = (s32[40,768,5]{1,0,2:T(8,128)S(1)}, s32[40,768,5]{1,0,2:T(8,128)}, u32[]{:S(2)}) copy-start(s32[40,768,5]{1,0,2:T(8,128)} %param.15) | copy-start | bytes 1843204
  169.9 17.8 %all-to-all-start.3 = ((bf16[4,96,10,128]{3,1,2,0:T(8,128)(2,1)}), bf16[4,96,10,128]{3,1,2,0:T(8,128)(2,1)S(1)}, u32[]{:S(2)}, u32[]{:S(2)}) async-start(bf16[4,96,10,128]{3,1,2,0:T(8,128)(2,1)} %copy.177), calls=%async_computation.3 | async-start | bytes 1966080 | tf_op jit(solution)/shard_map/all_to_all | solution.py:181

commit v11 on v10

--- a/solution.py
+++ b/solution.py
@@ -103,14 +103,13 @@
     )
     slots = jnp.sum(jnp.where(unslots[None, :] == heads[:, None], heads[None, :], 0), axis=1)
 
-    columns = jnp.concatenate(
-        [
-            queries.reshape(tokens_here, head_count, width),
-            key_vectors.reshape(tokens_here, head_count, width),
-            value_vectors.reshape(tokens_here, head_count, width),
-        ],
-        axis=1,
-    )
+    tile_rows = 8
+    tiles = tokens_here // tile_rows
+
+    def tiled(array):
+        return jnp.transpose(array.reshape(tiles, tile_rows, head_count, width), (0, 2, 1, 3))
+
+    columns = jnp.concatenate([tiled(queries), tiled(key_vectors), tiled(value_vectors)], axis=1)
     grid = slots.reshape(groups, per_group)
     lo, hi = slice(0, lines_per_group), slice(lines_per_group, per_group)
     order = jnp.concatenate(
@@ -120,7 +119,9 @@
     picks = (
         order[:, :, None] == jnp.arange(3 * head_count, dtype=jnp.int32)[None, None, :]
     ).astype(jnp.bfloat16)
-    stacked = jnp.einsum("gsh,thd->gtsd", picks, columns, preferred_element_type=jnp.bfloat16)
+    stacked = jnp.einsum(
+        "gsh,ahrd->garsd", picks, columns, preferred_element_type=jnp.bfloat16
+    ).reshape(groups, tokens_here, 3 * per_group, width)
     frame_rows = lax.all_to_all(stacked, "x", split_axis=0, concat_axis=0, tiled=True)
     frame_rows = frame_rows.reshape(rows, 3 * per_group, width)
     line_part = frame_rows[:, : 3 * lines_per_group]

time: 190 us -> 189 us (level)
    reshape x0 -> x1, local copies, waits for them, and re-layouts: none -> 3.53 us  [shards(): stacked = jnp.einsum('gsh,ahrd->garsd', picks, columns, preferred_element...]
    unnamed x42 -> x38, local copies, waits for them, and re-layouts: 8.23 us -> 4.78 us
where the time goes in v11:
time: 189 us; the launch traced here: 188 us
  waiting for transfers between devices  84.1 us (44%)
  starting transfers between devices  54.5 us (29%)
  local copies, waits for them, and re-layouts  36.4 us (19%)
  matrix products  6.74 us (4%)
  other arithmetic  6.17 us (3%)
    all_to_all x1, waiting for transfers between devices, shards(): lax.all_to_all(jnp.transpose(pieces, (1, 0, 2, 3, 4)).reshape(frames, pie...  24 us
    all_to_all x1, waiting for transfers between devices, shards(): lax.all_to_all(stacked, 'x', split_axis=0, concat_axis=0, tiled=True)  19.3 us
    ppermute x2, waiting for transfers between devices, with_halo(): lower = lax.ppermute(cells[-width:], axes, pairs)  16.7 us
    all_to_all x1, starting transfers between devices, shards(): lax.all_to_all(jnp.transpose(pieces, (1, 0, 2, 3, 4)).reshape(frames, pie...  16.4 us
    ppermute x2, starting transfers between devices, with_halo(): upper = lax.ppermute(cells[:width], axes, [(b, a) for a, b in pairs])  15 us
    all_to_all x1, waiting for transfers between devices, shards(): lax.all_to_all(frame_outputs.reshape(groups, tokens_here, per_group, widt...  14.3 us
    ppermute x2, starting transfers between devices, with_halo(): lower = lax.ppermute(cells[-width:], axes, pairs)  11.1 us
    all_to_all x1, waiting for transfers between devices, shards(): lax.all_to_all(back, 'frame', split_axis=0, concat_axis=0, tiled=True)  7.7 us
  transfers between devices with their start and end apart: 8, of which 6 were waited for; matrix products, arithmetic and copies ran while one was open for 14% of the time, Pallas kernels for 0%

profile of v11, /device:TPU:1, one launch (start us, length us, event | category | flops | bytes accessed | tf_op | source)
XLA Modules:
  0.0 188.5 jit_solution(16512094959122541875)
XLA Ops:
  0.0 0.7 broadcast_compare_fusion.2
  0.8 0.7 fusion.66
  1.8 1.4 copy.235
  3.2 2.8 %bitcast_bitcast_fusion = (bf16[12,40,8,128]{3,1,2,0:T(8,128)(2,1)S(1)}, bf16[12,40,8,128]{3,1,2,0:T(8,128)(2,1)}) fusion(bf16[12,8,40,128]{3,1,2,0:T(8,128)(2,1)} %bitcast.163, bf16[12,8,40,128]{3,1,2,0:T(8,128)(2,1)} %bitcast.164), kind=kLoop, calls=%fused_computation.54 | loop fusion | bytes 3932160 | tf_op jit(solution)/shard_map/transpose | solution.py:110
  6.1 2.2 %fusion.6 = bf16[12,8,128,4,30]{2,4,3,1,0:T(8,128)(2,1)S(1)} fusion(bf16[12,40,8,128]{3,1,2,0:T(8,128)(2,1)S(1)} %get-tuple-element.69, bf16[12,40,8,128]{3,1,2,0:T(8,128)(2,1)} %get-tuple-element.70, bf16[12,40,8,128]{3,1,2,0:T(8,128)(2,1)S(1)} %bitcast.162, s32[4,30]{1,0:T(4,128)S(1)} %concatenate.41), kind=kOutput, calls=%fused_computation.22 | convolution fusion | flops 362756160 | bytes 5898720 | tf_op jit(solution)/shard_map/gsh,ahrd->garsd/dot_general | solution.py:122
  8.3 3.5 %copy.149 = bf16[4,96,30,128]{3,1,2,0:T(8,128)(2,1)} copy(bf16[4,96,30,128]{3,2,0,1:T(8,128)(2,1)S(1)} %bitcast.134) | data formatting | bytes 5898240 | tf_op jit(solution)/shard_map/reshape | solution.py:124
  11.9 4.8 %all-to-all-start = ((bf16[4,96,30,128]{3,1,2,0:T(8,128)(2,1)}), bf16[4,96,30,128]{3,1,2,0:T(8,128)(2,1)}, u32[]{:S(2)}, u32[]{:S(2)}) async-start(bf16[4,96,30,128]{3,1,2,0:T(8,128)(2,1)} %copy.149), calls=%async_computation | async-start | bytes 5898240 | tf_op jit(solution)/shard_map/all_to_all | solution.py:125
  16.9 0.7 gather_fusion.2
  17.8 0.6 gather_fusion.3
  18.4 0.7 gather_fusion
  19.1 0.6 gather_fusion.1
  19.7 0.7 gather_fusion.10
  20.4 0.7 gather_fusion.9
  21.0 0.7 gather_fusion.8
  21.9 2.1 %copy.171 = s32[6,768,5]{2,1,0:T(8,128)} copy(s32[6,768,5]{1,0,2:T(8,128)S(1)} %broadcast_select_fusion) | data formatting | bytes 184320 | tf_op jit(solution)/shard_map/jit(_take)/select_n | solution.py:26
  24.1 1.6 gather_fusion.6
  26.0 1.0 gather_fusion.7
  27.1 19.3 %all-to-all-done = bf16[4,96,30,128]{3,1,2,0:T(8,128)(2,1)} async-done(((bf16[4,96,30,128]{3,1,2,0:T(8,128)(2,1)}), bf16[4,96,30,128]{3,1,2,0:T(8,128)(2,1)}, u32[]{:S(2)}, u32[]{:S(2)}) %all-to-all-start) | async-done | bytes 2949152 | tf_op jit(solution)/shard_map/all_to_all | solution.py:125
  46.4 2.2 %copy.150 = bf16[4,96,30,128]{3,1,0,2:T(8,128)(2,1)S(1)} copy(bf16[4,96,30,128]{3,1,2,0:T(8,128)(2,1)} %all-to-all-done) | data formatting | bytes 5898240 | tf_op jit(solution)/shard_map/all_to_all | solution.py:125
  48.8 1.6 copy.151
  50.6 16.4 %all-to-all-start.1 = ((bf16[16,24,12,128]{3,1,2,0:T(8,128)(2,1)}), bf16[16,24,12,128]{3,1,2,0:T(8,128)(2,1)S(1)}, u32[]{:S(2)}, u32[]{:S(2)}) async-start(bf16[16,24,12,128]{3,1,2,0:T(8,128)(2,1)} %bitcast.131), calls=%async_computation.1 | async-start | bytes 2359296 | tf_op jit(solution)/shard_map/all_to_all | solution.py:132
  67.4 1.7 copy.158
  69.2 1.4 gather_fusion.4
  70.8 0.9 gather_fusion.5
  72.0 1.1 slice.269
  73.1 24.0 %all-to-all-done.1 = bf16[16,24,12,128]{3,1,2,0:T(8,128)(2,1)S(1)} async-done(((bf16[16,24,12,128]{3,1,2,0:T(8,128)(2,1)}), bf16[16,24,12,128]{3,1,2,0:T(8,128)(2,1)S(1)}, u32[]{:S(2)}, u32[]{:S(2)}) %all-to-all-start.1) | async-done | bytes 1179680 | tf_op jit(solution)/shard_map/all_to_all | solution.py:132
  97.0 0.8 fusion.78
  97.9 1.1 fusion.77
  99.5 9.0 %collective-permute-start.2 = (bf16[128,12,128]{2,0,1:T(8,128)(2,1)}, bf16[128,12,128]{2,0,1:T(8,128)(2,1)S(1)}, u32[]{:S(2)}, u32[]{:S(2)}) collective-permute-start(bf16[128,12,128]{2,0,1:T(8,128)(2,1)} %get-tuple-element.42), channel_id=1, source_target_pairs={{0,256},{256,1},{1,257},{257,2},{2,258},{258,3},{3,259},{259,4},{4... | collective-permute-start | bytes 1179656 | tf_op jit(solution)/shard_map/ppermute | solution.py:18
  108.6 8.3 %collective-permute-start.3 = (bf16[128,12,128]{2,0,1:T(8,128)(2,1)S(1)}, bf16[128,12,128]{2,0,1:T(8,128)(2,1)S(1)}, u32[]{:S(2)}, u32[]{:S(2)}) collective-permute-start(bf16[128,12,128]{2,0,1:T(8,128)(2,1)S(1)} %get-tuple-element.41), channel_id=1, source_target_pairs={{256,0},{1,256},{257,1},{2,257},{258,2},{3,258},{259,3},{4,259},{2... | collective-permute-start | bytes 1179656 | tf_op jit(solution)/shard_map/ppermute | solution.py:19
  116.9 6.6 %collective-permute-start.1 = (bf16[128,8,128]{2,0,1:T(8,128)(2,1)S(1)}, bf16[128,8,128]{2,0,1:T(8,128)(2,1)S(1)}, u32[]{:S(2)}, u32[]{:S(2)}) collective-permute-start(bf16[128,8,128]{2,0,1:T(8,128)(2,1)S(1)} %get-tuple-element.37), channel_id=1, source_target_pairs={{8,0},{16,8},{24,16},{32,24},{40,32},{48,40},{56,48},{4,56},{12,4}... | collective-permute-start | bytes 786440 | tf_op jit(solution)/shard_map/ppermute | solution.py:19
  123.6 2.1 %collective-permute-start = (bf16[128,8,128]{2,0,1:T(8,128)(2,1)S(1)}, bf16[128,8,128]{2,0,1:T(8,128)(2,1)S(1)}, u32[]{:S(2)}, u32[]{:S(2)}) collective-permute-start(bf16[128,8,128]{2,0,1:T(8,128)(2,1)S(1)} %get-tuple-element.38), channel_id=1, source_target_pairs={{0,8},{8,16},{16,24},{24,32},{32,40},{40,48},{48,56},{56,4},{4,12}... | collective-permute-start | bytes 786440 | tf_op jit(solution)/shard_map/ppermute | solution.py:18
  125.8 2.1 %collective-permute-done.1 = bf16[128,8,128]{2,0,1:T(8,128)(2,1)S(1)} collective-permute-done((bf16[128,8,128]{2,0,1:T(8,128)(2,1)S(1)}, bf16[128,8,128]{2,0,1:T(8,128)(2,1)S(1)}, u32[]{:S(2)}, u32[]{:S(2)}) %collective-permute-start.1) | collective-permute-done | bytes 262176 | tf_op jit(solution)/shard_map/ppermute | solution.py:19
  127.8 16.7 %collective-permute-done = bf16[128,8,128]{2,0,1:T(8,128)(2,1)S(1)} collective-permute-done((bf16[128,8,128]{2,0,1:T(8,128)(2,1)S(1)}, bf16[128,8,128]{2,0,1:T(8,128)(2,1)S(1)}, u32[]{:S(2)}, u32[]{:S(2)}) %collective-permute-start) | collective-permute-done | bytes 262176 | tf_op jit(solution)/shard_map/ppermute | solution.py:18
  145.4 0.7 fusion.3
  146.1 1.2 fusion.4
  147.7 0.8 fusion.44
  148.5 0.9 copy.164
  149.4 3.6 %all-to-all-start.2 = ((bf16[16,24,4,128]{3,1,2,0:T(8,128)(2,1)}), bf16[16,24,4,128]{3,1,2,0:T(8,128)(2,1)S(1)}, u32[]{:S(2)}, u32[]{:S(2)}) async-start(bf16[16,24,4,128]{3,1,2,0:T(8,128)(2,1)} %copy.164), calls=%async_computation.2 | async-start | bytes 786432 | tf_op jit(solution)/shard_map/all_to_all | solution.py:177
  155.3 1.2 fusion
  156.5 1.9 fusion.1
  158.9 1.2 fusion.29
  160.1 7.7 %all-to-all-done.2 = bf16[16,24,4,128]{3,1,2,0:T(8,128)(2,1)S(1)} async-done(((bf16[16,24,4,128]{3,1,2,0:T(8,128)(2,1)}), bf16[16,24,4,128]{3,1,2,0:T(8,128)(2,1)S(1)}, u32[]{:S(2)}, u32[]{:S(2)}) %all-to-all-start.2) | async-done | bytes 393248 | tf_op jit(solution)/shard_map/all_to_all | solution.py:177
  168.0 1.0 copy.177
  169.0 3.5 %all-to-all-start.3 = ((bf16[4,96,10,128]{3,1,2,0:T(8,128)(2,1)}), bf16[4,96,10,128]{3,1,2,0:T(8,128)(2,1)S(1)}, u32[]{:S(2)}, u32[]{:S(2)}) async-start(bf16[4,96,10,128]{3,1,2,0:T(8,128)(2,1)} %copy.177), calls=%async_computation.3 | async-start | bytes 1966080 | tf_op jit(solution)/shard_map/all_to_all | solution.py:182
  172.5 14.3 %all-to-all-done.3 = bf16[4,96,10,128]{3,1,2,0:T(8,128)(2,1)S(1)} async-done(((bf16[4,96,10,128]{3,1,2,0:T(8,128)(2,1)}), bf16[4,96,10,128]{3,1,2,0:T(8,128)(2,1)S(1)}, u32[]{:S(2)}, u32[]{:S(2)}) %all-to-all-start.3) | async-done | bytes 983072 | tf_op jit(solution)/shard_map/all_to_all | solution.py:182
  186.8 0.6 fusion.17
  187.4 1.1 copy.234
  (104 shorter events, 7.4 us)
Async XLA Ops:
  0.0 16.9 %copy-start = (s32[40,768,5]{1,0,2:T(8,128)S(1)}, s32[40,768,5]{1,0,2:T(8,128)}, u32[]{:S(2)}) copy-start(s32[40,768,5]{1,0,2:T(8,128)} %param.15) | copy-start | bytes 1843204
  11.9 34.5 %all-to-all-start = ((bf16[4,96,30,128]{3,1,2,0:T(8,128)(2,1)}), bf16[4,96,30,128]{3,1,2,0:T(8,128)(2,1)}, u32[]{:S(2)}, u32[]{:S(2)}) async-start(bf16[4,96,30,128]{3,1,2,0:T(8,128)(2,1)} %copy.149), calls=%async_computation | async-start | bytes 5898240 | tf_op jit(solution)/shard_map/all_to_all | solution.py:125
  16.9 0.9 copy-start.8
  18.4 1.3 copy-start.2
  18.4 2.0 %copy-start.3 = (f32[40]{0:T(128)S(1)}, f32[40]{0:T(128)}, u32[]{:S(2)}) copy-start(f32[40]{0:T(128)} %param.18) | copy-start | bytes 484
  18.4 2.6 %copy-start.4 = (f32[40]{0:T(128)S(1)}, f32[40]{0:T(128)}, u32[]{:S(2)}) copy-start(f32[40]{0:T(128)} %param.17) | copy-start | bytes 484
  48.6 2.0 %copy-start.5 = (bf16[4,96,30,128]{3,1,0,2:T(8,128)(2,1)}, bf16[4,96,30,128]{3,1,0,2:T(8,128)(2,1)S(1)}, u32[]{:S(2)}) copy-start(bf16[4,96,30,128]{3,1,0,2:T(8,128)(2,1)S(1)} %copy.150) | copy-start | bytes 8847364
  50.6 46.4 %all-to-all-start.1 = ((bf16[16,24,12,128]{3,1,2,0:T(8,128)(2,1)}), bf16[16,24,12,128]{3,1,2,0:T(8,128)(2,1)S(1)}, u32[]{:S(2)}, u32[]{:S(2)}) async-start(bf16[16,24,12,128]{3,1,2,0:T(8,128)(2,1)} %bitcast.131), calls=%async_computation.1 | async-start | bytes 2359296 | tf_op jit(solution)/shard_map/all_to_all | solution.py:132
  99.5 53.5 %collective-permute-start.2 = (bf16[128,12,128]{2,0,1:T(8,128)(2,1)}, bf16[128,12,128]{2,0,1:T(8,128)(2,1)S(1)}, u32[]{:S(2)}, u32[]{:S(2)}) collective-permute-start(bf16[128,12,128]{2,0,1:T(8,128)(2,1)} %get-tuple-element.42), channel_id=1, source_target_pairs={{0,256},{256,1},{1,257},{257,2},{2,258},{258,3},{3,259},{259,4},{4... | collective-permute-start | bytes 1179656 | tf_op jit(solution)/shard_map/ppermute | solution.py:18
  108.6 45.4 %collective-permute-start.3 = (bf16[128,12,128]{2,0,1:T(8,128)(2,1)S(1)}, bf16[128,12,128]{2,0,1:T(8,128)(2,1)S(1)}, u32[]{:S(2)}, u32[]{:S(2)}) collective-permute-start(bf16[128,12,128]{2,0,1:T(8,128)(2,1)S(1)} %get-tuple-element.41), channel_id=1, source_target_pairs={{256,0},{1,256},{257,1},{2,257},{258,2},{3,258},{259,3},{4,259},{2... | collective-permute-start | bytes 1179656 | tf_op jit(solution)/shard_map/ppermute | solution.py:19
  116.9 10.9 %collective-permute-start.1 = (bf16[128,8,128]{2,0,1:T(8,128)(2,1)S(1)}, bf16[128,8,128]{2,0,1:T(8,128)(2,1)S(1)}, u32[]{:S(2)}, u32[]{:S(2)}) collective-permute-start(bf16[128,8,128]{2,0,1:T(8,128)(2,1)S(1)} %get-tuple-element.37), channel_id=1, source_target_pairs={{8,0},{16,8},{24,16},{32,24},{40,32},{48,40},{56,48},{4,56},{12,4}... | collective-permute-start | bytes 786440 | tf_op jit(solution)/shard_map/ppermute | solution.py:19
  123.6 21.0 %collective-permute-start = (bf16[128,8,128]{2,0,1:T(8,128)(2,1)S(1)}, bf16[128,8,128]{2,0,1:T(8,128)(2,1)S(1)}, u32[]{:S(2)}, u32[]{:S(2)}) collective-permute-start(bf16[128,8,128]{2,0,1:T(8,128)(2,1)S(1)} %get-tuple-element.38), channel_id=1, source_target_pairs={{0,8},{8,16},{16,24},{24,32},{32,40},{40,48},{48,56},{56,4},{4,12}... | collective-permute-start | bytes 786440 | tf_op jit(solution)/shard_map/ppermute | solution.py:18
  149.4 18.4 %all-to-all-start.2 = ((bf16[16,24,4,128]{3,1,2,0:T(8,128)(2,1)}), bf16[16,24,4,128]{3,1,2,0:T(8,128)(2,1)S(1)}, u32[]{:S(2)}, u32[]{:S(2)}) async-start(bf16[16,24,4,128]{3,1,2,0:T(8,128)(2,1)} %copy.164), calls=%async_computation.2 | async-start | bytes 786432 | tf_op jit(solution)/shard_map/all_to_all | solution.py:177
  154.0 1.1 copy-start.7
  156.5 2.1 %copy-start.6 = (bf16[384,6,128]{2,0,1:T(8,128)(2,1)S(1)}, bf16[384,6,128]{2,0,1:T(8,128)(2,1)}, u32[]{:S(2)}) copy-start(bf16[384,6,128]{2,0,1:T(8,128)(2,1)} %get-tuple-element.39) | copy-start | bytes 1769476
  167.9 20.5 %copy-start.1 = (s32[40,768,5]{1,0,2:T(8,128)S(1)}, s32[40,768,5]{1,0,2:T(8,128)}, u32[]{:S(2)}) copy-start(s32[40,768,5]{1,0,2:T(8,128)} %param.15) | copy-start | bytes 1843204
  169.0 17.8 %all-to-all-start.3 = ((bf16[4,96,10,128]{3,1,2,0:T(8,128)(2,1)}), bf16[4,96,10,128]{3,1,2,0:T(8,128)(2,1)S(1)}, u32[]{:S(2)}, u32[]{:S(2)}) async-start(bf16[4,96,10,128]{3,1,2,0:T(8,128)(2,1)} %copy.177), calls=%async_computation.3 | async-start | bytes 1966080 | tf_op jit(solution)/shard_map/all_to_all | solution.py:182

commit v12 on v11

--- a/solution.py
+++ b/solution.py
@@ -137,7 +137,6 @@
         tiled=True,
     )
     space_kv = space_part[:, spaces_per_group:]
-    moved, space_kv = lax.optimization_barrier((moved, space_kv))
     line_rows = jnp.transpose(moved, (1, 0, 2, 3)).reshape(rows, 3 * lines_per_group, width)
 
     def linear(half, frame, quarter):

time: 189 us -> 198 us (1.048)
  waiting for transfers between devices: 84.1 us -> 77.4 us
  starting transfers between devices: 54.5 us -> 59.9 us
  other arithmetic: 6.17 us -> 10.2 us
  local copies, waits for them, and re-layouts: 36.4 us -> 39.3 us
  matrix products: 6.74 us -> 8.86 us
    ppermute x2, starting transfers between devices: 15 us -> 34.4 us  [with_halo(): upper = lax.ppermute(cells[:width], axes, [(b, a) for a, b in pairs])]
    ppermute x2, waiting for transfers between devices: 16.7 us -> 26.7 us  [with_halo(): lower = lax.ppermute(cells[-width:], axes, pairs)]
    all_to_all x1, starting transfers between devices: 16.4 us -> 8.79 us  [shards(): lax.all_to_all(jnp.transpose(pieces, (1, 0, 2, 3, 4)).reshape(frames, pie...]
    ppermute x2, starting transfers between devices: 11.1 us -> 4.02 us  [with_halo(): lower = lax.ppermute(cells[-width:], axes, pairs)]
    all_to_all x1, waiting for transfers between devices: 14.3 us -> 9.33 us  [shards(): lax.all_to_all(frame_outputs.reshape(groups, tokens_here, per_group, widt...]
    all_to_all x1, waiting for transfers between devices: 7.7 us -> 3.16 us  [shards(): lax.all_to_all(back, 'frame', split_axis=0, concat_axis=0, tiled=True)]
    unnamed x38 -> x52, local copies, waits for them, and re-layouts: 4.78 us -> 9.28 us
    all_to_all x1, waiting for transfers between devices: 24 us -> 19.7 us  [shards(): lax.all_to_all(jnp.transpose(pieces, (1, 0, 2, 3, 4)).reshape(frames, pie...]
  transfers between devices with their start and end apart: 8 -> 8, of which waited for: 6 -> 7; matrix products, arithmetic and copies ran while one was open for 14% -> 16% of each run, Pallas kernels for 0% -> 0%
where the time goes in v12:
time: 198 us; the launch traced here: 196 us
  waiting for transfers between devices  77.4 us (39%)
  starting transfers between devices  59.9 us (30%)
  local copies, waits for them, and re-layouts  39.3 us (20%)
  other arithmetic  10.2 us (5%)
  matrix products  8.86 us (4%)
    ppermute x2, starting transfers between devices, with_halo(): upper = lax.ppermute(cells[:width], axes, [(b, a) for a, b in pairs])  34.4 us
    ppermute x2, waiting for transfers between devices, with_halo(): lower = lax.ppermute(cells[-width:], axes, pairs)  26.7 us
    all_to_all x1, waiting for transfers between devices, shards(): lax.all_to_all(jnp.transpose(pieces, (1, 0, 2, 3, 4)).reshape(frames, pie...  19.7 us
    all_to_all x1, waiting for transfers between devices, shards(): lax.all_to_all(stacked, 'x', split_axis=0, concat_axis=0, tiled=True)  17.3 us
    all_to_all x1, waiting for transfers between devices, shards(): lax.all_to_all(frame_outputs.reshape(groups, tokens_here, per_group, widt...  9.33 us
    unnamed x52, local copies, waits for them, and re-layouts  9.28 us
    all_to_all x1, starting transfers between devices, shards(): lax.all_to_all(jnp.transpose(pieces, (1, 0, 2, 3, 4)).reshape(frames, pie...  8.79 us
    all_to_all x1, starting transfers between devices, shards(): lax.all_to_all(stacked, 'x', split_axis=0, concat_axis=0, tiled=True)  4.97 us
  transfers between devices with their start and end apart: 8, of which 7 were waited for; matrix products, arithmetic and copies ran while one was open for 16% of the time, Pallas kernels for 0%

profile of v12, /device:TPU:1, one launch (start us, length us, event | category | flops | bytes accessed | tf_op | source)
XLA Modules:
  0.0 196.4 jit_solution(4707698778980261543)
XLA Ops:
  0.0 0.8 broadcast_compare_fusion.2
  2.3 1.4 copy.235
  3.7 1.7 bitcast_bitcast_fusion
  5.5 2.5 %fusion.6 = bf16[12,8,128,4,30]{2,4,3,1,0:T(8,128)(2,1)S(1)} fusion(bf16[12,40,8,128]{3,1,2,0:T(8,128)(2,1)} %get-tuple-element.68, bf16[12,40,8,128]{3,1,2,0:T(8,128)(2,1)} %get-tuple-element.69, bf16[12,40,8,128]{3,1,2,0:T(8,128)(2,1)S(1)} %bitcast.161, s32[4,30]{1,0:T(4,128)S(1)} %concatenate.41), kind=kOutput, calls=%fused_computation.22 | convolution fusion | flops 362756160 | bytes 5898720 | tf_op jit(solution)/shard_map/gsh,ahrd->garsd/dot_general | solution.py:122
  8.1 3.5 %copy.149 = bf16[4,96,30,128]{3,1,2,0:T(8,128)(2,1)} copy(bf16[4,96,30,128]{3,2,0,1:T(8,128)(2,1)S(1)} %bitcast.134) | data formatting | bytes 5898240 | tf_op jit(solution)/shard_map/reshape | solution.py:124
  11.6 5.0 %all-to-all-start = ((bf16[4,96,30,128]{3,1,2,0:T(8,128)(2,1)}), bf16[4,96,30,128]{3,1,2,0:T(8,128)(2,1)}, u32[]{:S(2)}, u32[]{:S(2)}) async-start(bf16[4,96,30,128]{3,1,2,0:T(8,128)(2,1)} %copy.149), calls=%async_computation | async-start | bytes 5898240 | tf_op jit(solution)/shard_map/all_to_all | solution.py:125
  18.7 0.7 gather_fusion.2
  23.1 0.9 gather_fusion.5
  24.1 1.0 gather_fusion.7
  25.7 0.7 gather_fusion.4
  26.9 0.7 copy.171
  27.6 0.9 gather_fusion.6
  28.9 17.3 %all-to-all-done = bf16[4,96,30,128]{3,1,2,0:T(8,128)(2,1)} async-done(((bf16[4,96,30,128]{3,1,2,0:T(8,128)(2,1)}), bf16[4,96,30,128]{3,1,2,0:T(8,128)(2,1)}, u32[]{:S(2)}, u32[]{:S(2)}) %all-to-all-start) | async-done | bytes 2949152 | tf_op jit(solution)/shard_map/all_to_all | solution.py:125
  46.2 2.2 %copy.150 = bf16[4,96,30,128]{3,1,0,2:T(8,128)(2,1)S(1)} copy(bf16[4,96,30,128]{3,1,2,0:T(8,128)(2,1)} %all-to-all-done) | data formatting | bytes 5898240 | tf_op jit(solution)/shard_map/all_to_all | solution.py:125
  48.4 1.0 fusion.80
  49.4 17.9 %collective-permute-start.3 = (bf16[128,12,128]{2,0,1:T(8,128)(2,1)}, bf16[128,12,128]{2,0,1:T(8,128)(2,1)S(1)}, u32[]{:S(2)}, u32[]{:S(2)}) collective-permute-start(bf16[128,12,128]{2,0,1:T(8,128)(2,1)} %get-tuple-element.25), channel_id=1, source_target_pairs={{256,0},{1,256},{257,1},{2,257},{258,2},{3,258},{259,3},{4,259},{2... | collective-permute-start | bytes 1179656 | tf_op jit(solution)/shard_map/ppermute | solution.py:19
  67.3 1.9 collective-permute-start.2
  69.3 1.2 fusion.78
  70.5 1.3 copy.151
  71.7 8.8 %all-to-all-start.1 = ((bf16[16,24,12,128]{3,1,2,0:T(8,128)(2,1)}), bf16[16,24,12,128]{3,1,2,0:T(8,128)(2,1)}, u32[]{:S(2)}, u32[]{:S(2)}) async-start(bf16[16,24,12,128]{3,1,2,0:T(8,128)(2,1)} %bitcast.131), calls=%async_computation.1 | async-start | bytes 2359296 | tf_op jit(solution)/shard_map/all_to_all | solution.py:132
  80.5 0.9 fusion.79
  81.5 15.4 %collective-permute-done.2 = bf16[128,12,128]{2,0,1:T(8,128)(2,1)} collective-permute-done((bf16[128,12,128]{2,0,1:T(8,128)(2,1)}, bf16[128,12,128]{2,0,1:T(8,128)(2,1)}, u32[]{:S(2)}, u32[]{:S(2)}) %collective-permute-start.2) | collective-permute-done | bytes 393248 | tf_op jit(solution)/shard_map/ppermute | solution.py:18
  96.9 3.4 %fusion.51 = (bf16[384,6,128]{2,0,1:T(8,128)(2,1)S(1)}, bf16[384,6,128]{2,0,1:T(8,128)(2,1)}, bf16[384,6,128]{2,0,1:T(8,128)(2,1)S(1)}, bf16[384,6,128]{2,0,1:T(...) fusion(bf16[384,12,128]{2,0,1:T(8,128)(2,1)S(1)} %copy-done.5, ...), kind=kLoop, calls=%fused_computation.72 | loop fusion | flops 9437184 | bytes 6684672 | tf_op jit(solution)/shard_map/concatenate | solution.py:20
  100.9 1.6 copy-done.10
  102.5 1.2 fusion
  103.7 1.9 fusion.1
  106.2 19.7 %all-to-all-done.1 = bf16[16,24,12,128]{3,1,2,0:T(8,128)(2,1)} async-done(((bf16[16,24,12,128]{3,1,2,0:T(8,128)(2,1)}), bf16[16,24,12,128]{3,1,2,0:T(8,128)(2,1)}, u32[]{:S(2)}, u32[]{:S(2)}) %all-to-all-start.1) | async-done | bytes 1179680 | tf_op jit(solution)/shard_map/all_to_all | solution.py:132
  126.0 1.7 copy.152
  127.8 16.5 %collective-permute-start.1 = (bf16[128,8,128]{2,0,1:T(8,128)(2,1)S(1)}, bf16[128,8,128]{2,0,1:T(8,128)(2,1)S(1)}, u32[]{:S(2)}, u32[]{:S(2)}) collective-permute-start(bf16[128,8,128]{2,0,1:T(8,128)(2,1)S(1)} %get-tuple-element.38), channel_id=1, source_target_pairs={{8,0},{16,8},{24,16},{32,24},{40,32},{48,40},{56,48},{4,56},{12,4}... | collective-permute-start | bytes 786440 | tf_op jit(solution)/shard_map/ppermute | solution.py:19
  144.3 2.1 %collective-permute-start = (bf16[128,8,128]{2,0,1:T(8,128)(2,1)S(1)}, bf16[128,8,128]{2,0,1:T(8,128)(2,1)S(1)}, u32[]{:S(2)}, u32[]{:S(2)}) collective-permute-start(bf16[128,8,128]{2,0,1:T(8,128)(2,1)S(1)} %get-tuple-element.39), channel_id=1, source_target_pairs={{0,8},{8,16},{16,24},{24,32},{32,40},{40,48},{48,56},{56,4},{4,12}... | collective-permute-start | bytes 786440 | tf_op jit(solution)/shard_map/ppermute | solution.py:18
  146.5 1.1 collective-permute-done.1
  147.6 11.3 %collective-permute-done = bf16[128,8,128]{2,0,1:T(8,128)(2,1)S(1)} collective-permute-done((bf16[128,8,128]{2,0,1:T(8,128)(2,1)S(1)}, bf16[128,8,128]{2,0,1:T(8,128)(2,1)S(1)}, u32[]{:S(2)}, u32[]{:S(2)}) %collective-permute-start) | collective-permute-done | bytes 262176 | tf_op jit(solution)/shard_map/ppermute | solution.py:18
  159.6 0.7 fusion.3
  160.4 1.2 fusion.4
  162.0 0.8 fusion.44
  162.8 0.9 copy.164
  163.7 4.2 %all-to-all-start.2 = ((bf16[16,24,4,128]{3,1,2,0:T(8,128)(2,1)}), bf16[16,24,4,128]{3,1,2,0:T(8,128)(2,1)}, u32[]{:S(2)}, u32[]{:S(2)}) async-start(bf16[16,24,4,128]{3,1,2,0:T(8,128)(2,1)} %copy.164), calls=%async_computation.2 | async-start | bytes 786432 | tf_op jit(solution)/shard_map/all_to_all | solution.py:176
  167.9 1.9 constant_dynamic-update-slice_fusion.12
  169.9 0.7 copy.175
  170.6 1.9 constant_dynamic-update-slice_fusion.11
  172.5 0.9 constant_dynamic-update-slice_fusion.10
  173.4 3.0 %fusion.29 = bf16[6,64,6,128]{3,1,2,0:T(8,128)(2,1)S(1)} fusion(bf16[6,6,64,5,64]{2,4,3,1,0:T(8,128)(2,1)S(1)} %get-tuple-element.17, bf16[6,5,64,6,128]{4,2,0,3,1:T(8,128)(2,1)} %constant_dynamic-update-slice_fusion.10, f32[6,64,6]{1,2,0:T(8,128)S(1)} %copy.175), kind=kOutput, calls=%fused_computation.55 | convolution fusion | flops 189333504 | bytes 5022720 | tf_op jit(solution)/shard_map/hbqok,bokhd->bqhd/dot_general | solution.py:52
  176.5 3.2 %all-to-all-done.2 = bf16[16,24,4,128]{3,1,2,0:T(8,128)(2,1)} async-done(((bf16[16,24,4,128]{3,1,2,0:T(8,128)(2,1)}), bf16[16,24,4,128]{3,1,2,0:T(8,128)(2,1)}, u32[]{:S(2)}, u32[]{:S(2)}) %all-to-all-start.2) | async-done | bytes 393248 | tf_op jit(solution)/shard_map/all_to_all | solution.py:176
  179.6 1.0 copy.165
  180.8 1.0 copy.177
  181.8 3.5 %all-to-all-start.3 = ((bf16[4,96,10,128]{3,1,2,0:T(8,128)(2,1)}), bf16[4,96,10,128]{3,1,2,0:T(8,128)(2,1)S(1)}, u32[]{:S(2)}, u32[]{:S(2)}) async-start(bf16[4,96,10,128]{3,1,2,0:T(8,128)(2,1)} %copy.177), calls=%async_computation.3 | async-start | bytes 1966080 | tf_op jit(solution)/shard_map/all_to_all | solution.py:181
  185.3 9.3 %all-to-all-done.3 = bf16[4,96,10,128]{3,1,2,0:T(8,128)(2,1)S(1)} async-done(((bf16[4,96,10,128]{3,1,2,0:T(8,128)(2,1)}), bf16[4,96,10,128]{3,1,2,0:T(8,128)(2,1)S(1)}, u32[]{:S(2)}, u32[]{:S(2)}) %all-to-all-start.3) | async-done | bytes 983072 | tf_op jit(solution)/shard_map/all_to_all | solution.py:181
  195.3 1.1 copy.234
  (115 shorter events, 11.9 us)
Async XLA Ops:
  0.0 18.0 %copy-start = (s32[40,768,5]{1,0,2:T(8,128)S(1)}, s32[40,768,5]{1,0,2:T(8,128)}, u32[]{:S(2)}) copy-start(s32[40,768,5]{1,0,2:T(8,128)} %param.15) | copy-start | bytes 1843204
  0.0 3.7 %copy-start.6 = (bf16[96,5120]{1,0:T(8,128)(2,1)S(1)}, bf16[96,5120]{1,0:T(8,128)(2,1)}, u32[]{:S(2)}) copy-start(bf16[96,5120]{1,0:T(8,128)(2,1)} %param.13) | copy-start | bytes 2949124
  1.6 0.5 copy-start.14
  2.2 1.5 copy-start.7
  11.6 5.2 %copy-start.8 = (s32[40,768]{1,0:T(8,128)S(1)}, s32[40,768]{1,0:T(8,128)}, u32[]{:S(2)}) copy-start(s32[40,768]{1,0:T(8,128)} %param.16) | copy-start | bytes 368644
  11.6 34.6 %all-to-all-start = ((bf16[4,96,30,128]{3,1,2,0:T(8,128)(2,1)}), bf16[4,96,30,128]{3,1,2,0:T(8,128)(2,1)}, u32[]{:S(2)}, u32[]{:S(2)}) async-start(bf16[4,96,30,128]{3,1,2,0:T(8,128)(2,1)} %copy.149), calls=%async_computation | async-start | bytes 5898240 | tf_op jit(solution)/shard_map/all_to_all | solution.py:125
  18.7 1.0 copy-start.2
  18.7 1.6 copy-start.3
  18.7 2.3 %copy-start.4 = (f32[40]{0:T(128)S(1)}, f32[40]{0:T(128)}, u32[]{:S(2)}) copy-start(f32[40]{0:T(128)} %param.17) | copy-start | bytes 484
  21.7 3.4 %copy-start.12 = (f32[10]{0:T(128)}, f32[10]{0:T(128)S(1)}, u32[]{:S(2)}) copy-start(f32[10]{0:T(128)S(1)} %get-tuple-element.62) | copy-start | bytes 124
  49.4 32.1 %collective-permute-start.3 = (bf16[128,12,128]{2,0,1:T(8,128)(2,1)}, bf16[128,12,128]{2,0,1:T(8,128)(2,1)S(1)}, u32[]{:S(2)}, u32[]{:S(2)}) collective-permute-start(bf16[128,12,128]{2,0,1:T(8,128)(2,1)} %get-tuple-element.25), channel_id=1, source_target_pairs={{256,0},{1,256},{257,1},{2,257},{258,2},{3,258},{259,3},{4,259},{2... | collective-permute-start | bytes 1179656 | tf_op jit(solution)/shard_map/ppermute | solution.py:19
  67.3 29.6 %collective-permute-start.2 = (bf16[128,12,128]{2,0,1:T(8,128)(2,1)}, bf16[128,12,128]{2,0,1:T(8,128)(2,1)}, u32[]{:S(2)}, u32[]{:S(2)}) collective-permute-start(bf16[128,12,128]{2,0,1:T(8,128)(2,1)} %get-tuple-element.26), channel_id=1, source_target_pairs={{0,256},{256,1},{1,257},{257,2},{2,258},{258,3},{3,259},{259,4},{4... | collective-permute-start | bytes 1179656 | tf_op jit(solution)/shard_map/ppermute | solution.py:18
  71.7 54.3 %all-to-all-start.1 = ((bf16[16,24,12,128]{3,1,2,0:T(8,128)(2,1)}), bf16[16,24,12,128]{3,1,2,0:T(8,128)(2,1)}, u32[]{:S(2)}, u32[]{:S(2)}) async-start(bf16[16,24,12,128]{3,1,2,0:T(8,128)(2,1)} %bitcast.131), calls=%async_computation.1 | async-start | bytes 2359296 | tf_op jit(solution)/shard_map/all_to_all | solution.py:132
  80.5 16.4 %copy-start.5 = (bf16[384,12,128]{2,0,1:T(8,128)(2,1)S(1)}, bf16[384,12,128]{2,0,1:T(8,128)(2,1)}, u32[]{:S(2)}) copy-start(bf16[384,12,128]{2,0,1:T(8,128)(2,1)} %get-tuple-element.21) | copy-start | bytes 3538948
  81.5 15.4 %copy-start.9 = (bf16[128,12,128]{2,0,1:T(8,128)(2,1)}, bf16[128,12,128]{2,0,1:T(8,128)(2,1)S(1)}, u32[]{:S(2)}) copy-start(bf16[128,12,128]{2,0,1:T(8,128)(2,1)S(1)} %collective-permute-done.3) | copy-start | bytes 1179652
  100.6 1.9 copy-start.11
  100.9 1.6 copy-start.10
  103.6 1.9 copy-start.16
  127.8 19.8 %collective-permute-start.1 = (bf16[128,8,128]{2,0,1:T(8,128)(2,1)S(1)}, bf16[128,8,128]{2,0,1:T(8,128)(2,1)S(1)}, u32[]{:S(2)}, u32[]{:S(2)}) collective-permute-start(bf16[128,8,128]{2,0,1:T(8,128)(2,1)S(1)} %get-tuple-element.38), channel_id=1, source_target_pairs={{8,0},{16,8},{24,16},{32,24},{40,32},{48,40},{56,48},{4,56},{12,4}... | collective-permute-start | bytes 786440 | tf_op jit(solution)/shard_map/ppermute | solution.py:19
  144.3 14.6 %collective-permute-start = (bf16[128,8,128]{2,0,1:T(8,128)(2,1)S(1)}, bf16[128,8,128]{2,0,1:T(8,128)(2,1)S(1)}, u32[]{:S(2)}, u32[]{:S(2)}) collective-permute-start(bf16[128,8,128]{2,0,1:T(8,128)(2,1)S(1)} %get-tuple-element.39), channel_id=1, source_target_pairs={{0,8},{8,16},{16,24},{24,32},{32,40},{40,48},{48,56},{56,4},{4,12}... | collective-permute-start | bytes 786440 | tf_op jit(solution)/shard_map/ppermute | solution.py:18
  160.4 1.2 copy-start.13
  163.7 15.9 %all-to-all-start.2 = ((bf16[16,24,4,128]{3,1,2,0:T(8,128)(2,1)}), bf16[16,24,4,128]{3,1,2,0:T(8,128)(2,1)}, u32[]{:S(2)}, u32[]{:S(2)}) async-start(bf16[16,24,4,128]{3,1,2,0:T(8,128)(2,1)} %copy.164), calls=%async_computation.2 | async-start | bytes 786432 | tf_op jit(solution)/shard_map/all_to_all | solution.py:176
  180.8 13.9 %copy-start.15 = (s32[40]{0:T(128)S(1)}, s32[40]{0:T(128)}, u32[]{:S(2)}) copy-start(s32[40]{0:T(128)} %copy-done.14) | copy-start | bytes 484
  181.8 12.9 %all-to-all-start.3 = ((bf16[4,96,10,128]{3,1,2,0:T(8,128)(2,1)}), bf16[4,96,10,128]{3,1,2,0:T(8,128)(2,1)S(1)}, u32[]{:S(2)}, u32[]{:S(2)}) async-start(bf16[4,96,10,128]{3,1,2,0:T(8,128)(2,1)} %copy.177), calls=%async_computation.3 | async-start | bytes 1966080 | tf_op jit(solution)/shard_map/all_to_all | solution.py:181
  185.3 11.0 %copy-start.1 = (s32[40,768,5]{1,0,2:T(8,128)S(1)}, s32[40,768,5]{1,0,2:T(8,128)}, u32[]{:S(2)}) copy-start(s32[40,768,5]{1,0,2:T(8,128)} %param.15) | copy-start | bytes 1843204

commit v13 on v11

--- a/solution.py
+++ b/solution.py
@@ -41,16 +41,24 @@
     q = query_rows.reshape(blocks, BLOCK, heads, width)
     kb = key_ext.reshape(blocks + 2 * MARGIN, BLOCK, heads, width)
     vb = value_ext.reshape(blocks + 2 * MARGIN, BLOCK, heads, width)
-    kw = jnp.stack([kb[o : o + blocks] for o in range(span)], axis=1)
-    vw = jnp.stack([vb[o : o + blocks] for o in range(span)], axis=1)
-    logits = jnp.einsum("bqhd,bokhd->hbqok", q, kw, preferred_element_type=jnp.float32)
+    logits = jnp.stack(
+        [
+            jnp.einsum("bqhd,bkhd->hbqk", q, kb[o : o + blocks], preferred_element_type=jnp.float32)
+            for o in range(span)
+        ],
+        axis=3,
+    )
     logits = logits * logit_scale[:, None, None, None, None]
     logits = jnp.where(allowed[:, :, None, :, None], logits, -jnp.inf)
     peak = jnp.max(logits, axis=(3, 4), keepdims=True)
     weight = jnp.exp(logits - peak)
     total = jnp.sum(weight, axis=(3, 4))
-    mixed = jnp.einsum(
-        "hbqok,bokhd->bqhd", weight.astype(jnp.bfloat16), vw, preferred_element_type=jnp.float32
+    weight_b = weight.astype(jnp.bfloat16)
+    mixed = sum(
+        jnp.einsum(
+            "hbqk,bkhd->bqhd", weight_b[:, :, :, o], vb[o : o + blocks], preferred_element_type=jnp.float32
+        )
+        for o in range(span)
     )
     factor = value_factor[:, None, None] / total
     out = mixed * jnp.transpose(factor, (1, 2, 0))[:, :, :, None]

time: 189 us -> 196 us (1.037)
  the two profiles are of different devices: /device:TPU:1 before, /device:TPU:120 now
where the time goes in v13:
time: 196 us; the launch traced here: 195 us
  waiting for transfers between devices  96.7 us (49%)
  starting transfers between devices  47.6 us (24%)
  local copies, waits for them, and re-layouts  32.3 us (16%)
  matrix products  10.4 us (5%)
  other arithmetic  7.76 us (4%)
    all_to_all x1, waiting for transfers between devices, shards(): lax.all_to_all(jnp.transpose(pieces, (1, 0, 2, 3, 4)).reshape(frames, pie...  30.3 us
    all_to_all x1, waiting for transfers between devices, shards(): lax.all_to_all(stacked, 'x', split_axis=0, concat_axis=0, tiled=True)  25 us
    ppermute x2, waiting for transfers between devices, with_halo(): lower = lax.ppermute(cells[-width:], axes, pairs)  16.9 us
    all_to_all x1, waiting for transfers between devices, shards(): lax.all_to_all(frame_outputs.reshape(groups, tokens_here, per_group, widt...  14.9 us
    ppermute x2, starting transfers between devices, with_halo(): lower = lax.ppermute(cells[-width:], axes, pairs)  14.2 us
    all_to_all x1, starting transfers between devices, shards(): lax.all_to_all(jnp.transpose(pieces, (1, 0, 2, 3, 4)).reshape(frames, pie...  10.5 us
    all_to_all x1, starting transfers between devices, shards(): lax.all_to_all(back, 'frame', split_axis=0, concat_axis=0, tiled=True)  10.3 us
    ppermute x2, waiting for transfers between devices, with_halo(): upper = lax.ppermute(cells[:width], axes, [(b, a) for a, b in pairs])  9.54 us
  transfers between devices with their start and end apart: 8, of which 6 were waited for; matrix products, arithmetic and copies ran while one was open for 15% of the time, Pallas kernels for 0%

profile of v13, /device:TPU:120, one launch (start us, length us, event | category | flops | bytes accessed | tf_op | source)
XLA Modules:
  0.0 195.3 jit_solution(6652630075381284641)
XLA Ops:
  0.0 0.7 broadcast_compare_fusion.2
  0.8 0.7 fusion.69
  1.8 1.4 copy.307
  3.2 2.8 %bitcast_bitcast_fusion = (bf16[12,40,8,128]{3,1,2,0:T(8,128)(2,1)S(1)}, bf16[12,40,8,128]{3,1,2,0:T(8,128)(2,1)}) fusion(bf16[12,8,40,128]{3,1,2,0:T(8,128)(2,1)} %bitcast.233, bf16[12,8,40,128]{3,1,2,0:T(8,128)(2,1)} %bitcast.234), kind=kLoop, calls=%fused_computation.75 | loop fusion | bytes 3932160 | tf_op jit(solution)/shard_map/transpose | solution.py:118
  6.1 2.2 %fusion.6 = bf16[12,8,128,4,30]{2,4,3,1,0:T(8,128)(2,1)S(1)} fusion(bf16[12,40,8,128]{3,1,2,0:T(8,128)(2,1)S(1)} %get-tuple-element.75, bf16[12,40,8,128]{3,1,2,0:T(8,128)(2,1)} %get-tuple-element.76, bf16[12,40,8,128]{3,1,2,0:T(8,128)(2,1)S(1)} %bitcast.232, s32[4,30]{1,0:T(4,128)S(1)} %concatenate.41), kind=kOutput, calls=%fused_computation.22 | convolution fusion | flops 362756160 | bytes 5898720 | tf_op jit(solution)/shard_map/gsh,ahrd->garsd/dot_general | solution.py:130
  8.3 3.5 %copy.197 = bf16[4,96,30,128]{3,1,2,0:T(8,128)(2,1)} copy(bf16[4,96,30,128]{3,2,0,1:T(8,128)(2,1)S(1)} %bitcast.206) | data formatting | bytes 5898240 | tf_op jit(solution)/shard_map/reshape | solution.py:132
  11.9 4.6 %all-to-all-start = ((bf16[4,96,30,128]{3,1,2,0:T(8,128)(2,1)}), bf16[4,96,30,128]{3,1,2,0:T(8,128)(2,1)}, u32[]{:S(2)}, u32[]{:S(2)}) async-start(bf16[4,96,30,128]{3,1,2,0:T(8,128)(2,1)} %copy.197), calls=%async_computation | async-start | bytes 5898240 | tf_op jit(solution)/shard_map/all_to_all | solution.py:133
  16.6 0.7 gather_fusion
  17.5 0.6 gather_fusion.1
  18.2 0.6 gather_fusion.3
  18.7 0.7 gather_fusion.2
  20.3 0.7 gather_fusion.4
  21.2 0.9 gather_fusion.5
  22.2 0.7 gather_fusion.8
  22.8 0.7 gather_fusion.9
  23.5 0.7 gather_fusion.10
  24.4 1.0 gather_fusion.7
  25.5 0.7 copy.217
  26.2 0.9 gather_fusion.6
  27.3 25.0 %all-to-all-done = bf16[4,96,30,128]{3,1,2,0:T(8,128)(2,1)} async-done(((bf16[4,96,30,128]{3,1,2,0:T(8,128)(2,1)}), bf16[4,96,30,128]{3,1,2,0:T(8,128)(2,1)}, u32[]{:S(2)}, u32[]{:S(2)}) %all-to-all-start) | async-done | bytes 2949152 | tf_op jit(solution)/shard_map/all_to_all | solution.py:133
  52.3 2.2 %copy.198 = bf16[4,96,30,128]{3,1,0,2:T(8,128)(2,1)S(1)} copy(bf16[4,96,30,128]{3,1,2,0:T(8,128)(2,1)} %all-to-all-done) | data formatting | bytes 5898240 | tf_op jit(solution)/shard_map/all_to_all | solution.py:133
  54.7 1.5 copy.199
  56.5 10.5 %all-to-all-start.1 = ((bf16[16,24,12,128]{3,1,2,0:T(8,128)(2,1)}), bf16[16,24,12,128]{3,1,2,0:T(8,128)(2,1)S(1)}, u32[]{:S(2)}, u32[]{:S(2)}) async-start(bf16[16,24,12,128]{3,1,2,0:T(8,128)(2,1)} %bitcast.203), calls=%async_computation.1 | async-start | bytes 2359296 | tf_op jit(solution)/shard_map/all_to_all | solution.py:140
  67.3 1.1 slice.371
  68.4 30.3 %all-to-all-done.1 = bf16[16,24,12,128]{3,1,2,0:T(8,128)(2,1)S(1)} async-done(((bf16[16,24,12,128]{3,1,2,0:T(8,128)(2,1)}), bf16[16,24,12,128]{3,1,2,0:T(8,128)(2,1)S(1)}, u32[]{:S(2)}, u32[]{:S(2)}) %all-to-all-start.1) | async-done | bytes 1179680 | tf_op jit(solution)/shard_map/all_to_all | solution.py:140
  99.2 0.9 fusion.81
  100.2 5.4 %collective-permute-start = (bf16[128,8,128]{2,0,1:T(8,128)(2,1)S(1)}, bf16[128,8,128]{2,0,1:T(8,128)(2,1)S(1)}, u32[]{:S(2)}, u32[]{:S(2)}) collective-permute-start(bf16[128,8,128]{2,0,1:T(8,128)(2,1)S(1)} %get-tuple-element.48), channel_id=1, source_target_pairs={{0,8},{8,16},{16,24},{24,32},{32,40},{40,48},{48,56},{56,4},{4,12}... | collective-permute-start | bytes 786440 | tf_op jit(solution)/shard_map/ppermute | solution.py:18
  105.7 2.3 %collective-permute-start.1 = (bf16[128,8,128]{2,0,1:T(8,128)(2,1)S(1)}, bf16[128,8,128]{2,0,1:T(8,128)(2,1)S(1)}, u32[]{:S(2)}, u32[]{:S(2)}) collective-permute-start(bf16[128,8,128]{2,0,1:T(8,128)(2,1)S(1)} %get-tuple-element.47), channel_id=1, source_target_pairs={{8,0},{16,8},{24,16},{32,24},{40,32},{48,40},{56,48},{4,56},{12,4}... | collective-permute-start | bytes 786440 | tf_op jit(solution)/shard_map/ppermute | solution.py:19
  108.0 8.8 %collective-permute-start.2 = (bf16[128,12,128]{2,0,1:T(8,128)(2,1)}, bf16[128,12,128]{2,0,1:T(8,128)(2,1)}, u32[]{:S(2)}, u32[]{:S(2)}) collective-permute-start(bf16[128,12,128]{2,0,1:T(8,128)(2,1)} %get-tuple-element.52), channel_id=1, source_target_pairs={{0,256},{256,1},{1,257},{257,2},{2,258},{258,3},{3,259},{259,4},{4... | collective-permute-start | bytes 1179656 | tf_op jit(solution)/shard_map/ppermute | solution.py:18
  116.8 2.1 %collective-permute-start.3 = (bf16[128,12,128]{2,0,1:T(8,128)(2,1)}, bf16[128,12,128]{2,0,1:T(8,128)(2,1)}, u32[]{:S(2)}, u32[]{:S(2)}) collective-permute-start(bf16[128,12,128]{2,0,1:T(8,128)(2,1)} %get-tuple-element.51), channel_id=1, source_target_pairs={{256,0},{1,256},{257,1},{2,257},{258,2},{3,258},{259,3},{4,259},{2... | collective-permute-start | bytes 1179656 | tf_op jit(solution)/shard_map/ppermute | solution.py:19
  119.0 1.4 collective-permute-done.1
  122.6 0.6 fusion.3
  123.2 1.2 fusion.4
  126.4 0.8 copy.215
  127.2 10.3 %all-to-all-start.2 = ((bf16[16,24,4,128]{3,1,2,0:T(8,128)(2,1)}), bf16[16,24,4,128]{3,1,2,0:T(8,128)(2,1)S(1)}, u32[]{:S(2)}, u32[]{:S(2)}) async-start(bf16[16,24,4,128]{3,1,2,0:T(8,128)(2,1)} %copy.215), calls=%async_computation.2 | async-start | bytes 786432 | tf_op jit(solution)/shard_map/all_to_all | solution.py:185
  137.5 16.9 %collective-permute-done.2 = bf16[128,12,128]{2,0,1:T(8,128)(2,1)} collective-permute-done((bf16[128,12,128]{2,0,1:T(8,128)(2,1)}, bf16[128,12,128]{2,0,1:T(8,128)(2,1)}, u32[]{:S(2)}, u32[]{:S(2)}) %collective-permute-start.2) | collective-permute-done | bytes 393248 | tf_op jit(solution)/shard_map/ppermute | solution.py:18
  154.4 1.0 constant_dynamic-update-slice_fusion.1
  156.3 8.2 %collective-permute-done.3 = bf16[128,12,128]{2,0,1:T(8,128)(2,1)} collective-permute-done((bf16[128,12,128]{2,0,1:T(8,128)(2,1)}, bf16[128,12,128]{2,0,1:T(8,128)(2,1)}, u32[]{:S(2)}, u32[]{:S(2)}) %collective-permute-start.3) | collective-permute-done | bytes 393248 | tf_op jit(solution)/shard_map/ppermute | solution.py:19
  164.5 1.0 constant_dynamic-update-slice_fusion.2
  168.2 1.0 fusion
  169.2 1.9 fusion.1
  171.1 0.6 slice_bitcast_fusion
  173.3 0.6 fusion.20
  174.2 1.0 copy.231
  175.2 3.5 %all-to-all-start.3 = ((bf16[4,96,10,128]{3,1,2,0:T(8,128)(2,1)}), bf16[4,96,10,128]{3,1,2,0:T(8,128)(2,1)S(1)}, u32[]{:S(2)}, u32[]{:S(2)}) async-start(bf16[4,96,10,128]{3,1,2,0:T(8,128)(2,1)} %copy.231), calls=%async_computation.3 | async-start | bytes 1966080 | tf_op jit(solution)/shard_map/all_to_all | solution.py:190
  178.7 14.9 %all-to-all-done.3 = bf16[4,96,10,128]{3,1,2,0:T(8,128)(2,1)S(1)} async-done(((bf16[4,96,10,128]{3,1,2,0:T(8,128)(2,1)}), bf16[4,96,10,128]{3,1,2,0:T(8,128)(2,1)S(1)}, u32[]{:S(2)}, u32[]{:S(2)}) %all-to-all-start.3) | async-done | bytes 983072 | tf_op jit(solution)/shard_map/all_to_all | solution.py:190
  193.6 0.6 fusion.11
  194.2 1.1 copy.306
  (98 shorter events, 13.1 us)
Async XLA Ops:
  0.0 16.6 %copy-start = (s32[40,768,5]{1,0,2:T(8,128)S(1)}, s32[40,768,5]{1,0,2:T(8,128)}, u32[]{:S(2)}) copy-start(s32[40,768,5]{1,0,2:T(8,128)} %param.15) | copy-start | bytes 1843204
  11.9 40.4 %all-to-all-start = ((bf16[4,96,30,128]{3,1,2,0:T(8,128)(2,1)}), bf16[4,96,30,128]{3,1,2,0:T(8,128)(2,1)}, u32[]{:S(2)}, u32[]{:S(2)}) async-start(bf16[4,96,30,128]{3,1,2,0:T(8,128)(2,1)} %copy.197), calls=%async_computation | async-start | bytes 5898240 | tf_op jit(solution)/shard_map/all_to_all | solution.py:133
  16.6 0.9 copy-start.6
  19.5 2.7 %copy-start.2 = (f32[40]{0:T(128)S(1)}, f32[40]{0:T(128)}, u32[]{:S(2)}) copy-start(f32[40]{0:T(128)} %param.17) | copy-start | bytes 484
  19.5 3.4 %copy-start.3 = (f32[40]{0:T(128)S(1)}, f32[40]{0:T(128)}, u32[]{:S(2)}) copy-start(f32[40]{0:T(128)} %param.18) | copy-start | bytes 484
  19.5 4.0 %copy-start.4 = (f32[40]{0:T(128)S(1)}, f32[40]{0:T(128)}, u32[]{:S(2)}) copy-start(f32[40]{0:T(128)} %param.19) | copy-start | bytes 484
  54.5 2.0 %copy-start.5 = (bf16[4,96,30,128]{3,1,0,2:T(8,128)(2,1)}, bf16[4,96,30,128]{3,1,0,2:T(8,128)(2,1)S(1)}, u32[]{:S(2)}) copy-start(bf16[4,96,30,128]{3,1,0,2:T(8,128)(2,1)S(1)} %copy.198) | copy-start | bytes 8847364
  56.5 42.2 %all-to-all-start.1 = ((bf16[16,24,12,128]{3,1,2,0:T(8,128)(2,1)}), bf16[16,24,12,128]{3,1,2,0:T(8,128)(2,1)S(1)}, u32[]{:S(2)}, u32[]{:S(2)}) async-start(bf16[16,24,12,128]{3,1,2,0:T(8,128)(2,1)} %bitcast.203), calls=%async_computation.1 | async-start | bytes 2359296 | tf_op jit(solution)/shard_map/all_to_all | solution.py:140
  100.2 18.8 %collective-permute-start = (bf16[128,8,128]{2,0,1:T(8,128)(2,1)S(1)}, bf16[128,8,128]{2,0,1:T(8,128)(2,1)S(1)}, u32[]{:S(2)}, u32[]{:S(2)}) collective-permute-start(bf16[128,8,128]{2,0,1:T(8,128)(2,1)S(1)} %get-tuple-element.48), channel_id=1, source_target_pairs={{0,8},{8,16},{16,24},{24,32},{32,40},{40,48},{48,56},{56,4},{4,12}... | collective-permute-start | bytes 786440 | tf_op jit(solution)/shard_map/ppermute | solution.py:18
  105.7 14.8 %collective-permute-start.1 = (bf16[128,8,128]{2,0,1:T(8,128)(2,1)S(1)}, bf16[128,8,128]{2,0,1:T(8,128)(2,1)S(1)}, u32[]{:S(2)}, u32[]{:S(2)}) collective-permute-start(bf16[128,8,128]{2,0,1:T(8,128)(2,1)S(1)} %get-tuple-element.47), channel_id=1, source_target_pairs={{8,0},{16,8},{24,16},{32,24},{40,32},{48,40},{56,48},{4,56},{12,4}... | collective-permute-start | bytes 786440 | tf_op jit(solution)/shard_map/ppermute | solution.py:19
  108.0 46.4 %collective-permute-start.2 = (bf16[128,12,128]{2,0,1:T(8,128)(2,1)}, bf16[128,12,128]{2,0,1:T(8,128)(2,1)}, u32[]{:S(2)}, u32[]{:S(2)}) collective-permute-start(bf16[128,12,128]{2,0,1:T(8,128)(2,1)} %get-tuple-element.52), channel_id=1, source_target_pairs={{0,256},{256,1},{1,257},{257,2},{2,258},{258,3},{3,259},{259,4},{4... | collective-permute-start | bytes 1179656 | tf_op jit(solution)/shard_map/ppermute | solution.py:18
  116.8 47.6 %collective-permute-start.3 = (bf16[128,12,128]{2,0,1:T(8,128)(2,1)}, bf16[128,12,128]{2,0,1:T(8,128)(2,1)}, u32[]{:S(2)}, u32[]{:S(2)}) collective-permute-start(bf16[128,12,128]{2,0,1:T(8,128)(2,1)} %get-tuple-element.51), channel_id=1, source_target_pairs={{256,0},{1,256},{257,1},{2,257},{258,2},{3,258},{259,3},{4,259},{2... | collective-permute-start | bytes 1179656 | tf_op jit(solution)/shard_map/ppermute | solution.py:19
  127.2 46.8 %all-to-all-start.2 = ((bf16[16,24,4,128]{3,1,2,0:T(8,128)(2,1)}), bf16[16,24,4,128]{3,1,2,0:T(8,128)(2,1)S(1)}, u32[]{:S(2)}, u32[]{:S(2)}) async-start(bf16[16,24,4,128]{3,1,2,0:T(8,128)(2,1)} %copy.215), calls=%async_computation.2 | async-start | bytes 786432 | tf_op jit(solution)/shard_map/all_to_all | solution.py:185
  174.2 21.2 %copy-start.1 = (s32[40,768,5]{1,0,2:T(8,128)S(1)}, s32[40,768,5]{1,0,2:T(8,128)}, u32[]{:S(2)}) copy-start(s32[40,768,5]{1,0,2:T(8,128)} %param.15) | copy-start | bytes 1843204
  175.2 18.4 %all-to-all-start.3 = ((bf16[4,96,10,128]{3,1,2,0:T(8,128)(2,1)}), bf16[4,96,10,128]{3,1,2,0:T(8,128)(2,1)S(1)}, u32[]{:S(2)}, u32[]{:S(2)}) async-start(bf16[4,96,10,128]{3,1,2,0:T(8,128)(2,1)} %copy.231), calls=%async_computation.3 | async-start | bytes 1966080 | tf_op jit(solution)/shard_map/all_to_all | solution.py:190
